TPU v7x, 32 devices: a whole 2x2x4 slice. The times are simulated.
32 devices in a mesh: dp: 16 (over z, y, x), mp: 2 (over core).
Axes of the slice: x: 2, y: 2, z: 4, core: 2. Of those that a mesh axis runs over, the one named last changes fastest.
Arguments:
- text_input: bfloat16 [16384, 768], P(('dp', 'mp')), may hold values from -6 to 6
- layout_input: bfloat16 [16384, 192], P(('dp', 'mp')), may hold values from -6 to 6
- repeated: int32 [16384], P('dp'), may hold values 0 or 1
- key_mask: int32 [16384], P('dp'), may hold values 0 or 1
- text_qkv: bfloat16 [3, 768, 768], P(None, None, 'mp'), may hold values from -0.21875 to 0.21875
- text_qvbias: bfloat16 [2, 768], P(None, 'mp'), may hold values from -3 to 3
- text_wout: bfloat16 [768, 768], P('mp'), may hold values from -1.75 to 1.75
- text_outbias: bfloat16 [2, 768], replicated, may hold values from -2 to 2
- text_wup: bfloat16 [768, 3072], P(None, 'mp'), may hold values from -0.21875 to 0.21875
- text_upbias: bfloat16 [3072], P('mp'), may hold values from -3 to 3
- text_wdown: bfloat16 [3072, 768], P('mp'), may hold values from -0.21875 to 0.21875
- text_gains: bfloat16 [2, 768], replicated, may hold values from 0.5 to 1.5
- text_shifts: bfloat16 [2, 768], replicated, may hold values from -2 to 2
- layout_qkv: bfloat16 [3, 192, 192], P(None, None, 'mp'), may hold values from -0.4375 to 0.4375
- layout_qvbias: bfloat16 [2, 192], P(None, 'mp'), may hold values from -3 to 3
- layout_wout: bfloat16 [192, 192], P('mp'), may hold values from -1.75 to 1.75
- layout_outbias: bfloat16 [2, 192], replicated, may hold values from -2 to 2
- layout_wup: bfloat16 [192, 768], P(None, 'mp'), may hold values from -0.4375 to 0.4375
- layout_upbias: bfloat16 [768], P('mp'), may hold values from -3 to 3
- layout_wdown: bfloat16 [768, 192], P('mp'), may hold values from -0.4375 to 0.4375
- layout_gains: bfloat16 [2, 192], replicated, may hold values from 0.5 to 1.5
- layout_shifts: bfloat16 [2, 192], replicated, may hold values from -2 to 2
- text_cotan: bfloat16 [16384, 768], P(('dp', 'mp')), may hold values from -6 to 6
- layout_cotan: bfloat16 [16384, 192], P(('dp', 'mp')), may hold values from -6 to 6
Outputs:
- text_result: bfloat16 [16384, 768], P(('dp', 'mp'))
- layout_result: bfloat16 [16384, 192], P(('dp', 'mp'))
- text_dinput: bfloat16 [16384, 768], P(('dp', 'mp'))
- layout_dinput: bfloat16 [16384, 192], P(('dp', 'mp'))
- text_qkv_grad: float32 [3, 768, 768], P(None, 'dp', 'mp')
- text_qvbias_grad: float32 [2, 768], P(None, 'mp')
- text_wout_grad: float32 [768, 768], P('mp', 'dp')
- text_outbias_grad: float32 [2, 768], replicated
- text_wup_grad: float32 [768, 3072], P('dp', 'mp')
- text_upbias_grad: float32 [3072], P('mp')
- text_wdown_grad: float32 [3072, 768], P('mp', 'dp')
- text_gains_grad: float32 [2, 768], replicated
- text_shifts_grad: float32 [2, 768], replicated
- layout_qkv_grad: float32 [3, 192, 192], P(None, None, 'mp')
- layout_qvbias_grad: float32 [2, 192], P(None, 'mp')
- layout_wout_grad: float32 [192, 192], P('mp')
- layout_outbias_grad: float32 [2, 192], replicated
- layout_wup_grad: float32 [192, 768], P(None, 'mp')
- layout_upbias_grad: float32 [768], P('mp')
- layout_wdown_grad: float32 [768, 192], P('mp')
- layout_gains_grad: float32 [2, 192], replicated
- layout_shifts_grad: float32 [2, 192], replicated
All inputs are finite; a program needn't handle non-finite values. No bound on the sum of `repeated` or of `key_mask` on one device may be relied on, other than what follows from the above.
Results may differ from a plain program's by a relative error of at most 0.02.
The roundings to bfloat16 on the way count: a program that leaves them out, or rounds other values in their place, can miss the bound.
Values may be sent and summed in bfloat16 or wider, within the bound.
No kernel may reach another device: no remote copies, remote signals or barrier semaphores. Data moves between devices by JAX's collectives and lax.ppermute only.
A program may use at most 128 MiB of HBM per device.

v0:
```python
import jax
import jax.numpy as jnp
from jax import lax
from jax.sharding import PartitionSpec as P

D = 768
H = 12
DL = 192
WINDOW = 512


EPSILON = 1e-05
MASKED = -1000000000.0


def layer_norm(values, gain, shift):
    centered = values - jnp.mean(values, axis=-1, keepdims=True)
    variance = jnp.mean(centered * centered, axis=-1, keepdims=True)
    return centered * lax.rsqrt(variance + EPSILON) * gain + shift


def gelu(values):
    return 0.5 * values * (1.0 + lax.erf(values * 0.7071067811865476))


def project_path(rows, weight_qkv, biases):
    joined = jnp.einsum("rd,kde->kre", rows, weight_qkv, preferred_element_type=jnp.float32)
    queries = (joined[0] + biases[0]).astype(jnp.bfloat16)
    key_rows = joined[1].astype(jnp.bfloat16)
    value_rows = (joined[2] + biases[1]).astype(jnp.bfloat16)
    return (queries, key_rows, value_rows)


def blocked(values, head_size):
    return values.reshape(-1, WINDOW, values.shape[-1] // head_size, head_size)


def unblocked(values):
    return values.reshape(-1, values.shape[-2] * values.shape[-1])


def coupled_scores(text_queries, text_keys, layout_queries, layout_keys, usable):
    scores = jnp.einsum(
        "qhd,khd->hqk", text_queries, text_keys, preferred_element_type=jnp.float32
    ) * (D // H) ** (-0.5)
    scores = scores + jnp.einsum(
        "qhd,khd->hqk", layout_queries, layout_keys, preferred_element_type=jnp.float32
    ) * (DL // H) ** (-0.5)
    return jnp.where(usable[None, None, :], scores, MASKED)


def attend_window(pieces):
    text_queries, text_keys, text_values, layout_queries, layout_keys, layout_values, usable = (
        pieces
    )
    scores = coupled_scores(text_queries, text_keys, layout_queries, layout_keys, usable)
    peak = jnp.max(scores, axis=-1, keepdims=True)
    powers = jnp.exp(scores - peak)
    total = jnp.sum(powers, axis=-1, keepdims=True)
    probs = (powers / total).astype(jnp.bfloat16)
    text_context = jnp.einsum(
        "hqk,khd->qhd", probs, text_values, preferred_element_type=jnp.float32
    ).astype(jnp.bfloat16)
    layout_context = jnp.einsum(
        "hqk,khd->qhd", probs, layout_values, preferred_element_type=jnp.float32
    ).astype(jnp.bfloat16)
    return (text_context, layout_context, peak + jnp.log(total))


def attend_back(pieces):
    (
        text_queries,
        text_keys,
        text_values,
        layout_queries,
        layout_keys,
        layout_values,
        usable,
        log_totals,
        text_cgrad,
        layout_cgrad,
    ) = pieces
    text_scale = (D // H) ** (-0.5)
    layout_scale = (DL // H) ** (-0.5)
    scores = coupled_scores(text_queries, text_keys, layout_queries, layout_keys, usable)
    probs = jnp.exp(scores - log_totals)
    probs_low = probs.astype(jnp.bfloat16)
    probs_grad = jnp.einsum(
        "qhd,khd->hqk", text_cgrad, text_values, preferred_element_type=jnp.float32
    )
    probs_grad = probs_grad + jnp.einsum(
        "qhd,khd->hqk", layout_cgrad, layout_values, preferred_element_type=jnp.float32
    )
    scores_grad = (
        probs * (probs_grad - jnp.sum(probs_grad * probs, axis=-1, keepdims=True))
    ).astype(jnp.bfloat16)
    text_vgrad = jnp.einsum(
        "hqk,qhd->khd", probs_low, text_cgrad, preferred_element_type=jnp.float32
    ).astype(jnp.bfloat16)
    layout_vgrad = jnp.einsum(
        "hqk,qhd->khd", probs_low, layout_cgrad, preferred_element_type=jnp.float32
    ).astype(jnp.bfloat16)
    text_qgrad = (
        jnp.einsum("hqk,khd->qhd", scores_grad, text_keys, preferred_element_type=jnp.float32)
        * text_scale
    ).astype(jnp.bfloat16)
    text_kgrad = (
        jnp.einsum("hqk,qhd->khd", scores_grad, text_queries, preferred_element_type=jnp.float32)
        * text_scale
    ).astype(jnp.bfloat16)
    layout_qgrad = (
        jnp.einsum("hqk,khd->qhd", scores_grad, layout_keys, preferred_element_type=jnp.float32)
        * layout_scale
    ).astype(jnp.bfloat16)
    layout_kgrad = (
        jnp.einsum("hqk,qhd->khd", scores_grad, layout_queries, preferred_element_type=jnp.float32)
        * layout_scale
    ).astype(jnp.bfloat16)
    return (text_qgrad, text_kgrad, text_vgrad, layout_qgrad, layout_kgrad, layout_vgrad)


def feed_forward(full_rows, w_up, up_bias, w_down):
    hidden = jnp.dot(full_rows, w_up, preferred_element_type=jnp.float32) + up_bias
    active, gelu_back = jax.vjp(gelu, hidden)
    active_low = active.astype(jnp.bfloat16)
    return (active_low, gelu_back, jnp.dot(active_low, w_down, preferred_element_type=jnp.float32))


def feed_back(full_rows, active_low, gelu_back, full_grad, w_up, w_down):
    grad_down = jnp.einsum("rf,rd->fd", active_low, full_grad, preferred_element_type=jnp.float32)
    active_grad = jnp.einsum("rd,fd->rf", full_grad, w_down, preferred_element_type=jnp.float32)
    hidden_grad = gelu_back(active_grad)[0].astype(jnp.bfloat16)
    grad_up = jnp.einsum("rd,rf->df", full_rows, hidden_grad, preferred_element_type=jnp.float32)
    grad_bias = jnp.sum(hidden_grad, axis=0, dtype=jnp.float32)
    normed_part = jnp.einsum("rf,df->rd", hidden_grad, w_up, preferred_element_type=jnp.float32)
    return (grad_up, grad_bias, grad_down, normed_part)


def input_back(rows, weight_qkv, query_grad, key_grad, value_grad):
    grad_qkv = jnp.stack(
        [
            jnp.einsum("rd,re->de", rows, piece, preferred_element_type=jnp.float32)
            for piece in (query_grad, key_grad, value_grad)
        ]
    )
    input_part = jnp.einsum(
        "re,de->rd", query_grad, weight_qkv[0], preferred_element_type=jnp.float32
    )
    input_part = input_part + jnp.einsum(
        "re,de->rd", key_grad, weight_qkv[1], preferred_element_type=jnp.float32
    )
    input_part = input_part + jnp.einsum(
        "re,de->rd", value_grad, weight_qkv[2], preferred_element_type=jnp.float32
    )
    grad_bias = jnp.stack(
        [
            jnp.sum(query_grad, axis=0, dtype=jnp.float32),
            jnp.sum(value_grad, axis=0, dtype=jnp.float32),
        ]
    )
    return (grad_qkv, grad_bias, input_part)


def body(
    text_input,
    layout_input,
    repeated,
    key_mask,
    text_qkv,
    text_qvbias,
    text_wout,
    text_outbias,
    text_wup,
    text_upbias,
    text_wdown,
    text_gains,
    text_shifts,
    layout_qkv,
    layout_qvbias,
    layout_wout,
    layout_outbias,
    layout_wup,
    layout_upbias,
    layout_wdown,
    layout_gains,
    layout_shifts,
    text_cotan,
    layout_cotan,
):
    text_head = D // H
    layout_head = DL // H
    usable_group = jnp.logical_and(key_mask == 1, repeated == 0).reshape(-1, WINDOW)
    text_rows, layout_rows = (
        lax.all_gather(text_input, "mp", axis=0, tiled=True),
        lax.all_gather(layout_input, "mp", axis=0, tiled=True),
    )
    text_queries, text_keys, text_values = project_path(text_rows, text_qkv, text_qvbias)
    layout_queries, layout_keys, layout_values = project_path(
        layout_rows, layout_qkv, layout_qvbias
    )
    blocks = (
        blocked(text_queries, text_head),
        blocked(text_keys, text_head),
        blocked(text_values, text_head),
        blocked(layout_queries, layout_head),
        blocked(layout_keys, layout_head),
        blocked(layout_values, layout_head),
        usable_group,
    )
    text_context, layout_context, log_totals = lax.map(attend_window, blocks)
    text_context = unblocked(text_context)
    layout_context = unblocked(layout_context)
    text_mixed_part = jnp.dot(text_context, text_wout, preferred_element_type=jnp.float32)
    layout_mixed_part = jnp.dot(layout_context, layout_wout, preferred_element_type=jnp.float32)
    text_mixed, layout_mixed = (
        lax.psum_scatter(
            text_mixed_part.astype(jnp.bfloat16), "mp", scatter_dimension=0, tiled=True
        ).astype(jnp.float32),
        lax.psum_scatter(
            layout_mixed_part.astype(jnp.bfloat16), "mp", scatter_dimension=0, tiled=True
        ).astype(jnp.float32),
    )
    text_gain = text_gains.astype(jnp.float32)
    text_shift = text_shifts.astype(jnp.float32)
    layout_gain = layout_gains.astype(jnp.float32)
    layout_shift = layout_shifts.astype(jnp.float32)
    text_normed, text_first_back = jax.vjp(
        layer_norm,
        text_input.astype(jnp.float32) + text_mixed + text_outbias[0],
        text_gain[0],
        text_shift[0],
    )
    layout_normed, layout_first_back = jax.vjp(
        layer_norm,
        layout_input.astype(jnp.float32) + layout_mixed + layout_outbias[0],
        layout_gain[0],
        layout_shift[0],
    )
    text_full, layout_full = (
        lax.all_gather(text_normed.astype(jnp.bfloat16), "mp", axis=0, tiled=True),
        lax.all_gather(layout_normed.astype(jnp.bfloat16), "mp", axis=0, tiled=True),
    )
    text_active, text_gelu_back, text_branch_part = feed_forward(
        text_full, text_wup, text_upbias, text_wdown
    )
    layout_active, layout_gelu_back, layout_branch_part = feed_forward(
        layout_full, layout_wup, layout_upbias, layout_wdown
    )
    text_branch, layout_branch = (
        lax.psum_scatter(
            text_branch_part.astype(jnp.bfloat16), "mp", scatter_dimension=0, tiled=True
        ).astype(jnp.float32),
        lax.psum_scatter(
            layout_branch_part.astype(jnp.bfloat16), "mp", scatter_dimension=0, tiled=True
        ).astype(jnp.float32),
    )
    text_final, text_final_back = jax.vjp(
        layer_norm, text_normed + text_branch + text_outbias[1], text_gain[1], text_shift[1]
    )
    layout_final, layout_final_back = jax.vjp(
        layer_norm,
        layout_normed + layout_branch + layout_outbias[1],
        layout_gain[1],
        layout_shift[1],
    )
    text_sum_grad, text_gain_second, text_shift_second = text_final_back(
        text_cotan.astype(jnp.float32)
    )
    layout_sum_grad, layout_gain_second, layout_shift_second = layout_final_back(
        layout_cotan.astype(jnp.float32)
    )
    text_branch_grad = text_sum_grad.astype(jnp.bfloat16)
    layout_branch_grad = layout_sum_grad.astype(jnp.bfloat16)
    text_full_grad, layout_full_grad = (
        lax.all_gather(text_branch_grad, "mp", axis=0, tiled=True),
        lax.all_gather(layout_branch_grad, "mp", axis=0, tiled=True),
    )
    text_wup_grad, text_upbias_grad, text_wdown_grad, text_normed_part = feed_back(
        text_full, text_active, text_gelu_back, text_full_grad, text_wup, text_wdown
    )
    layout_wup_grad, layout_upbias_grad, layout_wdown_grad, layout_normed_part = feed_back(
        layout_full, layout_active, layout_gelu_back, layout_full_grad, layout_wup, layout_wdown
    )
    text_normed_grad, layout_normed_grad = (
        lax.psum_scatter(
            text_normed_part.astype(jnp.bfloat16), "mp", scatter_dimension=0, tiled=True
        ).astype(jnp.float32),
        lax.psum_scatter(
            layout_normed_part.astype(jnp.bfloat16), "mp", scatter_dimension=0, tiled=True
        ).astype(jnp.float32),
    )
    text_mixed_grad, text_gain_first, text_shift_first = text_first_back(
        text_normed_grad + text_sum_grad
    )
    layout_mixed_grad, layout_gain_first, layout_shift_first = layout_first_back(
        layout_normed_grad + layout_sum_grad
    )
    text_mixed_low = text_mixed_grad.astype(jnp.bfloat16)
    layout_mixed_low = layout_mixed_grad.astype(jnp.bfloat16)
    text_wide_grad, layout_wide_grad = (
        lax.all_gather(text_mixed_low, "mp", axis=0, tiled=True),
        lax.all_gather(layout_mixed_low, "mp", axis=0, tiled=True),
    )
    text_wout_grad = jnp.einsum(
        "re,rd->ed", text_context, text_wide_grad, preferred_element_type=jnp.float32
    )
    layout_wout_grad = jnp.einsum(
        "re,rd->ed", layout_context, layout_wide_grad, preferred_element_type=jnp.float32
    )
    text_context_grad = jnp.einsum(
        "rd,ed->re", text_wide_grad, text_wout, preferred_element_type=jnp.float32
    ).astype(jnp.bfloat16)
    layout_context_grad = jnp.einsum(
        "rd,ed->re", layout_wide_grad, layout_wout, preferred_element_type=jnp.float32
    ).astype(jnp.bfloat16)
    back_blocks = blocks + (
        log_totals,
        blocked(text_context_grad, text_head),
        blocked(layout_context_grad, layout_head),
    )
    text_qgrad, text_kgrad, text_vgrad, layout_qgrad, layout_kgrad, layout_vgrad = lax.map(
        attend_back, back_blocks
    )
    text_qkv_grad, text_qvbias_grad, text_input_part = input_back(
        text_rows, text_qkv, unblocked(text_qgrad), unblocked(text_kgrad), unblocked(text_vgrad)
    )
    layout_qkv_grad, layout_qvbias_grad, layout_input_part = input_back(
        layout_rows,
        layout_qkv,
        unblocked(layout_qgrad),
        unblocked(layout_kgrad),
        unblocked(layout_vgrad),
    )
    text_input_sum, layout_input_sum = (
        lax.psum_scatter(
            text_input_part.astype(jnp.bfloat16), "mp", scatter_dimension=0, tiled=True
        ).astype(jnp.float32),
        lax.psum_scatter(
            layout_input_part.astype(jnp.bfloat16), "mp", scatter_dimension=0, tiled=True
        ).astype(jnp.float32),
    )
    text_dinput = (text_mixed_grad + text_input_sum).astype(jnp.bfloat16)
    layout_dinput = (layout_mixed_grad + layout_input_sum).astype(jnp.bfloat16)
    qkv_share, wout_share, wup_share, wdown_share = (
        lax.psum_scatter(text_qkv_grad, "dp", scatter_dimension=1, tiled=True),
        lax.psum_scatter(text_wout_grad, "dp", scatter_dimension=1, tiled=True),
        lax.psum_scatter(text_wup_grad, "dp", scatter_dimension=0, tiled=True),
        lax.psum_scatter(text_wdown_grad, "dp", scatter_dimension=1, tiled=True),
    )
    summed = lax.psum(
        (
            text_qvbias_grad,
            text_upbias_grad,
            layout_qkv_grad,
            layout_qvbias_grad,
            layout_wout_grad,
            layout_wup_grad,
            layout_upbias_grad,
            layout_wdown_grad,
        ),
        "dp",
    )
    text_outbias_part = jnp.stack(
        [
            jnp.sum(text_mixed_low, axis=0, dtype=jnp.float32),
            jnp.sum(text_branch_grad, axis=0, dtype=jnp.float32),
        ]
    )
    layout_outbias_part = jnp.stack(
        [
            jnp.sum(layout_mixed_low, axis=0, dtype=jnp.float32),
            jnp.sum(layout_branch_grad, axis=0, dtype=jnp.float32),
        ]
    )
    shared = lax.psum(
        (
            text_outbias_part,
            jnp.stack([text_gain_first, text_gain_second]),
            jnp.stack([text_shift_first, text_shift_second]),
            layout_outbias_part,
            jnp.stack([layout_gain_first, layout_gain_second]),
            jnp.stack([layout_shift_first, layout_shift_second]),
        ),
        ("dp", "mp"),
    )
    return (
        text_final.astype(jnp.bfloat16),
        layout_final.astype(jnp.bfloat16),
        text_dinput,
        layout_dinput,
        qkv_share,
        summed[0],
        wout_share,
        shared[0],
        wup_share,
        summed[1],
        wdown_share,
        shared[1],
        shared[2],
        summed[2],
        summed[3],
        summed[4],
        shared[3],
        summed[5],
        summed[6],
        summed[7],
        shared[4],
        shared[5],
    )


def solution(mesh):
    in_specs = (
        P(("dp", "mp"), None),
        P(("dp", "mp"), None),
        P("dp"),
        P("dp"),
        P(None, None, "mp"),
        P(None, "mp"),
        P("mp", None),
        P(),
        P(None, "mp"),
        P("mp"),
        P("mp", None),
        P(),
        P(),
        P(None, None, "mp"),
        P(None, "mp"),
        P("mp", None),
        P(),
        P(None, "mp"),
        P("mp"),
        P("mp", None),
        P(),
        P(),
        P(("dp", "mp"), None),
        P(("dp", "mp"), None),
    )
    out_specs = (
        P(("dp", "mp"), None),
        P(("dp", "mp"), None),
        P(("dp", "mp"), None),
        P(("dp", "mp"), None),
        P(None, "dp", "mp"),
        P(None, "mp"),
        P("mp", "dp"),
        P(),
        P("dp", "mp"),
        P("mp"),
        P("mp", "dp"),
        P(),
        P(),
        P(None, None, "mp"),
        P(None, "mp"),
        P("mp", None),
        P(),
        P(None, "mp"),
        P("mp"),
        P("mp", None),
        P(),
        P(),
    )
    return jax.shard_map(body, mesh=mesh, in_specs=in_specs, out_specs=out_specs, check_vma=False)
```

profile of v0, /device:TPU:0, one launch (start us, length us, event | category | flops | bytes accessed | tf_op | source)
XLA Modules:
  0.0 894.9 jit_solution(11696981941289662175)
XLA Ops:
  22.1 4.0 convolution_bitcast_fusion
  28.1 3.6 squeeze.90
  34.4 3.4 squeeze.89
  37.8 3.7 fusion.101
  43.1 18.1 %while.34 = (s32[]{:T(128)}, bf16[2,512,6,64]{1,3,2,0:T(8,128)(2,1)}, bf16[2,512,6,16]{1,3,2,0:T(8,128)(2,1)}, f32[2,6,512,1]{2,1,3,0:T(8,128)}, bf16[2,512,6,64...) while((s32[]{:T(128)}, ...), condition=%wide.region_3.4_spmd, body=%wide.region_0.3_spmd.sunk | while | flops 519287808 | bytes 54970212 | solution.py:210
  68.3 8.6 reduce-scatter.12.cloned.1.call-done
  83.1 9.9 %all-gather.7.cloned.1.call-done = bf16[1024,768]{1,0:T(8,128)(2,1)} async-done(((bf16[512,768]{1,0:T(8,128)(2,1)}), bf16[1024,768]{1,0:T(8,128)(2,1)}) %all-gather.7.cloned.1.call-update) | async-done | bytes 1572880 | tf_op jit(solution)/shard_map/all_gather | solution.py:240
  93.0 7.1 multiply_convert_fusion.1
  101.7 3.7 convolution_convert_fusion.4
  139.9 8.2 convert_reduce_fusion
  149.7 3.7 convolution_convert_fusion.3
  171.6 3.7 reduce-scatter.22.cloned.1.call-done
  182.1 6.1 all-gather.11.cloned.1.call-done
  196.7 32.9 %while.35 = (s32[]{:T(128)}, bf16[2,512,6,64]{1,3,2,0:T(8,128)(2,1)}, bf16[2,512,6,64]{1,3,2,0:T(8,128)(2,1)}, bf16[2,512,6,64]{1,3,2,0:T(8,128)(2,1)}, bf16[2,5...) while((s32[]{:T(128)}, ...), condition=%wide.region_28.29_spmd, body=%wide.region_26.28_spmd.sunk | while | flops 1279964160 | bytes 114307136 | solution.py:321
  256.3 6.6 copy.128
  265.6 3.5 fusion.149
  269.1 6.5 fusion.151
  277.5 5.8 fusion.150
  285.4 43.8 %all-reduce.1 = (f32[2,768]{1,0:T(2,128)}, f32[2,768]{1,0:T(2,128)}, f32[2,768]{1,0:T(2,128)}, f32[2,192]{1,0:T(2,128)}, f32[2,192]{1,0:T(2,128)}, /*index=5*/f32[2,192]{1,0:T(2,128)}) all-reduce(f32[2,768]{1,0:T(2,128)S(1)} %pad_maximum_fusion.2, f32[2,768]{1,0:T(2,128)S(1)} %pad_maximum_fusion.3, ...), channel_id=1, replica_groups=mesh['dp'=16,'mp'=2] {'dp','mp'}, use_global_device_ids=true, to_apply=%region_38.39 | all-reduce | flops 5760 | bytes 46080 | tf_op jit(solution)/shard_map/psum | solution.py:375
  330.2 76.2 %all-reduce.2 = (f32[2,384]{1,0:T(2,128)}, f32[1536]{0:T(1024)}, f32[2,96]{1,0:T(2,128)}, f32[384]{0:T(512)}) all-reduce(f32[2,384]{1,0:T(2,128)S(1)} %pad_maximum_fusion.5, f32[1536]{0:T(1024)S(1)} %copy-done.120, f32[2,96]{1,0:T(2,128)S(1)} %pad_maximum_fusion.9, f32[384]{0:T(512)S(1)} %copy-done.131), channel_id=1, replica_groups=mesh['dp'=16,'mp'=2] {'dp'}, use_global_device_ids=true, to_apply=%region_34.35 | all-reduce | flops 2880 | bytes 23040 | tf_op jit(solution)/shard_map/psum | solution.py:350
  411.1 58.9 %all-reduce.6.cloned.1.call-done = (f32[3,768,384]{2,0,1:T(4,128)}, f32[3,192,96]{1,2,0:T(8,128)}, f32[96,192]{1,0:T(8,128)}, f32[192,384]{1,0:T(8,128)}, f32[384,192]{0,1:T(8,128)}) async-done(((f32[3,768,384]{2,0,1:T(4,128)}, f32[3,192,96]{1,2,0:T(8,128)}, f32[96,192]{1,0:T(8,128)}, f32[192,384]{1,0:T(8,128)}, f32[384,192]{0,1:T(8,128)}), (f32[3,768,384]{2,0,1:T(4,128)}, f32[3,192,96]{1,2,0:T(8,128)}, ...) | async-done | bytes 4423696
  473.6 125.7 %reduce-scatter.28.cloned.1.call-done = f32[384,48]{0,1:T(8,128)} async-done(((f32[384,768]{0,1:T(8,128)}), f32[384,48]{0,1:T(8,128)}) %reduce-scatter.28.cloned.1.call-update) | async-done | bytes 73744 | tf_op jit(solution)/shard_map/reduce_scatter | solution.py:346
  599.3 143.1 %reduce-scatter.32.cloned.1.call-done = f32[1536,48]{0,1:T(8,128)} async-done(((f32[1536,768]{0,1:T(8,128)}), f32[1536,48]{0,1:T(8,128)}) %reduce-scatter.32.cloned.1.call-update) | async-done | bytes 294928 | tf_op jit(solution)/shard_map/reduce_scatter | solution.py:348
  742.4 143.4 %reduce-scatter.30.cloned.1.call-done = f32[48,1536]{1,0:T(8,128)} async-done(((f32[768,1536]{1,0:T(8,128)}), f32[48,1536]{1,0:T(8,128)}) %reduce-scatter.30.cloned.1.call-update) | async-done | bytes 294928 | tf_op jit(solution)/shard_map/reduce_scatter | solution.py:347
  (559 shorter events, 198.7 us)
Async XLA Ops:
  7.2 85.8 %copy-start = (bf16[768,1536]{1,0:T(8,128)(2,1)S(1)}, bf16[768,1536]{1,0:T(8,128)(2,1)}, u32[]{:S(2)}) copy-start(bf16[768,1536]{1,0:T(8,128)(2,1)} %param.36) | copy-start | bytes 7077892
  7.2 14.9 %all-gather.5.cloned.1.call-start = ((), (), s32[]{:S(2)}) async-start(), calls=%async_computation.11 | async-start | bytes 2359296 | tf_op jit(solution)/shard_map/all_gather | solution.py:194
  7.9 69.0 %reduce-scatter.12.cloned.1.call-start = ((), (), s32[]{:S(2)}) async-start(), calls=%async_computation.12 | async-start | bytes 2359296 | tf_op jit(solution)/shard_map/reduce_scatter | solution.py:216
  66.5 26.4 %all-gather.7.cloned.1.call-start = ((), (), s32[]{:S(2)}) async-start(), calls=%async_computation.13 | async-start | bytes 2359296 | tf_op jit(solution)/shard_map/all_gather | solution.py:240
  81.7 34.0 %reduce-scatter.14.cloned.1.call-start = ((), (), s32[]{:S(2)}) async-start(), calls=%async_computation.14 | async-start | bytes 2359296 | tf_op jit(solution)/shard_map/reduce_scatter | solution.py:250
  105.4 21.6 %reduce-scatter.16.cloned.1.call-start = ((), (), s32[]{:S(2)}) async-start(), calls=%async_computation.15 | async-start | bytes 589824 | tf_op jit(solution)/shard_map/reduce_scatter | solution.py:219
  114.4 25.5 %all-gather.9.cloned.1.call-start = ((), (), s32[]{:S(2)}) async-start(), calls=%async_computation.17 | async-start | bytes 2359296 | tf_op jit(solution)/shard_map/all_gather | solution.py:275
  125.1 28.5 %reduce-scatter.18.cloned.1.call-start = ((), (), s32[]{:S(2)}) async-start(), calls=%async_computation.16 | async-start | bytes 589824 | tf_op jit(solution)/shard_map/reduce_scatter | solution.py:253
  138.0 26.1 %reduce-scatter.20.cloned.1.call-start = ((), (), s32[]{:S(2)}) async-start(), calls=%async_computation.18 | async-start | bytes 2359296 | tf_op jit(solution)/shard_map/reduce_scatter | solution.py:285
  153.5 21.7 %reduce-scatter.22.cloned.1.call-start = ((), (), s32[]{:S(2)}) async-start(), calls=%async_computation.20 | async-start | bytes 589824 | tf_op jit(solution)/shard_map/reduce_scatter | solution.py:288
  164.1 24.1 %all-gather.11.cloned.1.call-start = ((), (), s32[]{:S(2)}) async-start(), calls=%async_computation.19 | async-start | bytes 2359296 | tf_op jit(solution)/shard_map/all_gather | solution.py:301
  171.6 234.9 %reduce-scatter.26.cloned.1.call-start = ((), (), s32[]{:S(2)}) async-start(), calls=%async_computation.22 | async-start | bytes 589824 | tf_op jit(solution)/shard_map/reduce_scatter | solution.py:338
  238.8 169.3 %reduce-scatter.24.cloned.1.call-start = ((), (), s32[]{:S(2)}) async-start(), calls=%async_computation.21 | async-start | bytes 2359296 | tf_op jit(solution)/shard_map/reduce_scatter | solution.py:335
  244.9 225.0 %all-reduce.6.cloned.1.call-start = ((), (), s32[]{:S(2)}) async-start(), calls=%async_computation.26 | async-start | bytes 11403264
  264.5 334.8 %reduce-scatter.28.cloned.1.call-start = ((), (), s32[]{:S(2)}) async-start(), calls=%async_computation.23 | async-start | bytes 1253376 | tf_op jit(solution)/shard_map/reduce_scatter | solution.py:346
  269.1 473.4 %reduce-scatter.32.cloned.1.call-start = ((), (), s32[]{:S(2)}) async-start(), calls=%async_computation.25 | async-start | bytes 5013504 | tf_op jit(solution)/shard_map/reduce_scatter | solution.py:348
  275.6 610.2 %reduce-scatter.30.cloned.1.call-start = ((), (), s32[]{:S(2)}) async-start(), calls=%async_computation.24 | async-start | bytes 5013504 | tf_op jit(solution)/shard_map/reduce_scatter | solution.py:347
  283.4 123.0 %copy-start.31 = (f32[512,192]{0,1:T(8,128)S(1)}, f32[512,192]{0,1:T(8,128)}, u32[]{:S(2)}) copy-start(f32[512,192]{0,1:T(8,128)} %copy-done.30) | copy-start | bytes 1179652
  283.4 123.0 %copy-start.103 = (f32[512]{0:T(512)S(1)}, f32[512]{0:T(512)}, u32[]{:S(2)}) copy-start(f32[512]{0:T(512)} %copy-done.102) | copy-start | bytes 6148
  283.5 124.7 %copy-start.109 = (f32[512]{0:T(512)S(1)}, f32[512]{0:T(512)}, u32[]{:S(2)}) copy-start(f32[512]{0:T(512)} %copy-done.108) | copy-start | bytes 6148
  408.1 479.8 %copy-start.1 = (bf16[768,1536]{1,0:T(8,128)(2,1)S(1)}, bf16[768,1536]{1,0:T(8,128)(2,1)}, u32[]{:S(2)}) copy-start(bf16[768,1536]{1,0:T(8,128)(2,1)} %param.36) | copy-start | bytes 7077892
  470.0 415.9 %copy-start.83 = (f32[96,192]{1,0:T(8,128)S(1)}, f32[96,192]{1,0:T(8,128)}, u32[]{:S(2)}) copy-start(f32[96,192]{1,0:T(8,128)} %get-tuple-element.758) | copy-start | bytes 221188
  470.0 416.5 %copy-start.75 = (f32[192,384]{1,0:T(8,128)S(1)}, f32[192,384]{1,0:T(8,128)}, u32[]{:S(2)}) copy-start(f32[192,384]{1,0:T(8,128)} %get-tuple-element.760) | copy-start | bytes 884740
  470.0 417.2 %copy-start.74 = (f32[384,192]{0,1:T(8,128)S(1)}, f32[384,192]{0,1:T(8,128)}, u32[]{:S(2)}) copy-start(f32[384,192]{0,1:T(8,128)} %get-tuple-element.762) | copy-start | bytes 884740
  (152 other events, 583.7 us)
Sparse Core Ops, SparseCore 0:
  9.6 12.5 all-gather.4
  66.7 10.2 reduce-scatter.11
  81.9 11.0 all-gather.6
  105.5 10.2 reduce-scatter.13
  117.8 9.1 reduce-scatter.15
  128.9 10.8 all-gather.8
  142.1 8.9 reduce-scatter.17
  153.7 10.2 reduce-scatter.19
  166.1 9.0 reduce-scatter.21
  177.2 10.9 all-gather.10
  238.9 8.9 reduce-scatter.25
  250.0 10.1 reduce-scatter.23
  267.8 202.1 all-reduce.5
  475.1 124.1 reduce-scatter.27
  604.9 137.4 reduce-scatter.31
  748.0 137.7 reduce-scatter.29
where the time goes:
time: 900 us; the launch traced here: 895 us
  waiting for transfers between devices  507 us (56%)
  blocking collectives  129 us (14%)
  matrix products  105 us (12%)
  local copies, waits for them, and re-layouts  79.5 us (9%)
  other arithmetic  55.6 us (6%)
  between operations  16.5 us (2%)
    reduce_scatter x1, waiting for transfers between devices, body(): lax.psum_scatter(text_wup_grad, 'dp', scatter_dimension=0, tiled=True)  143 us
    reduce_scatter x1, waiting for transfers between devices, body(): lax.psum_scatter(text_wdown_grad, 'dp', scatter_dimension=1, tiled=True)  143 us
    reduce_scatter x1, waiting for transfers between devices, body(): lax.psum_scatter(text_wout_grad, 'dp', scatter_dimension=1, tiled=True)  126 us
    psum x1, blocking collectives, body(): lax.psum((text_qvbias_grad, text_upbias_grad, layout_qkv_grad, layout_qvb...  76.2 us
    unnamed x17, waiting for transfers between devices  59.8 us
    psum x1, blocking collectives, body(): lax.psum((text_outbias_part, jnp.stack([text_gain_first, text_gain_second...  43.8 us
    unnamed x251, local copies, waits for them, and re-layouts  27.7 us
  transfers between devices with their start and end apart: 16, of which 12 were waited for; matrix products, arithmetic and copies ran while one was open for 13% of the time, Pallas kernels for 0%

commit v1 on v0

--- a/solution.py
+++ b/solution.py
@@ -126,8 +126,8 @@
     return (active_low, gelu_back, jnp.dot(active_low, w_down, preferred_element_type=jnp.float32))
 
 
-def feed_back(full_rows, active_low, gelu_back, full_grad, w_up, w_down):
-    grad_down = jnp.einsum("rf,rd->fd", active_low, full_grad, preferred_element_type=jnp.float32)
+def feed_back(full_rows, active_low, gelu_back, full_grad, w_up, w_down, down_spec="rf,rd->fd"):
+    grad_down = jnp.einsum(down_spec, active_low, full_grad, preferred_element_type=jnp.float32)
     active_grad = jnp.einsum("rd,fd->rf", full_grad, w_down, preferred_element_type=jnp.float32)
     hidden_grad = gelu_back(active_grad)[0].astype(jnp.bfloat16)
     grad_up = jnp.einsum("rd,rf->df", full_rows, hidden_grad, preferred_element_type=jnp.float32)
@@ -136,12 +136,13 @@
     return (grad_up, grad_bias, grad_down, normed_part)
 
 
-def input_back(rows, weight_qkv, query_grad, key_grad, value_grad):
+def input_back(rows, weight_qkv, query_grad, key_grad, value_grad, stack_axis=0):
     grad_qkv = jnp.stack(
         [
             jnp.einsum("rd,re->de", rows, piece, preferred_element_type=jnp.float32)
             for piece in (query_grad, key_grad, value_grad)
-        ]
+        ],
+        axis=stack_axis,
     )
     input_part = jnp.einsum(
         "re,de->rd", query_grad, weight_qkv[0], preferred_element_type=jnp.float32
@@ -159,6 +160,92 @@
         ]
     )
     return (grad_qkv, grad_bias, input_part)
+
+
+def xor_sum(values, axis, size):
+    step = 1
+    while step < size:
+        values = values + lax.ppermute(
+            values, axis, [(i, i ^ step) for i in range(size)]
+        )
+        step *= 2
+    return values
+
+
+def xor_exchange(values, step, size):
+    return lax.ppermute(values, "dp", [(i, i ^ step) for i in range(size)])
+
+
+def bit_orders(bits, colours):
+    if bits <= 1:
+        return [list(range(bits))] * colours
+    main = list(range(bits - 1))
+    orders = []
+    for colour in range(colours):
+        shift = colour % len(main)
+        orders.append(main[shift:] + main[:shift] + [bits - 1])
+    return orders
+
+
+def halve(chunk, order, me, size, bits):
+    axes = list(range(bits - 1, -1, -1))
+    for bit in order:
+        where = axes.index(bit)
+        mine = (me >> bit) & 1
+        keep = lax.dynamic_index_in_dim(chunk, mine, axis=where, keepdims=False)
+        send = lax.dynamic_index_in_dim(chunk, 1 - mine, axis=where, keepdims=False)
+        chunk = keep + xor_exchange(send, 1 << bit, size)
+        axes.pop(where)
+    return chunk
+
+
+def double(block, order, me, size, bits):
+    held = []
+    for bit in reversed(order):
+        other = xor_exchange(block, 1 << bit, size)
+        mine = (me >> bit) & 1
+        block = jnp.where(mine == 0, jnp.stack([block, other]), jnp.stack([other, block]))
+        held.insert(0, bit)
+    canonical = list(range(bits - 1, -1, -1))
+    block = jnp.transpose(block, [held.index(bit) for bit in canonical] + [len(held)])
+    return block.reshape(-1)
+
+
+def dp_reduce(scattered, replicated, size, colours=3):
+    bits = size.bit_length() - 1
+    me = lax.axis_index("dp")
+    rows = [piece.reshape(size, -1) for piece in scattered]
+    widths = [row.shape[1] for row in rows]
+    flat = jnp.concatenate([piece.reshape(-1) for piece in replicated])
+    pad = (-flat.shape[0]) % size
+    flat = jnp.pad(flat, (0, pad))
+    rep_width = flat.shape[0] // size
+    joined = jnp.concatenate(rows + [flat.reshape(size, rep_width)], axis=1)
+    total = joined.shape[1]
+    bounds = [total * colour // colours for colour in range(colours + 1)]
+    bounds = [bound // 128 * 128 for bound in bounds[:-1]] + [total]
+    orders = bit_orders(bits, colours)
+    shaped = joined.reshape((2,) * bits + (total,))
+    reduced = jnp.concatenate(
+        [
+            halve(shaped[..., bounds[c] : bounds[c + 1]], orders[c], me, size, bits)
+            for c in range(colours)
+        ]
+    )
+    scattered_out = []
+    offset = 0
+    for piece, width in zip(scattered, widths):
+        share = reduced[offset : offset + width]
+        scattered_out.append(share.reshape((piece.shape[0] // size,) + piece.shape[1:]))
+        offset += width
+    rep_block = reduced[offset : offset + rep_width]
+    full = double(rep_block, orders[0], me, size, bits)[: flat.shape[0] - pad]
+    replicated_out = []
+    offset = 0
+    for piece in replicated:
+        replicated_out.append(full[offset : offset + piece.size].reshape(piece.shape))
+        offset += piece.size
+    return scattered_out, replicated_out
 
 
 def body(
@@ -275,8 +362,8 @@
         lax.all_gather(text_branch_grad, "mp", axis=0, tiled=True),
         lax.all_gather(layout_branch_grad, "mp", axis=0, tiled=True),
     )
-    text_wup_grad, text_upbias_grad, text_wdown_grad, text_normed_part = feed_back(
-        text_full, text_active, text_gelu_back, text_full_grad, text_wup, text_wdown
+    text_wup_grad, text_upbias_grad, text_wdown_grad_t, text_normed_part = feed_back(
+        text_full, text_active, text_gelu_back, text_full_grad, text_wup, text_wdown, "rf,rd->df"
     )
     layout_wup_grad, layout_upbias_grad, layout_wdown_grad, layout_normed_part = feed_back(
         layout_full, layout_active, layout_gelu_back, layout_full_grad, layout_wup, layout_wdown
@@ -301,8 +388,8 @@
         lax.all_gather(text_mixed_low, "mp", axis=0, tiled=True),
         lax.all_gather(layout_mixed_low, "mp", axis=0, tiled=True),
     )
-    text_wout_grad = jnp.einsum(
-        "re,rd->ed", text_context, text_wide_grad, preferred_element_type=jnp.float32
+    text_wout_grad_t = jnp.einsum(
+        "re,rd->de", text_context, text_wide_grad, preferred_element_type=jnp.float32
     )
     layout_wout_grad = jnp.einsum(
         "re,rd->ed", layout_context, layout_wide_grad, preferred_element_type=jnp.float32
@@ -321,8 +408,13 @@
     text_qgrad, text_kgrad, text_vgrad, layout_qgrad, layout_kgrad, layout_vgrad = lax.map(
         attend_back, back_blocks
     )
-    text_qkv_grad, text_qvbias_grad, text_input_part = input_back(
-        text_rows, text_qkv, unblocked(text_qgrad), unblocked(text_kgrad), unblocked(text_vgrad)
+    text_qkv_grad_t, text_qvbias_grad, text_input_part = input_back(
+        text_rows,
+        text_qkv,
+        unblocked(text_qgrad),
+        unblocked(text_kgrad),
+        unblocked(text_vgrad),
+        stack_axis=1,
     )
     layout_qkv_grad, layout_qvbias_grad, layout_input_part = input_back(
         layout_rows,
@@ -341,48 +433,62 @@
     )
     text_dinput = (text_mixed_grad + text_input_sum).astype(jnp.bfloat16)
     layout_dinput = (layout_mixed_grad + layout_input_sum).astype(jnp.bfloat16)
-    qkv_share, wout_share, wup_share, wdown_share = (
-        lax.psum_scatter(text_qkv_grad, "dp", scatter_dimension=1, tiled=True),
-        lax.psum_scatter(text_wout_grad, "dp", scatter_dimension=1, tiled=True),
-        lax.psum_scatter(text_wup_grad, "dp", scatter_dimension=0, tiled=True),
-        lax.psum_scatter(text_wdown_grad, "dp", scatter_dimension=1, tiled=True),
-    )
-    summed = lax.psum(
-        (
-            text_qvbias_grad,
-            text_upbias_grad,
-            layout_qkv_grad,
-            layout_qvbias_grad,
-            layout_wout_grad,
-            layout_wup_grad,
-            layout_upbias_grad,
-            layout_wdown_grad,
-        ),
-        "dp",
-    )
-    text_outbias_part = jnp.stack(
+    n_dp = lax.axis_size("dp")
+    n_mp = lax.axis_size("mp")
+    small = jnp.concatenate(
         [
-            jnp.sum(text_mixed_low, axis=0, dtype=jnp.float32),
-            jnp.sum(text_branch_grad, axis=0, dtype=jnp.float32),
+            part.reshape(-1)
+            for part in (
+                jnp.stack(
+                    [
+                        jnp.sum(text_mixed_low, axis=0, dtype=jnp.float32),
+                        jnp.sum(text_branch_grad, axis=0, dtype=jnp.float32),
+                    ]
+                ),
+                jnp.stack([text_gain_first, text_gain_second]),
+                jnp.stack([text_shift_first, text_shift_second]),
+                jnp.stack(
+                    [
+                        jnp.sum(layout_mixed_low, axis=0, dtype=jnp.float32),
+                        jnp.sum(layout_branch_grad, axis=0, dtype=jnp.float32),
+                    ]
+                ),
+                jnp.stack([layout_gain_first, layout_gain_second]),
+                jnp.stack([layout_shift_first, layout_shift_second]),
+            )
         ]
     )
-    layout_outbias_part = jnp.stack(
-        [
-            jnp.sum(layout_mixed_low, axis=0, dtype=jnp.float32),
-            jnp.sum(layout_branch_grad, axis=0, dtype=jnp.float32),
-        ]
-    )
-    shared = lax.psum(
-        (
-            text_outbias_part,
-            jnp.stack([text_gain_first, text_gain_second]),
-            jnp.stack([text_shift_first, text_shift_second]),
-            layout_outbias_part,
-            jnp.stack([layout_gain_first, layout_gain_second]),
-            jnp.stack([layout_shift_first, layout_shift_second]),
-        ),
-        ("dp", "mp"),
-    )
+    small = xor_sum(small, "mp", n_mp)
+    scattered = (
+        text_qkv_grad_t,
+        text_wout_grad_t,
+        text_wup_grad,
+        text_wdown_grad_t,
+    )
+    replicated = (
+        text_qvbias_grad,
+        text_upbias_grad,
+        layout_qkv_grad,
+        layout_qvbias_grad,
+        layout_wout_grad,
+        layout_wup_grad,
+        layout_upbias_grad,
+        layout_wdown_grad,
+        small,
+    )
+    scattered_out, replicated_out = dp_reduce(scattered, replicated, n_dp)
+    qkv_share = jnp.transpose(scattered_out[0], (1, 0, 2))
+    wout_share = scattered_out[1].T
+    wup_share = scattered_out[2]
+    wdown_share = scattered_out[3].T
+    summed = replicated_out[:8]
+    small_sum = replicated_out[8]
+    sizes = (2 * D, 2 * D, 2 * D, 2 * DL, 2 * DL, 2 * DL)
+    shared = []
+    offset = 0
+    for size in sizes:
+        shared.append(small_sum[offset : offset + size].reshape(2, -1))
+        offset += size
     return (
         text_final.astype(jnp.bfloat16),
         layout_final.astype(jnp.bfloat16),

time: 900 us -> 640 us (0.71)
  waiting for transfers between devices: 507 us -> 183 us
  blocking collectives: 129 us -> 8.85 us
  local copies, waits for them, and re-layouts: 79.5 us -> 178 us
  other arithmetic: 55.6 us -> 112 us
  starting transfers between devices: 1.13 us -> 24.8 us
    reduce_scatter x3 -> x0, waiting for transfers between devices: 412 us -> none  [the longest x1 143 us: body(): lax.psum_scatter(text_wup_grad, 'dp', scatter_dimension=0, tiled=True)]
    ppermute x0 -> x17, waiting for transfers between devices: none -> 166 us  [the longest x16 166 us: xor_exchange(): return lax.ppermute(values, 'dp', [(i, i ^ step) for i in range(size)])]
    psum x2 -> x0, blocking collectives: 120 us -> none  [the longest x1 76.2 us: body(): lax.psum((text_qvbias_grad, text_upbias_grad, layout_qkv_grad, layout_qvb...]
    unnamed x17 -> x12, waiting for transfers between devices: 59.8 us -> 0.86 us
    concatenate x0 -> x7, local copies, waits for them, and re-layouts: none -> 34.3 us  [the longest x5 27.6 us: dp_reduce(): joined = jnp.concatenate(rows + [flat.reshape(size, rep_width)], axis=1)]
    dynamic_slice x0 -> x9, local copies, waits for them, and re-layouts: none -> 23.8 us  [the longest x6 18.6 us: halve(): keep = lax.dynamic_index_in_dim(chunk, mine, axis=where, keepdims=False)]
    ppermute x0 -> x17, starting transfers between devices: none -> 23.4 us  [the longest x16 23.3 us: xor_exchange(): return lax.ppermute(values, 'dp', [(i, i ^ step) for i in range(size)])]
    add x0 -> x13, other arithmetic: none -> 21.6 us  [the longest x12 21 us: halve(): chunk = keep + xor_exchange(send, 1 << bit, size)]
  transfers between devices with their start and end apart: 16 -> 29, of which waited for: 12 -> 19; matrix products, arithmetic and copies ran while one was open for 13% -> 37% of each run, Pallas kernels for 0% -> 0%
where the time goes in v1:
time: 640 us; the launch traced here: 633 us
  waiting for transfers between devices  183 us (29%)
  local copies, waits for them, and re-layouts  178 us (28%)
  other arithmetic  112 us (18%)
  matrix products  109 us (17%)
  starting transfers between devices  24.8 us (4%)
  between operations  16 us (2%)
  blocking collectives  8.85 us (1%)
    ppermute x16, waiting for transfers between devices, xor_exchange(): return lax.ppermute(values, 'dp', [(i, i ^ step) for i in range(size)])  166 us
    unnamed x201, local copies, waits for them, and re-layouts  29.4 us
    concatenate x5, local copies, waits for them, and re-layouts, dp_reduce(): joined = jnp.concatenate(rows + [flat.reshape(size, rep_width)], axis=1)  27.6 us
    ppermute x16, starting transfers between devices, xor_exchange(): return lax.ppermute(values, 'dp', [(i, i ^ step) for i in range(size)])  23.3 us
    add x12, other arithmetic, halve(): chunk = keep + xor_exchange(send, 1 << bit, size)  21 us
    dynamic_slice x6, local copies, waits for them, and re-layouts, halve(): keep = lax.dynamic_index_in_dim(chunk, mine, axis=where, keepdims=False)  18.6 us
    reduce_sum x8, other arithmetic, layer_norm(): centered = values - jnp.mean(values, axis=-1, keepdims=True)  14.4 us
  transfers between devices with their start and end apart: 29, of which 19 were waited for; matrix products, arithmetic and copies ran while one was open for 37% of the time, Pallas kernels for 0%

profile of v1, /device:TPU:0, one launch (start us, length us, event | category | flops | bytes accessed | tf_op | source)
XLA Modules:
  0.0 633.3 jit_solution(15449891833704998443)
XLA Ops:
  43.2 18.1 %while.34 = (s32[]{:T(128)}, bf16[2,512,6,64]{1,3,2,0:T(8,128)(2,1)}, bf16[2,512,6,16]{1,3,2,0:T(8,128)(2,1)}, f32[2,6,512,1]{2,1,3,0:T(8,128)}, bf16[2,512,6,64...) while((s32[]{:T(128)}, ...), condition=%wide.region_3.4_spmd, body=%wide.region_0.3_spmd.sunk | while | flops 519287808 | bytes 54970212 | solution.py:297
  83.6 5.3 reduce-scatter.13.cloned.1.call-done
  101.8 7.1 %multiply_convert_fusion.1 = (bf16[1024,1536]{1,0:T(8,128)(2,1)S(1)}, f32[1024,1536]{1,0:T(8,128)}) fusion(f32[1536]{0:T(1024)} %convert_element_type.271, bf16[1024,768]{1,0:T(8,128)(2,1)} %all-gather.7.cloned.1.call-done, bf16[768,1536]{1,0:T(8,128)(2,1)S(1)} %copy-done), kind=kOutput, calls=%fused_computation.103 | convolution fusion | flops 2425356288 | bytes 13375488 | tf_op jit(solution)/shard_map/dot_general | solution.py:123
  118.9 6.9 %reduce-scatter.11.cloned.1.call-done = bf16[512,768]{1,0:T(8,128)(2,1)} async-done(((bf16[1024,768]{1,0:T(8,128)(2,1)}), bf16[512,768]{1,0:T(8,128)(2,1)}) %reduce-scatter.11.cloned.1.call-update) | async-done | bytes 786448 | tf_op jit(solution)/shard_map/reduce_scatter | solution.py:337
  147.1 7.2 %fusion.164 = f32[768,1536]{1,0:T(8,128)} fusion(bf16[1024,768]{1,0:T(8,128)(2,1)} %all-gather.9.cloned.1.call-done, bf16[1024,1536]{1,0:T(8,128)(2,1)} %copy-done.39), kind=kOutput, calls=%fused_computation.347 | convolution fusion | flops 2415919104 | bytes 9437184 | tf_op jit(solution)/shard_map/rf,rd->df/dot_general | solution.py:130
  154.2 8.5 %concatenate.116 = f32[2,2,2,2,73728]{4,3,2,1,0:T(2,128)} reshape(f32[768,1536]{1,0:T(8,128)} %fusion.164) | data formatting | bytes 9437184 | tf_op jit(solution)/shard_map/concatenate | solution.py:223
  162.7 8.3 %convert_reduce_fusion = (f32[1536]{0:T(1024)}, bf16[1024,1536]{1,0:T(8,128)(2,1)S(1)}) fusion(f32[1024,1536]{1,0:T(8,128)} %get-tuple-element.430, f32[1536]{0:T(1024)} %convert_element_type.271, bf16[1024,768]{1,0:T(8,128)(2,1)} %all-gather.9.cloned.1.call-done, bf16[1536,768]{1,0:T(8,128)(2,1)} %param.38), kind=kOutput, calls=%fused_computation.101 | convolution fusion | flops 2441083392 | bytes 13381632 | tf_op jit(solution)/shard_map/rd,fd->rf/dot_general | solution.py:131
  177.0 8.4 %concatenate.114 = f32[2,2,2,2,73728]{4,3,2,1,0:T(2,128)} reshape(f32[768,1536]{1,0:T(8,128)} %fusion.163) | data formatting | bytes 9437184 | tf_op jit(solution)/shard_map/concatenate | solution.py:223
  218.6 5.7 convolution_convert_fusion.3
  224.6 22.2 %collective-permute-done.13 = f32[2,2,2,78464]{3,2,1,0:T(2,128)} collective-permute-done((f32[2,2,2,78464]{3,2,1,0:T(2,128)}, f32[2,2,2,78464]{3,2,1,0:T(2,128)}, u32[]{:S(2)}, u32[]{:S(2)}) %collective-permute-start.13) | collective-permute-done | bytes 2510880 | tf_op jit(solution)/shard_map/ppermute | solution.py:176
  269.7 13.0 %collective-permute-done.14 = f32[2,2,78464]{2,1,0:T(2,128)} collective-permute-done((f32[2,2,78464]{2,1,0:T(2,128)}, f32[2,2,78464]{2,1,0:T(2,128)}, u32[]{:S(2)}, u32[]{:S(2)}) %collective-permute-start.14) | collective-permute-done | bytes 1255456 | tf_op jit(solution)/shard_map/ppermute | solution.py:176
  289.1 13.0 %collective-permute-done.15 = f32[2,78464]{1,0:T(2,128)S(1)} collective-permute-done((f32[2,78464]{1,0:T(2,128)S(1)}, f32[2,78464]{1,0:T(2,128)S(1)}, u32[]{:S(2)}, u32[]{:S(2)}) %collective-permute-start.15) | collective-permute-done | bytes 627744 | tf_op jit(solution)/shard_map/ppermute | solution.py:176
  310.2 10.0 %collective-permute-done.16 = f32[78464]{0:T(1024)S(1)} collective-permute-done((f32[78464]{0:T(1024)S(1)}, f32[78464]{0:T(1024)S(1)}, u32[]{:S(2)}, u32[]{:S(2)}) %collective-permute-start.16) | collective-permute-done | bytes 313888 | tf_op jit(solution)/shard_map/ppermute | solution.py:176
  329.5 33.2 %while.35 = (s32[]{:T(128)}, bf16[2,512,6,64]{1,3,2,0:T(8,128)(2,1)}, bf16[2,512,6,64]{1,3,2,0:T(8,128)(2,1)}, bf16[2,512,6,64]{1,3,2,0:T(8,128)(2,1)}, bf16[2,5...) while((s32[]{:T(128)}, ...), condition=%wide.region_28.29_spmd, body=%wide.region_26.28_spmd.sunk | while | flops 1279964160 | bytes 114307136 | solution.py:408
  384.7 6.7 %concatenate.118 = f32[229824]{0:T(1024)S(1)} concatenate(f32[768]{0:T(1024)S(1)} %reshape.697, f32[1536]{0:T(1024)S(1)} %copy-done.96, f32[55296]{0:T(1024)S(1)} %reshape.698, f32[192]{0:T(256)S(1)} %reshape.699, f32[18432]{0:T(1024)S(1)} %copy-done.66, f32[73728]{0:T(1024)S(1)} %copy-done.59, f32[384]{0:T(512)S(1)} %copy-done.102, f32[73728]{0:T(1024)} %reshape.702, ...), dimensions={0} | concatenate | bytes 1838592 | tf_op jit(solution)/shard_map/concatenate | solution.py:219
  401.9 6.3 copy.100
  408.2 7.9 %concatenate.112 = f32[2,2,2,2,55296]{4,3,2,1,0:T(2,128)} reshape(f32[768,3,384]{2,1,0:T(4,128)} %copy.100) | data formatting | bytes 7077888 | tf_op jit(solution)/shard_map/concatenate | solution.py:223
  416.1 9.3 %pad_maximum_fusion = f32[2,2,2,2,78464]{4,3,2,1,0:T(2,128)} fusion(f32[2,2,2,2,73728]{4,3,2,1,0:T(2,128)} %concatenate.114, f32[2,2,2,2,18432]{4,3,2,1,0:T(2,128)S(1)} %concatenate.113, f32[2,2,2,2,55296]{4,3,2,1,0:T(2,128)} %concatenate.112), kind=kLoop, calls=%fused_computation.107 | loop fusion | flops 2510848 | bytes 14458880 | tf_op jit(solution)/shard_map/concatenate | solution.py:223
  425.5 9.8 %constant_dynamic-slice_fusion.11 = (f32[2,2,2,1,78464]{4,3,2,1,0:T(1,128)}, f32[2,2,2,1,78464]{4,3,2,1,0:T(1,128)S(1)}) fusion(f32[2,2,2,2,78464]{4,3,2,1,0:T(2,128)} %pad_maximum_fusion, s32[]{:T(128)S(6)} %select_n.140, s32[]{:T(128)S(6)} %select_n.141), kind=kLoop, calls=%fused_computation.282 | loop fusion | bytes 10043400 | tf_op jit(solution)/shard_map/jit(dynamic_index_in_dim)/dynamic_slice | solution.py:195
  448.2 46.0 %collective-permute-done = f32[2,2,2,78464]{3,2,1,0:T(2,128)} collective-permute-done((f32[2,2,2,78464]{3,2,1,0:T(2,128)}, f32[2,2,2,78464]{3,2,1,0:T(2,128)}, u32[]{:S(2)}, u32[]{:S(2)}) %collective-permute-start) | collective-permute-done | bytes 2510880 | tf_op jit(solution)/shard_map/ppermute | solution.py:176
  510.2 19.3 %collective-permute-done.1 = f32[2,2,78464]{2,1,0:T(2,128)S(1)} collective-permute-done((f32[2,2,78464]{2,1,0:T(2,128)S(1)}, f32[2,2,78464]{2,1,0:T(2,128)S(1)}, u32[]{:S(2)}, u32[]{:S(2)}) %collective-permute-start.1) | collective-permute-done | bytes 1255456 | tf_op jit(solution)/shard_map/ppermute | solution.py:176
  540.3 5.7 collective-permute-done.2
  560.4 11.2 %collective-permute-done.3 = f32[78464]{0:T(1024)} collective-permute-done((f32[78464]{0:T(1024)S(1)}, f32[78464]{0:T(1024)}, u32[]{:S(2)}, u32[]{:S(2)}) %collective-permute-start.3) | collective-permute-done | bytes 313888 | tf_op jit(solution)/shard_map/ppermute | solution.py:176
  599.8 6.1 collective-permute-done.12
  (619 shorter events, 372.5 us)
Async XLA Ops:
  7.2 14.9 %all-gather.5.cloned.1.call-start = ((), (), s32[]{:S(2)}) async-start(), calls=%async_computation.8 | async-start | bytes 2359296 | tf_op jit(solution)/shard_map/all_gather | solution.py:281
  7.9 70.7 %reduce-scatter.9.cloned.1.call-start = ((), (), s32[]{:S(2)}) async-start(), calls=%async_computation.9 | async-start | bytes 2359296 | tf_op jit(solution)/shard_map/reduce_scatter | solution.py:303
  66.5 22.3 %reduce-scatter.13.cloned.1.call-start = ((), (), s32[]{:S(2)}) async-start(), calls=%async_computation.12 | async-start | bytes 589824 | tf_op jit(solution)/shard_map/reduce_scatter | solution.py:306
  78.5 23.2 %all-gather.7.cloned.1.call-start = ((), (), s32[]{:S(2)}) async-start(), calls=%async_computation.10 | async-start | bytes 2359296 | tf_op jit(solution)/shard_map/all_gather | solution.py:327
  83.5 30.9 %reduce-scatter.15.cloned.1.call-start = ((), (), s32[]{:S(2)}) async-start(), calls=%async_computation.13 | async-start | bytes 589824 | tf_op jit(solution)/shard_map/reduce_scatter | solution.py:340
  99.9 25.9 %reduce-scatter.11.cloned.1.call-start = ((), (), s32[]{:S(2)}) async-start(), calls=%async_computation.11 | async-start | bytes 2359296 | tf_op jit(solution)/shard_map/reduce_scatter | solution.py:337
  114.3 32.8 %all-gather.9.cloned.1.call-start = ((), (), s32[]{:S(2)}) async-start(), calls=%async_computation.14 | async-start | bytes 2359296 | tf_op jit(solution)/shard_map/all_gather | solution.py:362
  135.0 61.3 %reduce-scatter.19.cloned.1.call-start = ((), (), s32[]{:S(2)}) async-start(), calls=%async_computation.17 | async-start | bytes 589824 | tf_op jit(solution)/shard_map/reduce_scatter | solution.py:375
  146.8 108.3 %reduce-scatter.17.cloned.1.call-start = ((), (), s32[]{:S(2)}) async-start(), calls=%async_computation.15 | async-start | bytes 2359296 | tf_op jit(solution)/shard_map/reduce_scatter | solution.py:372
  189.8 57.0 %collective-permute-start.13 = (f32[2,2,2,78464]{3,2,1,0:T(2,128)}, f32[2,2,2,78464]{3,2,1,0:T(2,128)}, u32[]{:S(2)}, u32[]{:S(2)}) collective-permute-start(f32[2,2,2,78464]{3,2,1,0:T(2,128)} %fusion.102), channel_id=1, source_target_pairs={{0,4},{2,6},{4,0},{6,2},{8,12},{10,14},{12,8},{14,10},{16,20},{18,... | collective-permute-start | bytes 7532552 | tf_op jit(solution)/shard_map/ppermute | solution.py:176
  224.3 96.6 %all-gather.11.cloned.1.call-start = ((), (), s32[]{:S(2)}) async-start(), calls=%async_computation.16 | async-start | bytes 2359296 | tf_op jit(solution)/shard_map/all_gather | solution.py:388
  253.4 29.3 %collective-permute-start.14 = (f32[2,2,78464]{2,1,0:T(2,128)}, f32[2,2,78464]{2,1,0:T(2,128)}, u32[]{:S(2)}, u32[]{:S(2)}) collective-permute-start(f32[2,2,78464]{2,1,0:T(2,128)} %dynamic-slice_bitcast_fusion.1), channel_id=1, source_target_pairs={{0,8},{2,10},{4,12},{6,14},{8,0},{10,2},{12,4},{14,6},{16,24},{18,... | collective-permute-start | bytes 3766280 | tf_op jit(solution)/shard_map/ppermute | solution.py:176
  269.6 286.8 %reduce-scatter.23.cloned.1.call-start = ((), (), s32[]{:S(2)}) async-start(), calls=%async_computation.19 | async-start | bytes 589824 | tf_op jit(solution)/shard_map/reduce_scatter | solution.py:430
  287.3 14.7 %collective-permute-start.15 = (f32[2,78464]{1,0:T(2,128)S(1)}, f32[2,78464]{1,0:T(2,128)S(1)}, u32[]{:S(2)}, u32[]{:S(2)}) collective-permute-start(f32[2,78464]{1,0:T(2,128)S(1)} %bitcast.463), channel_id=1, source_target_pairs={{0,2},{2,0},{4,6},{6,4},{8,10},{10,8},{12,14},{14,12},{16,18},{18,... | collective-permute-start | bytes 1883144 | tf_op jit(solution)/shard_map/ppermute | solution.py:176
  305.4 14.8 %collective-permute-start.16 = (f32[78464]{0:T(1024)S(1)}, f32[78464]{0:T(1024)S(1)}, u32[]{:S(2)}, u32[]{:S(2)}) collective-permute-start(f32[78464]{0:T(1024)S(1)} %get-tuple-element.292), channel_id=1, source_target_pairs={{0,16},{2,18},{4,20},{6,22},{8,24},{10,26},{12,28},{14,30},{16,0},... | collective-permute-start | bytes 941576 | tf_op jit(solution)/shard_map/ppermute | solution.py:176
  395.6 162.5 %reduce-scatter.21.cloned.1.call-start = ((), (), s32[]{:S(2)}) async-start(), calls=%async_computation.18 | async-start | bytes 2359296 | tf_op jit(solution)/shard_map/reduce_scatter | solution.py:427
  438.0 56.1 %collective-permute-start = (f32[2,2,2,78464]{3,2,1,0:T(2,128)}, f32[2,2,2,78464]{3,2,1,0:T(2,128)}, u32[]{:S(2)}, u32[]{:S(2)}) collective-permute-start(f32[2,2,2,78464]{3,2,1,0:T(2,128)} %bitcast.351), channel_id=1, source_target_pairs={{0,2},{2,0},{4,6},{6,4},{8,10},{10,8},{12,14},{14,12},{16,18},{18,... | collective-permute-start | bytes 7532552 | tf_op jit(solution)/shard_map/ppermute | solution.py:176
  443.4 59.0 %collective-permute-start.5 = (f32[2,2,2,78620]{3,2,1,0:T(2,128)}, f32[2,2,2,78620]{3,2,1,0:T(2,128)}, u32[]{:S(2)}, u32[]{:S(2)}) collective-permute-start(f32[2,2,2,78620]{3,2,1,0:T(2,128)} %fusion.97), channel_id=1, source_target_pairs={{0,8},{2,10},{4,12},{6,14},{8,0},{10,2},{12,4},{14,6},{16,24},{18,... | collective-permute-start | bytes 7547528 | tf_op jit(solution)/shard_map/ppermute | solution.py:176
  501.5 28.1 %collective-permute-start.1 = (f32[2,2,78464]{2,1,0:T(2,128)S(1)}, f32[2,2,78464]{2,1,0:T(2,128)S(1)}, u32[]{:S(2)}, u32[]{:S(2)}) collective-permute-start(f32[2,2,78464]{2,1,0:T(2,128)S(1)} %bitcast.452), channel_id=1, source_target_pairs={{0,4},{2,6},{4,0},{6,2},{8,12},{10,14},{12,8},{14,10},{16,20},{18,... | collective-permute-start | bytes 3766280 | tf_op jit(solution)/shard_map/ppermute | solution.py:176
  508.7 27.5 %collective-permute-start.6 = (f32[2,2,78620]{2,1,0:T(2,128)S(1)}, f32[2,2,78620]{2,1,0:T(2,128)S(1)}, u32[]{:S(2)}, u32[]{:S(2)}) collective-permute-start(f32[2,2,78620]{2,1,0:T(2,128)S(1)} %bitcast.451), channel_id=1, source_target_pairs={{0,2},{2,0},{4,6},{6,4},{8,10},{10,8},{12,14},{14,12},{16,18},{18,... | collective-permute-start | bytes 3773768 | tf_op jit(solution)/shard_map/ppermute | solution.py:176
  531.9 14.2 %collective-permute-start.2 = (f32[2,78464]{1,0:T(2,128)S(1)}, f32[2,78464]{1,0:T(2,128)S(1)}, u32[]{:S(2)}, u32[]{:S(2)}) collective-permute-start(f32[2,78464]{1,0:T(2,128)S(1)} %bitcast.464), channel_id=1, source_target_pairs={{0,8},{2,10},{4,12},{6,14},{8,0},{10,2},{12,4},{14,6},{16,24},{18,... | collective-permute-start | bytes 1883144 | tf_op jit(solution)/shard_map/ppermute | solution.py:176
  538.8 13.3 %collective-permute-start.7 = (f32[2,78620]{1,0:T(2,128)S(1)}, f32[2,78620]{1,0:T(2,128)S(1)}, u32[]{:S(2)}, u32[]{:S(2)}) collective-permute-start(f32[2,78620]{1,0:T(2,128)S(1)} %bitcast.462), channel_id=1, source_target_pairs={{0,4},{2,6},{4,0},{6,2},{8,12},{10,14},{12,8},{14,10},{16,20},{18,... | collective-permute-start | bytes 1886888 | tf_op jit(solution)/shard_map/ppermute | solution.py:176
  548.2 23.4 %collective-permute-start.3 = (f32[78464]{0:T(1024)S(1)}, f32[78464]{0:T(1024)}, u32[]{:S(2)}, u32[]{:S(2)}) collective-permute-start(f32[78464]{0:T(1024)S(1)} %get-tuple-element.294), channel_id=1, source_target_pairs={{0,16},{2,18},{4,20},{6,22},{8,24},{10,26},{12,28},{14,30},{16,0},... | collective-permute-start | bytes 941576 | tf_op jit(solution)/shard_map/ppermute | solution.py:176
  554.3 23.1 %collective-permute-start.8 = (f32[78620]{0:T(1024)S(1)}, f32[78620]{0:T(1024)}, u32[]{:S(2)}, u32[]{:S(2)}) collective-permute-start(f32[78620]{0:T(1024)S(1)} %get-tuple-element.290), channel_id=1, source_target_pairs={{0,16},{2,18},{4,20},{6,22},{8,24},{10,26},{12,28},{14,30},{16,0},... | collective-permute-start | bytes 943448 | tf_op jit(solution)/shard_map/ppermute | solution.py:176
  (136 other events, 528.1 us)
Sparse Core Ops, SparseCore 0:
  9.6 12.5 all-gather.4
  66.7 10.2 reduce-scatter.8
  79.7 9.0 reduce-scatter.12
  90.8 10.8 all-gather.6
  104.4 8.9 reduce-scatter.14
  115.5 10.1 reduce-scatter.10
  135.1 11.0 all-gather.8
  148.5 8.9 reduce-scatter.18
  224.4 9.0 reduce-scatter.16
  269.8 9.9 all-gather.10
  395.7 8.4 reduce-scatter.22
  448.3 9.3 reduce-scatter.20

commit v2 on v1

--- a/solution.py
+++ b/solution.py
@@ -187,14 +187,14 @@
     return orders
 
 
-def halve(chunk, order, me, size, bits):
+def halve(chunk, order, me, size, bits, wire):
     axes = list(range(bits - 1, -1, -1))
     for bit in order:
         where = axes.index(bit)
         mine = (me >> bit) & 1
         keep = lax.dynamic_index_in_dim(chunk, mine, axis=where, keepdims=False)
         send = lax.dynamic_index_in_dim(chunk, 1 - mine, axis=where, keepdims=False)
-        chunk = keep + xor_exchange(send, 1 << bit, size)
+        chunk = keep + xor_exchange(send.astype(wire), 1 << bit, size).astype(chunk.dtype)
         axes.pop(where)
     return chunk
 
@@ -211,42 +211,26 @@
     return block.reshape(-1)
 
 
-def dp_reduce(scattered, replicated, size, colours=3):
+def dp_reduce(scattered, colours_of, replicated, size, wire):
     bits = size.bit_length() - 1
     me = lax.axis_index("dp")
-    rows = [piece.reshape(size, -1) for piece in scattered]
-    widths = [row.shape[1] for row in rows]
+    orders = bit_orders(bits, 3)
+    scattered_out = []
+    for piece, colour in zip(scattered, colours_of):
+        shaped = piece.reshape((2,) * bits + (piece.shape[0] // size,) + piece.shape[1:])
+        scattered_out.append(halve(shaped, orders[colour], me, size, bits, wire))
     flat = jnp.concatenate([piece.reshape(-1) for piece in replicated])
     pad = (-flat.shape[0]) % size
     flat = jnp.pad(flat, (0, pad))
-    rep_width = flat.shape[0] // size
-    joined = jnp.concatenate(rows + [flat.reshape(size, rep_width)], axis=1)
-    total = joined.shape[1]
-    bounds = [total * colour // colours for colour in range(colours + 1)]
-    bounds = [bound // 128 * 128 for bound in bounds[:-1]] + [total]
-    orders = bit_orders(bits, colours)
-    shaped = joined.reshape((2,) * bits + (total,))
-    reduced = jnp.concatenate(
-        [
-            halve(shaped[..., bounds[c] : bounds[c + 1]], orders[c], me, size, bits)
-            for c in range(colours)
-        ]
-    )
-    scattered_out = []
-    offset = 0
-    for piece, width in zip(scattered, widths):
-        share = reduced[offset : offset + width]
-        scattered_out.append(share.reshape((piece.shape[0] // size,) + piece.shape[1:]))
-        offset += width
-    rep_block = reduced[offset : offset + rep_width]
-    full = double(rep_block, orders[0], me, size, bits)[: flat.shape[0] - pad]
+    shaped = flat.reshape((2,) * bits + (flat.shape[0] // size,))
+    block = halve(shaped, orders[0], me, size, bits, wire)
+    full = double(block, orders[0], me, size, bits)[: flat.shape[0] - pad]
     replicated_out = []
     offset = 0
     for piece in replicated:
         replicated_out.append(full[offset : offset + piece.size].reshape(piece.shape))
         offset += piece.size
     return scattered_out, replicated_out
-
 
 def body(
     text_input,
@@ -476,7 +460,10 @@
         layout_wdown_grad,
         small,
     )
-    scattered_out, replicated_out = dp_reduce(scattered, replicated, n_dp)
+    scattered, replicated = lax.optimization_barrier((scattered, replicated))
+    scattered_out, replicated_out = dp_reduce(
+        scattered, (2, 2, 0, 1), replicated, n_dp, jnp.bfloat16
+    )
     qkv_share = jnp.transpose(scattered_out[0], (1, 0, 2))
     wout_share = scattered_out[1].T
     wup_share = scattered_out[2]

time: 640 us -> 461 us (0.72)
  waiting for transfers between devices: 183 us -> 72 us
  local copies, waits for them, and re-layouts: 178 us -> 142 us
  other arithmetic: 112 us -> 77.2 us
  starting transfers between devices: 24.8 us -> 31.9 us
    ppermute x16 -> x24, waiting for transfers between devices: 166 us -> 50.7 us  [xor_exchange(): return lax.ppermute(values, 'dp', [(i, i ^ step) for i in range(size)])]
    concatenate x5 -> x0, local copies, waits for them, and re-layouts: 27.6 us -> none  [dp_reduce(): joined = jnp.concatenate(rows + [flat.reshape(size, rep_width)], axis=1)]
    dynamic_slice x6 -> x4, local copies, waits for them, and re-layouts: 18.6 us -> 2.84 us  [halve(): keep = lax.dynamic_index_in_dim(chunk, mine, axis=where, keepdims=False)]
    convert_element_type x0 -> x20, local copies, waits for them, and re-layouts: none -> 15.8 us  [halve(): send.astype(wire)]
    concatenate x1, local copies, waits for them, and re-layouts: 6.67 us -> 16.4 us  [dp_reduce(): flat = jnp.concatenate([piece.reshape(-1) for piece in replicated])]
    concatenate x2 -> x0, other arithmetic: 9.37 us -> none  [the longest x1 9.32 us: dp_reduce(): joined = jnp.concatenate(rows + [flat.reshape(size, rep_width)], axis=1)]
    add x12 -> x17, other arithmetic: 21 us -> 12.2 us  [halve(): keep + xor_exchange(send.astype(wire), 1 << bit, size).astype(chunk.dtype)]
    squeeze x2 -> x0, other arithmetic: 8.39 us -> none  [halve(): send = lax.dynamic_index_in_dim(chunk, 1 - mine, axis=where, keepdims=False)]
  transfers between devices with their start and end apart: 29 -> 37, of which waited for: 19 -> 20; matrix products, arithmetic and copies ran while one was open for 37% -> 42% of each run, Pallas kernels for 0% -> 0%
where the time goes in v2:
time: 461 us; the launch traced here: 454 us
  local copies, waits for them, and re-layouts  142 us (31%)
  matrix products  105 us (23%)
  other arithmetic  77.2 us (17%)
  waiting for transfers between devices  72 us (16%)
  starting transfers between devices  31.9 us (7%)
  between operations  16.4 us (4%)
  blocking collectives  8.64 us (2%)
    ppermute x24, waiting for transfers between devices, xor_exchange(): return lax.ppermute(values, 'dp', [(i, i ^ step) for i in range(size)])  50.7 us
    ppermute x24, starting transfers between devices, xor_exchange(): return lax.ppermute(values, 'dp', [(i, i ^ step) for i in range(size)])  30.3 us
    unnamed x253, local copies, waits for them, and re-layouts  23.6 us
    concatenate x1, local copies, waits for them, and re-layouts, dp_reduce(): flat = jnp.concatenate([piece.reshape(-1) for piece in replicated])  16.4 us
    convert_element_type x20, local copies, waits for them, and re-layouts, halve(): send.astype(wire)  15.8 us
    reduce_sum x8, other arithmetic, layer_norm(): centered = values - jnp.mean(values, axis=-1, keepdims=True)  12.6 us
    add x17, other arithmetic, halve(): keep + xor_exchange(send.astype(wire), 1 << bit, size).astype(chunk.dtype)  12.2 us
    dot_general x2, matrix products, feed_back(): jnp.einsum('rd,fd->rf', full_grad, w_down, preferred_element_type=jnp.flo...  9.76 us
  transfers between devices with their start and end apart: 37, of which 20 were waited for; matrix products, arithmetic and copies ran while one was open for 42% of the time, Pallas kernels for 0%

profile of v2, /device:TPU:0, one launch (start us, length us, event | category | flops | bytes accessed | tf_op | source)
XLA Modules:
  0.0 454.4 jit_solution(2452676180156780847)
XLA Ops:
  22.1 4.0 convolution_bitcast_fusion
  28.2 3.6 squeeze.188
  34.4 3.4 squeeze.187
  37.8 3.6 fusion.101
  43.1 18.1 %while.34 = (s32[]{:T(128)}, bf16[2,512,6,64]{1,3,2,0:T(8,128)(2,1)}, bf16[2,512,6,16]{1,3,2,0:T(8,128)(2,1)}, f32[2,6,512,1]{2,1,3,0:T(8,128)}, bf16[2,512,6,64...) while((s32[]{:T(128)}, ...), condition=%wide.region_3.4_spmd, body=%wide.region_0.3_spmd.sunk | while | flops 519287808 | bytes 54970212 | solution.py:281
  83.1 5.7 %reduce-scatter.13.cloned.1.call-done = bf16[512,192]{0,1:T(8,128)(2,1)} async-done(((bf16[1024,192]{0,1:T(8,128)(2,1)}), bf16[512,192]{0,1:T(8,128)(2,1)}) %reduce-scatter.13.cloned.1.call-update) | async-done | bytes 196624 | tf_op jit(solution)/shard_map/reduce_scatter | solution.py:290
  101.7 7.1 %multiply_convert_fusion.1 = (bf16[1024,1536]{1,0:T(8,128)(2,1)S(1)}, f32[1024,1536]{1,0:T(8,128)}) fusion(f32[1536]{0:T(1024)} %convert_element_type.451, bf16[1024,768]{1,0:T(8,128)(2,1)} %all-gather.7.cloned.1.call-done, bf16[768,1536]{1,0:T(8,128)(2,1)S(1)} %copy-done), kind=kOutput, calls=%fused_computation.103 | convolution fusion | flops 2425356288 | bytes 13375488 | tf_op jit(solution)/shard_map/dot_general | solution.py:123
  110.5 3.7 convolution_convert_fusion.4
  118.9 6.8 %reduce-scatter.11.cloned.1.call-done = bf16[512,768]{1,0:T(8,128)(2,1)} async-done(((bf16[1024,768]{1,0:T(8,128)(2,1)}), bf16[512,768]{1,0:T(8,128)(2,1)}) %reduce-scatter.11.cloned.1.call-update) | async-done | bytes 786448 | tf_op jit(solution)/shard_map/reduce_scatter | solution.py:321
  146.1 8.2 %convert_reduce_fusion = (f32[1536]{0:T(1024)}, bf16[1024,1536]{1,0:T(8,128)(2,1)S(1)}) fusion(f32[1024,1536]{1,0:T(8,128)} %get-tuple-element.486, f32[1536]{0:T(1024)} %convert_element_type.451, bf16[1024,768]{1,0:T(8,128)(2,1)} %all-gather.9.cloned.1.call-done, bf16[1536,768]{1,0:T(8,128)(2,1)} %param.38), kind=kOutput, calls=%fused_computation.101 | convolution fusion | flops 2441083392 | bytes 13381632 | tf_op jit(solution)/shard_map/rd,fd->rf/dot_general | solution.py:131
  156.1 3.8 convolution_convert_fusion.3
  174.9 7.3 %fusion.173 = f32[768,1536]{1,0:T(8,128)} fusion(bf16[1024,768]{1,0:T(8,128)(2,1)} %all-gather.9.cloned.1.call-done, bf16[1024,1536]{1,0:T(8,128)(2,1)} %copy-done.48), kind=kOutput, calls=%fused_computation.365 | convolution fusion | flops 2415919104 | bytes 9437184 | tf_op jit(solution)/shard_map/rf,rd->df/dot_general | solution.py:130
  182.2 3.4 multiply_reduce_fusion.1
  190.4 6.2 %fusion.172 = f32[768,1536]{1,0:T(8,128)} fusion(bf16[1024,768]{1,0:T(8,128)(2,1)S(1)} %copy-done.64, bf16[1024,1536]{1,0:T(8,128)(2,1)} %copy-done.49), kind=kOutput, calls=%fused_computation.364 | convolution fusion | flops 2415919104 | bytes 9437184 | tf_op jit(solution)/shard_map/rd,rf->df/dot_general | solution.py:133
  197.3 3.5 all-gather.11.cloned.1.call-done
  209.2 32.9 %while.35 = (s32[]{:T(128)}, bf16[2,512,6,64]{1,3,2,0:T(8,128)(2,1)}, bf16[2,512,6,64]{1,3,2,0:T(8,128)(2,1)}, bf16[2,512,6,64]{1,3,2,0:T(8,128)(2,1)}, bf16[2,5...) while((s32[]{:T(128)}, ...), condition=%wide.region_28.29_spmd, body=%wide.region_26.28_spmd.sunk | while | flops 1279964160 | bytes 114307136 | solution.py:392
  268.0 5.3 %copy.151 = f32[768,3,384]{2,0,1:T(8,128)} copy(f32[768,3,384]{0,2,1:T(8,128)} %pad_maximum_fusion) | data formatting | bytes 7077888 | tf_op jit(solution)/shard_map/optimization_barrier | solution.py:463
  284.1 16.4 %concatenate.85 = f32[229824]{0:T(1024)} concatenate(f32[768]{0:T(1024)S(1)} %reshape.718, f32[1536]{0:T(1024)S(1)} %copy-done.121, f32[55296]{0:T(1024)} %reshape.719, f32[192]{0:T(256)S(1)} %reshape.720, f32[18432]{0:T(1024)} %reshape.721, f32[73728]{0:T(1024)} %reshape.722, f32[384]{0:T(512)} %get-tuple-element.202, f32[73728]{0:T(1024)} %reshape.723, f32[5760]{0:T(1024)} %add.503), dimensions={0} | concatenate | bytes 1838592 | tf_op jit(solution)/shard_map/concatenate | solution.py:222
  300.5 3.0 reshape.724
  313.0 3.0 fusion.107
  327.6 21.4 %collective-permute-done.6 = bf16[2,2,14364]{2,1,0:T(2,128)(2,1)S(1)} collective-permute-done((bf16[2,2,14364]{2,1,0:T(2,128)(2,1)S(1)}, bf16[2,2,14364]{2,1,0:T(2,128)(2,1)S(1)}, u32[]{:S(2)}, u32[]{:S(2)}) %collective-permute-start.6) | collective-permute-done | bytes 114944 | tf_op jit(solution)/shard_map/ppermute | solution.py:176
  403.6 4.6 %collective-permute-done.3 = bf16[2,48,3,384]{3,1,0,2:T(8,128)(2,1)S(1)} collective-permute-done((bf16[2,48,3,384]{3,1,0,2:T(8,128)(2,1)S(1)}, bf16[2,48,3,384]{3,1,0,2:T(8,128)(2,1)S(1)}, u32[]{:S(2)}, u32[]{:S(2)}) %collective-permute-start.3) | collective-permute-done | bytes 221216 | tf_op jit(solution)/shard_map/ppermute | solution.py:176
  428.5 4.6 %collective-permute-done.23 = bf16[2,48,1536]{2,1,0:T(8,128)(2,1)S(1)} collective-permute-done((bf16[2,48,1536]{2,1,0:T(8,128)(2,1)S(1)}, bf16[2,48,1536]{2,1,0:T(8,128)(2,1)S(1)}, u32[]{:S(2)}, u32[]{:S(2)}) %collective-permute-start.23) | collective-permute-done | bytes 294944 | tf_op jit(solution)/shard_map/ppermute | solution.py:176
  436.9 5.3 %collective-permute-done.24 = bf16[48,1536]{1,0:T(8,128)(2,1)S(1)} collective-permute-done((bf16[48,1536]{1,0:T(8,128)(2,1)S(1)}, bf16[48,1536]{1,0:T(8,128)(2,1)S(1)}, u32[]{:S(2)}, u32[]{:S(2)}) %collective-permute-start.24) | collective-permute-done | bytes 147488 | tf_op jit(solution)/shard_map/ppermute | solution.py:176
  (696 shorter events, 303.6 us)
Async XLA Ops:
  7.2 14.9 %all-gather.5.cloned.1.call-start = ((), (), s32[]{:S(2)}) async-start(), calls=%async_computation.8 | async-start | bytes 2359296 | tf_op jit(solution)/shard_map/all_gather | solution.py:265
  7.9 70.2 %reduce-scatter.9.cloned.1.call-start = ((), (), s32[]{:S(2)}) async-start(), calls=%async_computation.9 | async-start | bytes 2359296 | tf_op jit(solution)/shard_map/reduce_scatter | solution.py:287
  66.4 22.3 %reduce-scatter.13.cloned.1.call-start = ((), (), s32[]{:S(2)}) async-start(), calls=%async_computation.12 | async-start | bytes 589824 | tf_op jit(solution)/shard_map/reduce_scatter | solution.py:290
  78.1 23.6 %all-gather.7.cloned.1.call-start = ((), (), s32[]{:S(2)}) async-start(), calls=%async_computation.10 | async-start | bytes 2359296 | tf_op jit(solution)/shard_map/all_gather | solution.py:311
  83.0 31.4 %reduce-scatter.15.cloned.1.call-start = ((), (), s32[]{:S(2)}) async-start(), calls=%async_computation.13 | async-start | bytes 589824 | tf_op jit(solution)/shard_map/reduce_scatter | solution.py:324
  99.8 25.8 %reduce-scatter.11.cloned.1.call-start = ((), (), s32[]{:S(2)}) async-start(), calls=%async_computation.11 | async-start | bytes 2359296 | tf_op jit(solution)/shard_map/reduce_scatter | solution.py:321
  114.3 31.9 %all-gather.9.cloned.1.call-start = ((), (), s32[]{:S(2)}) async-start(), calls=%async_computation.14 | async-start | bytes 2359296 | tf_op jit(solution)/shard_map/all_gather | solution.py:346
  134.9 29.4 %reduce-scatter.19.cloned.1.call-start = ((), (), s32[]{:S(2)}) async-start(), calls=%async_computation.17 | async-start | bytes 589824 | tf_op jit(solution)/shard_map/reduce_scatter | solution.py:359
  145.1 37.1 %reduce-scatter.17.cloned.1.call-start = ((), (), s32[]{:S(2)}) async-start(), calls=%async_computation.15 | async-start | bytes 2359296 | tf_op jit(solution)/shard_map/reduce_scatter | solution.py:356
  159.9 40.9 %all-gather.11.cloned.1.call-start = ((), (), s32[]{:S(2)}) async-start(), calls=%async_computation.16 | async-start | bytes 2359296 | tf_op jit(solution)/shard_map/all_gather | solution.py:372
  189.6 185.6 %reduce-scatter.23.cloned.1.call-start = ((), (), s32[]{:S(2)}) async-start(), calls=%async_computation.19 | async-start | bytes 589824 | tf_op jit(solution)/shard_map/reduce_scatter | solution.py:414
  257.4 187.1 %reduce-scatter.21.cloned.1.call-start = ((), (), s32[]{:S(2)}) async-start(), calls=%async_computation.18 | async-start | bytes 2359296 | tf_op jit(solution)/shard_map/reduce_scatter | solution.py:411
  280.3 46.2 %collective-permute-start.13 = (bf16[2,2,2,48,384]{4,3,0,1,2:T(8,128)(2,1)}, bf16[2,2,2,48,384]{4,3,0,1,2:T(8,128)(2,1)}, u32[]{:S(2)}, u32[]{:S(2)}) collective-permute-start(bf16[2,2,2,48,384]{4,3,0,1,2:T(8,128)(2,1)} %fusion.134), channel_id=1, source_target_pairs={{0,8},{2,10},{4,12},{6,14},{8,0},{10,2},{12,4},{14,6},{16,24},{18,... | collective-permute-start | bytes 884744 | tf_op jit(solution)/shard_map/ppermute | solution.py:176
  308.4 15.9 %collective-permute-start.5 = (bf16[2,2,2,14364]{3,2,1,0:T(2,128)(2,1)}, bf16[2,2,2,14364]{3,2,1,0:T(2,128)(2,1)S(1)}, u32[]{:S(2)}, u32[]{:S(2)}) collective-permute-start(bf16[2,2,2,14364]{3,2,1,0:T(2,128)(2,1)} %bitcast.401), channel_id=1, source_target_pairs={{0,2},{2,0},{4,6},{6,4},{8,10},{10,8},{12,14},{14,12},{16,18},{18,... | collective-permute-start | bytes 689480 | tf_op jit(solution)/shard_map/ppermute | solution.py:176
  312.5 69.1 %collective-permute-start.1 = (bf16[2,2,2,48,3,384]{5,3,2,1,0,4:T(8,128)(2,1)}, bf16[2,2,2,48,3,384]{5,3,2,1,0,4:T(8,128)(2,1)}, u32[]{:S(2)}, u32[]{:S(2)}) collective-permute-start(bf16[2,2,2,48,3,384]{5,3,2,1,0,4:T(8,128)(2,1)} %fusion.110), channel_id=1, source_target_pairs={{0,8},{2,10},{4,12},{6,14},{8,0},{10,2},{12,4},{14,6},{16,24},{18,... | collective-permute-start | bytes 2654216 | tf_op jit(solution)/shard_map/ppermute | solution.py:176
  318.9 66.6 %collective-permute-start.21 = (bf16[2,2,2,48,1536]{4,3,0,2,1:T(8,128)(2,1)}, bf16[2,2,2,48,1536]{4,3,0,2,1:T(8,128)(2,1)}, u32[]{:S(2)}, u32[]{:S(2)}) collective-permute-start(bf16[2,2,2,48,1536]{4,3,0,2,1:T(8,128)(2,1)} %fusion.108), channel_id=1, source_target_pairs={{0,4},{2,6},{4,0},{6,2},{8,12},{10,14},{12,8},{14,10},{16,20},{18,... | collective-permute-start | bytes 3538952 | tf_op jit(solution)/shard_map/ppermute | solution.py:176
  320.4 70.9 %collective-permute-start.17 = (bf16[2,2,2,48,1536]{4,3,0,1,2:T(8,128)(2,1)}, bf16[2,2,2,48,1536]{4,3,0,1,2:T(8,128)(2,1)}, u32[]{:S(2)}, u32[]{:S(2)}) collective-permute-start(bf16[2,2,2,48,1536]{4,3,0,1,2:T(8,128)(2,1)} %fusion.107), channel_id=1, source_target_pairs={{0,2},{2,0},{4,6},{6,4},{8,10},{10,8},{12,14},{14,12},{16,18},{18,... | collective-permute-start | bytes 3538952 | tf_op jit(solution)/shard_map/ppermute | solution.py:176
  326.2 22.7 %collective-permute-start.6 = (bf16[2,2,14364]{2,1,0:T(2,128)(2,1)S(1)}, bf16[2,2,14364]{2,1,0:T(2,128)(2,1)S(1)}, u32[]{:S(2)}, u32[]{:S(2)}) collective-permute-start(bf16[2,2,14364]{2,1,0:T(2,128)(2,1)S(1)} %bitcast.515), channel_id=1, source_target_pairs={{0,4},{2,6},{4,0},{6,2},{8,12},{10,14},{12,8},{14,10},{16,20},{18,... | collective-permute-start | bytes 344744 | tf_op jit(solution)/shard_map/ppermute | solution.py:176
  379.9 15.4 %collective-permute-start.12 = (f32[2,2,2,14364]{3,0,1,2:T(2,128)S(1)}, f32[2,2,2,14364]{3,0,1,2:T(2,128)S(1)}, u32[]{:S(2)}, u32[]{:S(2)}) collective-permute-start(f32[2,2,2,14364]{3,0,1,2:T(2,128)S(1)} %maximum_select_fusion.1), channel_id=1, source_target_pairs={{0,2},{2,0},{4,6},{6,4},{8,10},{10,8},{12,14},{14,12},{16,18},{18,... | collective-permute-start | bytes 1378952 | tf_op jit(solution)/shard_map/ppermute | solution.py:176
  384.0 17.1 %collective-permute-start.2 = (bf16[2,2,48,3,384]{4,2,1,0,3:T(8,128)(2,1)}, bf16[2,2,48,3,384]{4,2,1,0,3:T(8,128)(2,1)}, u32[]{:S(2)}, u32[]{:S(2)}) collective-permute-start(bf16[2,2,48,3,384]{4,2,1,0,3:T(8,128)(2,1)} %fusion.123), channel_id=1, source_target_pairs={{0,2},{2,0},{4,6},{6,4},{8,10},{10,8},{12,14},{14,12},{16,18},{18,... | collective-permute-start | bytes 1327112 | tf_op jit(solution)/shard_map/ppermute | solution.py:176
  389.2 35.3 %collective-permute-start.22 = (bf16[2,2,48,1536]{3,2,0,1:T(8,128)(2,1)}, bf16[2,2,48,1536]{3,2,0,1:T(8,128)(2,1)}, u32[]{:S(2)}, u32[]{:S(2)}) collective-permute-start(bf16[2,2,48,1536]{3,2,0,1:T(8,128)(2,1)} %fusion.112), channel_id=1, source_target_pairs={{0,8},{2,10},{4,12},{6,14},{8,0},{10,2},{12,4},{14,6},{16,24},{18,... | collective-permute-start | bytes 1769480 | tf_op jit(solution)/shard_map/ppermute | solution.py:176
  393.9 33.0 %collective-permute-start.18 = (bf16[2,2,48,1536]{3,2,0,1:T(8,128)(2,1)}, bf16[2,2,48,1536]{3,2,0,1:T(8,128)(2,1)}, u32[]{:S(2)}, u32[]{:S(2)}) collective-permute-start(bf16[2,2,48,1536]{3,2,0,1:T(8,128)(2,1)} %fusion.111), channel_id=1, source_target_pairs={{0,4},{2,6},{4,0},{6,2},{8,12},{10,14},{12,8},{14,10},{16,20},{18,... | collective-permute-start | bytes 1769480 | tf_op jit(solution)/shard_map/ppermute | solution.py:176
  408.4 15.5 %collective-permute-start.4 = (bf16[48,3,384]{2,0,1:T(8,128)(2,1)S(1)}, bf16[48,3,384]{2,0,1:T(8,128)(2,1)S(1)}, u32[]{:S(2)}, u32[]{:S(2)}) collective-permute-start(bf16[48,3,384]{2,0,1:T(8,128)(2,1)S(1)} %fusion.141), channel_id=1, source_target_pairs={{0,16},{2,18},{4,20},{6,22},{8,24},{10,26},{12,28},{14,30},{16,0},... | collective-permute-start | bytes 331784 | tf_op jit(solution)/shard_map/ppermute | solution.py:176
  433.2 9.0 %collective-permute-start.24 = (bf16[48,1536]{1,0:T(8,128)(2,1)S(1)}, bf16[48,1536]{1,0:T(8,128)(2,1)S(1)}, u32[]{:S(2)}, u32[]{:S(2)}) collective-permute-start(bf16[48,1536]{1,0:T(8,128)(2,1)S(1)} %fusion.140), channel_id=1, source_target_pairs={{0,16},{2,18},{4,20},{6,22},{8,24},{10,26},{12,28},{14,30},{16,0},... | collective-permute-start | bytes 442376 | tf_op jit(solution)/shard_map/ppermute | solution.py:176
  (173 other events, 610.3 us)
Sparse Core Ops, SparseCore 0:
  9.6 12.5 all-gather.4
  66.6 10.2 reduce-scatter.8
  79.6 9.0 reduce-scatter.12
  90.7 10.9 all-gather.6
  104.3 8.9 reduce-scatter.14
  115.5 10.1 reduce-scatter.10
  135.0 11.0 all-gather.8
  148.4 8.9 reduce-scatter.18
  160.0 10.2 reduce-scatter.16
  189.7 10.9 all-gather.10
  257.6 8.9 reduce-scatter.22
  324.4 9.0 reduce-scatter.20

commit v3 on v2

--- a/solution.py
+++ b/solution.py
@@ -187,15 +187,12 @@
     return orders
 
 
-def halve(chunk, order, me, size, bits, wire):
-    axes = list(range(bits - 1, -1, -1))
+def halve(chunk, order, me, size, wire):
     for bit in order:
-        where = axes.index(bit)
         mine = (me >> bit) & 1
-        keep = lax.dynamic_index_in_dim(chunk, mine, axis=where, keepdims=False)
-        send = lax.dynamic_index_in_dim(chunk, 1 - mine, axis=where, keepdims=False)
+        keep = lax.dynamic_index_in_dim(chunk, mine, axis=0, keepdims=False)
+        send = lax.dynamic_index_in_dim(chunk, 1 - mine, axis=0, keepdims=False)
         chunk = keep + xor_exchange(send.astype(wire), 1 << bit, size).astype(chunk.dtype)
-        axes.pop(where)
     return chunk
 
 
@@ -207,29 +204,45 @@
         block = jnp.where(mine == 0, jnp.stack([block, other]), jnp.stack([other, block]))
         held.insert(0, bit)
     canonical = list(range(bits - 1, -1, -1))
-    block = jnp.transpose(block, [held.index(bit) for bit in canonical] + [len(held)])
-    return block.reshape(-1)
-
-
-def dp_reduce(scattered, colours_of, replicated, size, wire):
+    rest = list(range(len(held), block.ndim))
+    block = jnp.transpose(block, [held.index(bit) for bit in canonical] + rest)
+    return block.reshape((-1,) + block.shape[len(held) + 1 :])
+
+
+def ordered(piece, order, size, bits):
+    shaped = piece.reshape((2,) * bits + (piece.shape[0] // size,) + piece.shape[1:])
+    canonical = list(range(bits - 1, -1, -1))
+    rest = list(range(bits, shaped.ndim))
+    return jnp.transpose(shaped, [canonical.index(bit) for bit in order] + rest)
+
+
+def dp_reduce(scattered, colours_of, replicated, size, wire, lanes=128):
     bits = size.bit_length() - 1
     me = lax.axis_index("dp")
     orders = bit_orders(bits, 3)
     scattered_out = []
     for piece, colour in zip(scattered, colours_of):
-        shaped = piece.reshape((2,) * bits + (piece.shape[0] // size,) + piece.shape[1:])
-        scattered_out.append(halve(shaped, orders[colour], me, size, bits, wire))
-    flat = jnp.concatenate([piece.reshape(-1) for piece in replicated])
-    pad = (-flat.shape[0]) % size
-    flat = jnp.pad(flat, (0, pad))
-    shaped = flat.reshape((2,) * bits + (flat.shape[0] // size,))
-    block = halve(shaped, orders[0], me, size, bits, wire)
-    full = double(block, orders[0], me, size, bits)[: flat.shape[0] - pad]
+        chunk = ordered(piece, orders[colour], size, bits)
+        scattered_out.append(halve(chunk, orders[colour], me, size, wire))
+    blocks = []
+    for piece in replicated:
+        flat = piece.reshape(-1)
+        flat = jnp.pad(flat, (0, (-flat.shape[0]) % lanes))
+        blocks.append(flat.reshape(-1, lanes))
+    joined = jnp.concatenate(blocks)
+    rows = joined.shape[0]
+    joined = jnp.pad(joined, ((0, (-rows) % (size * 8)), (0, 0)))
+    chunk = ordered(joined, orders[0], size, bits)
+    block = halve(chunk, orders[0], me, size, wire)
+    full = double(block, orders[0], me, size, bits)
     replicated_out = []
     offset = 0
     for piece in replicated:
-        replicated_out.append(full[offset : offset + piece.size].reshape(piece.shape))
-        offset += piece.size
+        count = -(-piece.size // lanes)
+        replicated_out.append(
+            full[offset : offset + count].reshape(-1)[: piece.size].reshape(piece.shape)
+        )
+        offset += count
     return scattered_out, replicated_out
 
 def body(
@@ -444,8 +457,7 @@
     )
     small = xor_sum(small, "mp", n_mp)
     scattered = (
-        text_qkv_grad_t,
-        text_wout_grad_t,
+        jnp.concatenate([text_qkv_grad_t, text_wout_grad_t[:, None, :]], axis=1),
         text_wup_grad,
         text_wdown_grad_t,
     )
@@ -462,12 +474,12 @@
     )
     scattered, replicated = lax.optimization_barrier((scattered, replicated))
     scattered_out, replicated_out = dp_reduce(
-        scattered, (2, 2, 0, 1), replicated, n_dp, jnp.bfloat16
-    )
-    qkv_share = jnp.transpose(scattered_out[0], (1, 0, 2))
-    wout_share = scattered_out[1].T
-    wup_share = scattered_out[2]
-    wdown_share = scattered_out[3].T
+        scattered, (2, 0, 1), replicated, n_dp, jnp.bfloat16
+    )
+    qkv_share = jnp.transpose(scattered_out[0][:, :3], (1, 0, 2))
+    wout_share = scattered_out[0][:, 3].T
+    wup_share = scattered_out[1]
+    wdown_share = scattered_out[2].T
     summed = replicated_out[:8]
     small_sum = replicated_out[8]
     sizes = (2 * D, 2 * D, 2 * D, 2 * DL, 2 * DL, 2 * DL)

time: 461 us -> 411 us (0.89)
  local copies, waits for them, and re-layouts: 142 us -> 108 us
  waiting for transfers between devices: 72 us -> 61.6 us
  other arithmetic: 77.2 us -> 71.9 us
  matrix products: 105 us -> 110 us
    concatenate x1, local copies, waits for them, and re-layouts: 16.4 us -> 2.8 us  [dp_reduce(): joined = jnp.concatenate(blocks)]
    reshape x11 -> x9, local copies, waits for them, and re-layouts: 13.3 us -> 2.69 us  [the longest x6 1.96 us: dp_reduce(): blocks.append(flat.reshape(-1, lanes))]
    ppermute x24 -> x20, waiting for transfers between devices: 50.7 us -> 40.2 us  [xor_exchange(): return lax.ppermute(values, 'dp', [(i, i ^ step) for i in range(size)])]
    slice x10 -> x4, local copies, waits for them, and re-layouts: 8.29 us -> 1.56 us  [dp_reduce(): full[offset:offset + count].reshape(-1)[:piece.size].reshape(piece.shape)]
    convert_element_type x20 -> x16, local copies, waits for them, and re-layouts: 15.8 us -> 10.6 us  [halve(): send.astype(wire)]
    another operation x15 -> x13, local copies, waits for them, and re-layouts: 7.36 us -> 11.7 us
    ppermute x24 -> x20, starting transfers between devices: 30.3 us -> 27.1 us  [xor_exchange(): return lax.ppermute(values, 'dp', [(i, i ^ step) for i in range(size)])]
    unnamed x253 -> x236, local copies, waits for them, and re-layouts: 23.6 us -> 21.1 us
  transfers between devices with their start and end apart: 37 -> 33, of which waited for: 20 -> 14; matrix products, arithmetic and copies ran while one was open for 42% -> 39% of each run, Pallas kernels for 0% -> 0%
where the time goes in v3:
time: 411 us; the launch traced here: 406 us
  matrix products  110 us (27%)
  local copies, waits for them, and re-layouts  108 us (26%)
  other arithmetic  71.9 us (17%)
  waiting for transfers between devices  61.6 us (15%)
  starting transfers between devices  28.7 us (7%)
  between operations  16.3 us (4%)
  blocking collectives  8.64 us (2%)
    ppermute x20, waiting for transfers between devices, xor_exchange(): return lax.ppermute(values, 'dp', [(i, i ^ step) for i in range(size)])  40.2 us
    ppermute x20, starting transfers between devices, xor_exchange(): return lax.ppermute(values, 'dp', [(i, i ^ step) for i in range(size)])  27.1 us
    unnamed x236, local copies, waits for them, and re-layouts  21.1 us
    reduce_sum x8, other arithmetic, layer_norm(): centered = values - jnp.mean(values, axis=-1, keepdims=True)  12.6 us
    add x15, other arithmetic, halve(): keep + xor_exchange(send.astype(wire), 1 << bit, size).astype(chunk.dtype)  11.6 us
    convert_element_type x16, local copies, waits for them, and re-layouts, halve(): send.astype(wire)  10.6 us
    dot_general x2, matrix products, feed_back(): jnp.einsum('rd,fd->rf', full_grad, w_down, preferred_element_type=jnp.flo...  9.7 us
    dot_general x2, matrix products, feed_forward(): jnp.dot(full_rows, w_up, preferred_element_type=jnp.float32) + up_bias  9.5 us
  transfers between devices with their start and end apart: 33, of which 14 were waited for; matrix products, arithmetic and copies ran while one was open for 39% of the time, Pallas kernels for 0%

profile of v3, /device:TPU:0, one launch (start us, length us, event | category | flops | bytes accessed | tf_op | source)
XLA Modules:
  0.0 405.6 jit_solution(17291277014387920740)
XLA Ops:
  22.1 4.0 convolution_bitcast_fusion
  28.2 3.6 squeeze.169
  34.4 3.4 squeeze.168
  37.9 3.6 fusion.103
  43.1 18.1 %while.34 = (s32[]{:T(128)}, bf16[2,512,6,64]{1,3,2,0:T(8,128)(2,1)}, bf16[2,512,6,16]{1,3,2,0:T(8,128)(2,1)}, f32[2,6,512,1]{2,1,3,0:T(8,128)}, bf16[2,512,6,64...) while((s32[]{:T(128)}, ...), condition=%wide.region_3.4_spmd, body=%wide.region_0.3_spmd.sunk | while | flops 519287808 | bytes 54970212 | solution.py:294
  83.1 5.6 %reduce-scatter.13.cloned.1.call-done = bf16[512,192]{0,1:T(8,128)(2,1)} async-done(((bf16[1024,192]{0,1:T(8,128)(2,1)}), bf16[512,192]{0,1:T(8,128)(2,1)}) %reduce-scatter.13.cloned.1.call-update) | async-done | bytes 196624 | tf_op jit(solution)/shard_map/reduce_scatter | solution.py:303
  101.7 7.1 %multiply_convert_fusion.1 = (bf16[1024,1536]{1,0:T(8,128)(2,1)S(1)}, f32[1024,1536]{1,0:T(8,128)}) fusion(f32[1536]{0:T(1024)} %convert_element_type.431, bf16[1024,768]{1,0:T(8,128)(2,1)} %all-gather.7.cloned.1.call-done, bf16[768,1536]{1,0:T(8,128)(2,1)S(1)} %copy-done), kind=kOutput, calls=%fused_computation.103 | convolution fusion | flops 2425356288 | bytes 13375488 | tf_op jit(solution)/shard_map/dot_general | solution.py:123
  110.4 3.7 convolution_convert_fusion.4
  118.7 6.9 %reduce-scatter.11.cloned.1.call-done = bf16[512,768]{1,0:T(8,128)(2,1)} async-done(((bf16[1024,768]{1,0:T(8,128)(2,1)}), bf16[512,768]{1,0:T(8,128)(2,1)}) %reduce-scatter.11.cloned.1.call-update) | async-done | bytes 786448 | tf_op jit(solution)/shard_map/reduce_scatter | solution.py:334
  146.1 8.2 %convert_reduce_fusion = (f32[1536]{0:T(1024)}, bf16[1024,1536]{1,0:T(8,128)(2,1)S(1)}) fusion(f32[1024,1536]{1,0:T(8,128)} %get-tuple-element.411, f32[1536]{0:T(1024)} %convert_element_type.431, bf16[1024,768]{1,0:T(8,128)(2,1)} %all-gather.9.cloned.1.call-done, bf16[1536,768]{1,0:T(8,128)(2,1)} %param.38), kind=kOutput, calls=%fused_computation.101 | convolution fusion | flops 2441083392 | bytes 13381632 | tf_op jit(solution)/shard_map/rd,fd->rf/dot_general | solution.py:131
  156.1 3.8 convolution_convert_fusion.3
  174.9 7.3 %fusion.173 = f32[768,1536]{1,0:T(8,128)} fusion(bf16[1024,768]{1,0:T(8,128)(2,1)} %all-gather.9.cloned.1.call-done, bf16[1024,1536]{1,0:T(8,128)(2,1)} %copy-done.43), kind=kOutput, calls=%fused_computation.349 | convolution fusion | flops 2415919104 | bytes 9437184 | tf_op jit(solution)/shard_map/rf,rd->df/dot_general | solution.py:130
  182.3 3.4 multiply_reduce_fusion.1
  190.5 6.2 %fusion.172 = f32[768,1536]{1,0:T(8,128)} fusion(bf16[1024,768]{1,0:T(8,128)(2,1)S(1)} %copy-done.55, bf16[1024,1536]{1,0:T(8,128)(2,1)} %copy-done.44), kind=kOutput, calls=%fused_computation.348 | convolution fusion | flops 2415919104 | bytes 9437184 | tf_op jit(solution)/shard_map/rd,rf->df/dot_general | solution.py:133
  197.3 3.5 all-gather.11.cloned.1.call-done
  209.2 33.0 %while.35 = (s32[]{:T(128)}, bf16[2,512,6,64]{1,3,2,0:T(8,128)(2,1)}, bf16[2,512,6,64]{1,3,2,0:T(8,128)(2,1)}, bf16[2,512,6,64]{1,3,2,0:T(8,128)(2,1)}, bf16[2,5...) while((s32[]{:T(128)}, ...), condition=%wide.region_28.29_spmd, body=%wide.region_26.28_spmd.sunk | while | flops 1279964160 | bytes 114307136 | solution.py:405
  257.4 3.9 fusion.117
  275.2 3.8 fusion.119
  291.4 6.1 %copy.105 = f32[768,4,384]{2,0,1:T(8,128)} copy(f32[768,4,384]{0,2,1:T(8,128)} %pad_maximum_fusion) | data formatting | bytes 9437184 | tf_op jit(solution)/shard_map/optimization_barrier | solution.py:475
  306.9 5.2 %add_convert_fusion.1 = bf16[1024,768]{1,0:T(8,128)(2,1)} fusion(f32[1024,768]{1,0:T(8,128)} %fusion.119, f32[1024,768]{1,0:T(8,128)} %fusion.117, bf16[1024,384]{0,1:T(8,128)(2,1)S(1)} %bitcast.516, bf16[3,768,384]{2,1,0:T(8,128)(2,1)} %param.32), kind=kOutput, calls=%fused_computation.106 | convolution fusion | flops 606339072 | bytes 9240576 | tf_op jit(solution)/shard_map/re,de->rd/dot_general | solution.py:153
  312.2 19.6 %collective-permute-done.9 = f32[120,128]{1,0:T(8,128)S(1)} collective-permute-done((f32[120,128]{1,0:T(8,128)S(1)}, f32[120,128]{1,0:T(8,128)S(1)}, u32[]{:S(2)}, u32[]{:S(2)}) %collective-permute-start.9) | collective-permute-done | bytes 61472 | tf_op jit(solution)/shard_map/ppermute | solution.py:176
  333.4 3.4 collective-permute-done.10
  339.1 3.9 collective-permute-done.11
  386.0 6.7 %collective-permute-done.4 = bf16[48,4,384]{2,0,1:T(8,128)(2,1)S(1)} collective-permute-done((bf16[48,4,384]{2,0,1:T(8,128)(2,1)S(1)}, bf16[48,4,384]{2,0,1:T(8,128)(2,1)S(1)}, u32[]{:S(2)}, u32[]{:S(2)}) %collective-permute-start.4) | collective-permute-done | bytes 147488 | tf_op jit(solution)/shard_map/ppermute | solution.py:176
  (656 shorter events, 266.0 us)
Async XLA Ops:
  7.2 14.9 %all-gather.5.cloned.1.call-start = ((), (), s32[]{:S(2)}) async-start(), calls=%async_computation.8 | async-start | bytes 2359296 | tf_op jit(solution)/shard_map/all_gather | solution.py:278
  7.9 70.2 %reduce-scatter.9.cloned.1.call-start = ((), (), s32[]{:S(2)}) async-start(), calls=%async_computation.9 | async-start | bytes 2359296 | tf_op jit(solution)/shard_map/reduce_scatter | solution.py:300
  66.4 22.3 %reduce-scatter.13.cloned.1.call-start = ((), (), s32[]{:S(2)}) async-start(), calls=%async_computation.12 | async-start | bytes 589824 | tf_op jit(solution)/shard_map/reduce_scatter | solution.py:303
  78.1 23.6 %all-gather.7.cloned.1.call-start = ((), (), s32[]{:S(2)}) async-start(), calls=%async_computation.10 | async-start | bytes 2359296 | tf_op jit(solution)/shard_map/all_gather | solution.py:324
  83.1 31.2 %reduce-scatter.15.cloned.1.call-start = ((), (), s32[]{:S(2)}) async-start(), calls=%async_computation.13 | async-start | bytes 589824 | tf_op jit(solution)/shard_map/reduce_scatter | solution.py:337
  99.8 25.9 %reduce-scatter.11.cloned.1.call-start = ((), (), s32[]{:S(2)}) async-start(), calls=%async_computation.11 | async-start | bytes 2359296 | tf_op jit(solution)/shard_map/reduce_scatter | solution.py:334
  114.2 32.0 %all-gather.9.cloned.1.call-start = ((), (), s32[]{:S(2)}) async-start(), calls=%async_computation.14 | async-start | bytes 2359296 | tf_op jit(solution)/shard_map/all_gather | solution.py:359
  134.9 29.4 %reduce-scatter.19.cloned.1.call-start = ((), (), s32[]{:S(2)}) async-start(), calls=%async_computation.17 | async-start | bytes 589824 | tf_op jit(solution)/shard_map/reduce_scatter | solution.py:372
  145.1 37.2 %reduce-scatter.17.cloned.1.call-start = ((), (), s32[]{:S(2)}) async-start(), calls=%async_computation.15 | async-start | bytes 2359296 | tf_op jit(solution)/shard_map/reduce_scatter | solution.py:369
  159.9 40.9 %all-gather.11.cloned.1.call-start = ((), (), s32[]{:S(2)}) async-start(), calls=%async_computation.16 | async-start | bytes 2359296 | tf_op jit(solution)/shard_map/all_gather | solution.py:385
  189.6 147.8 %reduce-scatter.23.cloned.1.call-start = ((), (), s32[]{:S(2)}) async-start(), calls=%async_computation.19 | async-start | bytes 589824 | tf_op jit(solution)/shard_map/reduce_scatter | solution.py:427
  257.3 138.3 %reduce-scatter.21.cloned.1.call-start = ((), (), s32[]{:S(2)}) async-start(), calls=%async_computation.18 | async-start | bytes 2359296 | tf_op jit(solution)/shard_map/reduce_scatter | solution.py:424
  286.8 10.7 %collective-permute-start.7 = (bf16[2,120,128]{2,1,0:T(8,128)(2,1)S(1)}, bf16[2,120,128]{2,1,0:T(8,128)(2,1)S(1)}, u32[]{:S(2)}, u32[]{:S(2)}) collective-permute-start(bf16[2,120,128]{2,1,0:T(8,128)(2,1)S(1)} %fusion.143), channel_id=1, source_target_pairs={{0,8},{2,10},{4,12},{6,14},{8,0},{10,2},{12,4},{14,6},{16,24},{18,... | collective-permute-start | bytes 184328 | tf_op jit(solution)/shard_map/ppermute | solution.py:176
  302.8 40.8 %collective-permute-start.17 = (bf16[2,2,2,48,1536]{4,3,2,1,0:T(8,128)(2,1)}, bf16[2,2,2,48,1536]{4,3,2,1,0:T(8,128)(2,1)}, u32[]{:S(2)}, u32[]{:S(2)}) collective-permute-start(bf16[2,2,2,48,1536]{4,3,2,1,0:T(8,128)(2,1)} %fusion.111), channel_id=1, source_target_pairs={{0,4},{2,6},{4,0},{6,2},{8,12},{10,14},{12,8},{14,10},{16,20},{18,... | collective-permute-start | bytes 3538952 | tf_op jit(solution)/shard_map/ppermute | solution.py:176
  304.3 44.4 %collective-permute-start.13 = (bf16[2,2,2,48,1536]{4,3,2,1,0:T(8,128)(2,1)S(1)}, bf16[2,2,2,48,1536]{4,3,2,1,0:T(8,128)(2,1)}, u32[]{:S(2)}, u32[]{:S(2)}) collective-permute-start(bf16[2,2,2,48,1536]{4,3,2,1,0:T(8,128)(2,1)S(1)} %fusion.110), channel_id=1, source_target_pairs={{0,2},{2,0},{4,6},{6,4},{8,10},{10,8},{12,14},{14,12},{16,18},{18,... | collective-permute-start | bytes 3538952 | tf_op jit(solution)/shard_map/ppermute | solution.py:176
  305.8 47.0 %collective-permute-start.1 = (bf16[2,2,2,48,4,384]{5,3,0,1,2,4:T(8,128)(2,1)}, bf16[2,2,2,48,4,384]{5,3,0,1,2,4:T(8,128)(2,1)}, u32[]{:S(2)}, u32[]{:S(2)}) collective-permute-start(bf16[2,2,2,48,4,384]{5,3,0,1,2,4:T(8,128)(2,1)} %fusion.109), channel_id=1, source_target_pairs={{0,8},{2,10},{4,12},{6,14},{8,0},{10,2},{12,4},{14,6},{16,24},{18,... | collective-permute-start | bytes 3538952 | tf_op jit(solution)/shard_map/ppermute | solution.py:176
  306.4 25.4 %collective-permute-start.9 = (f32[120,128]{1,0:T(8,128)S(1)}, f32[120,128]{1,0:T(8,128)S(1)}, u32[]{:S(2)}, u32[]{:S(2)}) collective-permute-start(f32[120,128]{1,0:T(8,128)S(1)} %bitcast_add_fusion.13), channel_id=1, source_target_pairs={{0,16},{2,18},{4,20},{6,22},{8,24},{10,26},{12,28},{14,30},{16,0},... | collective-permute-start | bytes 184328 | tf_op jit(solution)/shard_map/ppermute | solution.py:176
  343.1 13.6 %collective-permute-start.12 = (f32[2,2,2,120,128]{4,3,2,1,0:T(8,128)S(1)}, f32[2,2,2,120,128]{4,3,2,1,0:T(8,128)S(1)}, u32[]{:S(2)}, u32[]{:S(2)}) collective-permute-start(f32[2,2,2,120,128]{4,3,2,1,0:T(8,128)S(1)} %maximum_select_fusion.2), channel_id=1, source_target_pairs={{0,2},{2,0},{4,6},{6,4},{8,10},{10,8},{12,14},{14,12},{16,18},{18,... | collective-permute-start | bytes 1474568 | tf_op jit(solution)/shard_map/ppermute | solution.py:176
  347.2 22.7 %collective-permute-start.18 = (bf16[2,2,48,1536]{3,2,1,0:T(8,128)(2,1)}, bf16[2,2,48,1536]{3,2,1,0:T(8,128)(2,1)}, u32[]{:S(2)}, u32[]{:S(2)}) collective-permute-start(bf16[2,2,48,1536]{3,2,1,0:T(8,128)(2,1)} %fusion.115), channel_id=1, source_target_pairs={{0,8},{2,10},{4,12},{6,14},{8,0},{10,2},{12,4},{14,6},{16,24},{18,... | collective-permute-start | bytes 1769480 | tf_op jit(solution)/shard_map/ppermute | solution.py:176
  352.1 20.2 %collective-permute-start.14 = (bf16[2,2,48,1536]{3,2,1,0:T(8,128)(2,1)}, bf16[2,2,48,1536]{3,2,1,0:T(8,128)(2,1)}, u32[]{:S(2)}, u32[]{:S(2)}) collective-permute-start(bf16[2,2,48,1536]{3,2,1,0:T(8,128)(2,1)} %fusion.114), channel_id=1, source_target_pairs={{0,4},{2,6},{4,0},{6,2},{8,12},{10,14},{12,8},{14,10},{16,20},{18,... | collective-permute-start | bytes 1769480 | tf_op jit(solution)/shard_map/ppermute | solution.py:176
  355.3 19.1 %collective-permute-start.2 = (bf16[2,2,48,4,384]{4,2,0,1,3:T(8,128)(2,1)}, bf16[2,2,48,4,384]{4,2,0,1,3:T(8,128)(2,1)}, u32[]{:S(2)}, u32[]{:S(2)}) collective-permute-start(bf16[2,2,48,4,384]{4,2,0,1,3:T(8,128)(2,1)} %fusion.113), channel_id=1, source_target_pairs={{0,2},{2,0},{4,6},{6,4},{8,10},{10,8},{12,14},{14,12},{16,18},{18,... | collective-permute-start | bytes 1769480 | tf_op jit(solution)/shard_map/ppermute | solution.py:176
  373.6 12.1 %collective-permute-start.15 = (bf16[2,48,1536]{2,1,0:T(8,128)(2,1)S(1)}, bf16[2,48,1536]{2,1,0:T(8,128)(2,1)S(1)}, u32[]{:S(2)}, u32[]{:S(2)}) collective-permute-start(bf16[2,48,1536]{2,1,0:T(8,128)(2,1)S(1)} %fusion.135), channel_id=1, source_target_pairs={{0,8},{2,10},{4,12},{6,14},{8,0},{10,2},{12,4},{14,6},{16,24},{18,... | collective-permute-start | bytes 884744 | tf_op jit(solution)/shard_map/ppermute | solution.py:176
  378.6 14.9 %collective-permute-start.20 = (bf16[48,1536]{1,0:T(8,128)(2,1)S(1)}, bf16[48,1536]{1,0:T(8,128)(2,1)S(1)}, u32[]{:S(2)}, u32[]{:S(2)}) collective-permute-start(bf16[48,1536]{1,0:T(8,128)(2,1)S(1)} %fusion.141), channel_id=1, source_target_pairs={{0,16},{2,18},{4,20},{6,22},{8,24},{10,26},{12,28},{14,30},{16,0},... | collective-permute-start | bytes 442376 | tf_op jit(solution)/shard_map/ppermute | solution.py:176
  382.5 10.3 %collective-permute-start.4 = (bf16[48,4,384]{2,0,1:T(8,128)(2,1)S(1)}, bf16[48,4,384]{2,0,1:T(8,128)(2,1)S(1)}, u32[]{:S(2)}, u32[]{:S(2)}) collective-permute-start(bf16[48,4,384]{2,0,1:T(8,128)(2,1)S(1)} %fusion.139), channel_id=1, source_target_pairs={{0,16},{2,18},{4,20},{6,22},{8,24},{10,26},{12,28},{14,30},{16,0},... | collective-permute-start | bytes 442376 | tf_op jit(solution)/shard_map/ppermute | solution.py:176
  (162 other events, 589.2 us)
Sparse Core Ops, SparseCore 0:
  9.6 12.5 all-gather.4
  66.6 10.2 reduce-scatter.8
  79.6 9.0 reduce-scatter.12
  90.7 10.9 all-gather.6
  104.3 8.9 reduce-scatter.14
  115.4 10.1 reduce-scatter.10
  135.0 11.0 all-gather.8
  148.4 8.9 reduce-scatter.18
  160.0 10.2 reduce-scatter.16
  189.7 10.9 all-gather.10
  257.5 8.9 reduce-scatter.22
  312.3 8.1 reduce-scatter.20

commit v4 on v3

--- a/solution.py
+++ b/solution.py
@@ -2,6 +2,7 @@
 import jax.numpy as jnp
 from jax import lax
 from jax.sharding import PartitionSpec as P
+
 
 D = 768
 H = 12
@@ -192,7 +193,8 @@
         mine = (me >> bit) & 1
         keep = lax.dynamic_index_in_dim(chunk, mine, axis=0, keepdims=False)
         send = lax.dynamic_index_in_dim(chunk, 1 - mine, axis=0, keepdims=False)
-        chunk = keep + xor_exchange(send.astype(wire), 1 << bit, size).astype(chunk.dtype)
+        received = xor_exchange(send.astype(wire), 1 << bit, size)
+        chunk = keep + received.astype(chunk.dtype)
     return chunk
 
 
@@ -216,14 +218,21 @@
     return jnp.transpose(shaped, [canonical.index(bit) for bit in order] + rest)
 
 
-def dp_reduce(scattered, colours_of, replicated, size, wire, lanes=128):
+def reduce_scattered(pieces, colours_of, size, wire):
     bits = size.bit_length() - 1
     me = lax.axis_index("dp")
     orders = bit_orders(bits, 3)
-    scattered_out = []
-    for piece, colour in zip(scattered, colours_of):
+    out = []
+    for piece, colour in zip(pieces, colours_of):
         chunk = ordered(piece, orders[colour], size, bits)
-        scattered_out.append(halve(chunk, orders[colour], me, size, wire))
+        out.append(halve(chunk, orders[colour], me, size, wire))
+    return out
+
+
+def reduce_replicated(replicated, size, wire, lanes=128):
+    bits = size.bit_length() - 1
+    me = lax.axis_index("dp")
+    order = bit_orders(bits, 3)[0]
     blocks = []
     for piece in replicated:
         flat = piece.reshape(-1)
@@ -232,20 +241,19 @@
     joined = jnp.concatenate(blocks)
     rows = joined.shape[0]
     joined = jnp.pad(joined, ((0, (-rows) % (size * 8)), (0, 0)))
-    chunk = ordered(joined, orders[0], size, bits)
-    block = halve(chunk, orders[0], me, size, wire)
-    full = double(block, orders[0], me, size, bits)
-    replicated_out = []
+    chunk = ordered(joined, order, size, bits)
+    block = halve(chunk, order, me, size, wire)
+    full = double(block, order, me, size, bits)
+    out = []
     offset = 0
     for piece in replicated:
         count = -(-piece.size // lanes)
-        replicated_out.append(
-            full[offset : offset + count].reshape(-1)[: piece.size].reshape(piece.shape)
-        )
+        out.append(full[offset : offset + count].reshape(-1)[: piece.size].reshape(piece.shape))
         offset += count
-    return scattered_out, replicated_out
-
-def body(
+    return out
+
+
+def layer_body(
     text_input,
     layout_input,
     repeated,
@@ -362,6 +370,10 @@
     text_wup_grad, text_upbias_grad, text_wdown_grad_t, text_normed_part = feed_back(
         text_full, text_active, text_gelu_back, text_full_grad, text_wup, text_wdown, "rf,rd->df"
     )
+    n_dp = lax.axis_size("dp")
+    wup_share, wdown_share_t = reduce_scattered(
+        (text_wup_grad, text_wdown_grad_t), (0, 1), n_dp, jnp.bfloat16
+    )
     layout_wup_grad, layout_upbias_grad, layout_wdown_grad, layout_normed_part = feed_back(
         layout_full, layout_active, layout_gelu_back, layout_full_grad, layout_wup, layout_wdown
     )
@@ -430,7 +442,6 @@
     )
     text_dinput = (text_mixed_grad + text_input_sum).astype(jnp.bfloat16)
     layout_dinput = (layout_mixed_grad + layout_input_sum).astype(jnp.bfloat16)
-    n_dp = lax.axis_size("dp")
     n_mp = lax.axis_size("mp")
     small = jnp.concatenate(
         [
@@ -456,11 +467,7 @@
         ]
     )
     small = xor_sum(small, "mp", n_mp)
-    scattered = (
-        jnp.concatenate([text_qkv_grad_t, text_wout_grad_t[:, None, :]], axis=1),
-        text_wup_grad,
-        text_wdown_grad_t,
-    )
+    scattered = (jnp.concatenate([text_qkv_grad_t, text_wout_grad_t[:, None, :]], axis=1),)
     replicated = (
         text_qvbias_grad,
         text_upbias_grad,
@@ -472,14 +479,11 @@
         layout_wdown_grad,
         small,
     )
-    scattered, replicated = lax.optimization_barrier((scattered, replicated))
-    scattered_out, replicated_out = dp_reduce(
-        scattered, (2, 0, 1), replicated, n_dp, jnp.bfloat16
-    )
+    scattered_out = reduce_scattered(scattered, (2,), n_dp, jnp.bfloat16)
+    replicated_out = reduce_replicated(replicated, n_dp, jnp.bfloat16)
     qkv_share = jnp.transpose(scattered_out[0][:, :3], (1, 0, 2))
     wout_share = scattered_out[0][:, 3].T
-    wup_share = scattered_out[1]
-    wdown_share = scattered_out[2].T
+    wdown_share = wdown_share_t.T
     summed = replicated_out[:8]
     small_sum = replicated_out[8]
     sizes = (2 * D, 2 * D, 2 * D, 2 * DL, 2 * DL, 2 * DL)
@@ -565,4 +569,4 @@
         P(),
         P(),
     )
-    return jax.shard_map(body, mesh=mesh, in_specs=in_specs, out_specs=out_specs, check_vma=False)
+    return jax.shard_map(layer_body, mesh=mesh, in_specs=in_specs, out_specs=out_specs, check_vma=False)

time: 411 us -> 483 us (1.18)
  waiting for transfers between devices: 61.6 us -> 116 us
  other arithmetic: 71.9 us -> 81.2 us
    ppermute x20, waiting for transfers between devices: 40.2 us -> 90.3 us  [xor_exchange(): return lax.ppermute(values, 'dp', [(i, i ^ step) for i in range(size)])]
    optimization_barrier x3 -> x0, local copies, waits for them, and re-layouts: 6.37 us -> none  [body(): scattered, replicated = lax.optimization_barrier((scattered, replicated))]
    dot_general x0 -> x4, local copies, waits for them, and re-layouts: none -> 6.29 us  [the longest x3 3.63 us: input_back(): jnp.einsum('rd,re->de', rows, piece, preferred_element_type=jnp.float32)]
    reshape x22, local copies, waits for them, and re-layouts: 8.52 us -> 14.8 us  [the longest x6 6.16 us: reduce_replicated(): blocks.append(flat.reshape(-1, lanes))]
    dot_general x6, matrix products: 8.34 us -> 13.6 us  [the longest x1 3.45 us: layer_body(): jnp.einsum('re,rd->de', text_context, text_wide_grad, preferred_element_t...]
    unnamed x236 -> x228, local copies, waits for them, and re-layouts: 21.1 us -> 24.9 us
    while x96 -> x64, local copies, waits for them, and re-layouts: 19.7 us -> 16.7 us  [the longest x8 8.46 us: layer_body(): lax.map(attend_back, back_blocks)]
    add x18 -> x17, other arithmetic: 13.4 us -> 14.1 us  [the longest x15 12.9 us: halve(): chunk = keep + received.astype(chunk.dtype)]
  transfers between devices with their start and end apart: 33 -> 33, of which waited for: 14 -> 17; matrix products, arithmetic and copies ran while one was open for 39% -> 32% of each run, Pallas kernels for 0% -> 0%
where the time goes in v4:
time: 483 us; the launch traced here: 477 us
  waiting for transfers between devices  116 us (24%)
  matrix products  113 us (23%)
  local copies, waits for them, and re-layouts  112 us (23%)
  other arithmetic  81.2 us (17%)
  starting transfers between devices  29.9 us (6%)
  between operations  16 us (3%)
  blocking collectives  8.85 us (2%)
    ppermute x20, waiting for transfers between devices, xor_exchange(): return lax.ppermute(values, 'dp', [(i, i ^ step) for i in range(size)])  90.3 us
    ppermute x20, starting transfers between devices, xor_exchange(): return lax.ppermute(values, 'dp', [(i, i ^ step) for i in range(size)])  28.2 us
    unnamed x228, local copies, waits for them, and re-layouts  24.9 us
    reduce_sum x8, other arithmetic, layer_norm(): centered = values - jnp.mean(values, axis=-1, keepdims=True)  12.9 us
    add x15, other arithmetic, halve(): chunk = keep + received.astype(chunk.dtype)  12.9 us
    dot_general x2, matrix products, feed_back(): jnp.einsum('rd,fd->rf', full_grad, w_down, preferred_element_type=jnp.flo...  9.91 us
  transfers between devices with their start and end apart: 33, of which 17 were waited for; matrix products, arithmetic and copies ran while one was open for 32% of the time, Pallas kernels for 0%

profile of v4, /device:TPU:0, one launch (start us, length us, event | category | flops | bytes accessed | tf_op | source)
XLA Modules:
  0.0 477.1 jit_solution(7509591699954342929)
XLA Ops:
  18.4 3.8 all-gather.5.cloned.1.call-done
  22.1 4.0 convolution_bitcast_fusion
  28.1 3.7 squeeze.168
  43.1 19.1 %while.34 = (s32[]{:T(128)}, bf16[2,512,6,64]{1,3,2,0:T(8,128)(2,1)}, bf16[2,512,6,16]{1,3,2,0:T(8,128)(2,1)}, f32[2,6,512,1]{2,1,3,0:T(8,128)}, bf16[2,512,6,64...) while((s32[]{:T(128)}, ...), condition=%wide.region_3.4_spmd, body=%wide.region_0.3_spmd.sunk | while | flops 519287808 | bytes 53192936 | solution.py:302
  69.1 6.0 %reduce-scatter.13.cloned.1.call-done = bf16[512,192]{0,1:T(8,128)(2,1)} async-done(((bf16[1024,192]{0,1:T(8,128)(2,1)}), bf16[512,192]{0,1:T(8,128)(2,1)}) %reduce-scatter.13.cloned.1.call-update) | async-done | bytes 196624 | tf_op jit(solution)/shard_map/reduce_scatter | solution.py:311
  99.5 7.8 %reduce-scatter.9.cloned.1.call-done = bf16[512,768]{1,0:T(8,128)(2,1)} async-done(((bf16[1024,768]{1,0:T(8,128)(2,1)}), bf16[512,768]{1,0:T(8,128)(2,1)}) %reduce-scatter.9.cloned.1.call-update) | async-done | bytes 786448 | tf_op jit(solution)/shard_map/reduce_scatter | solution.py:308
  123.4 7.1 %multiply_convert_fusion.1 = (bf16[1024,1536]{1,0:T(8,128)(2,1)S(1)}, f32[1024,1536]{1,0:T(8,128)}) fusion(f32[1536]{0:T(1024)} %convert_element_type.431, bf16[1024,768]{1,0:T(8,128)(2,1)} %all-gather.7.cloned.1.call-done, bf16[768,1536]{1,0:T(8,128)(2,1)S(1)} %copy-done), kind=kOutput, calls=%fused_computation.103 | convolution fusion | flops 2425356288 | bytes 13375488 | tf_op jit(solution)/shard_map/dot_general | solution.py:124
  132.2 3.7 convolution_convert_fusion.4
  183.6 5.2 %fusion.177 = f32[768,1536]{1,0:T(8,128)S(1)} fusion(bf16[1024,768]{1,0:T(8,128)(2,1)} %all-gather.9.cloned.1.call-done, bf16[1024,1536]{1,0:T(8,128)(2,1)} %copy-done.43), kind=kOutput, calls=%fused_computation.354 | convolution fusion | flops 2415919104 | bytes 9437184 | tf_op jit(solution)/shard_map/rf,rd->df/dot_general | solution.py:131
  193.9 8.3 %convert_reduce_fusion = (f32[1536]{0:T(1024)}, bf16[1024,1536]{1,0:T(8,128)(2,1)S(1)}) fusion(f32[1024,1536]{1,0:T(8,128)} %get-tuple-element.387, f32[1536]{0:T(1024)S(1)} %copy-done.102, bf16[1024,768]{1,0:T(8,128)(2,1)S(1)} %copy-done.54, bf16[1536,768]{1,0:T(8,128)(2,1)S(1)} %copy-done.115), kind=kOutput, calls=%fused_computation.101 | convolution fusion | flops 2441083392 | bytes 13381632 | tf_op jit(solution)/shard_map/rd,fd->rf/dot_general | solution.py:132
  209.7 3.8 convolution_convert_fusion.3
  213.6 7.1 %collective-permute-done.17 = bf16[2,2,2,48,1536]{4,3,2,1,0:T(8,128)(2,1)} collective-permute-done((bf16[2,2,2,48,1536]{4,3,2,1,0:T(8,128)(2,1)}, bf16[2,2,2,48,1536]{4,3,2,1,0:T(8,128)(2,1)}, u32[]{:S(2)}, u32[]{:S(2)}) %collective-permute-start.17) | collective-permute-done | bytes 1179680 | tf_op jit(solution)/shard_map/ppermute | solution.py:177
  225.2 11.2 %collective-permute-done.13 = bf16[2,2,2,48,1536]{4,3,2,1,0:T(8,128)(2,1)} collective-permute-done((bf16[2,2,2,48,1536]{4,3,2,1,0:T(8,128)(2,1)}, bf16[2,2,2,48,1536]{4,3,2,1,0:T(8,128)(2,1)}, u32[]{:S(2)}, u32[]{:S(2)}) %collective-permute-start.13) | collective-permute-done | bytes 1179680 | tf_op jit(solution)/shard_map/ppermute | solution.py:177
  240.6 12.1 %collective-permute-done.14 = bf16[2,2,48,1536]{3,2,1,0:T(8,128)(2,1)S(1)} collective-permute-done((bf16[2,2,48,1536]{3,2,1,0:T(8,128)(2,1)S(1)}, bf16[2,2,48,1536]{3,2,1,0:T(8,128)(2,1)S(1)}, u32[]{:S(2)}, u32[]{:S(2)}) %collective-permute-start.14) | collective-permute-done | bytes 589856 | tf_op jit(solution)/shard_map/ppermute | solution.py:177
  257.0 6.3 %collective-permute-done.15 = bf16[2,48,1536]{2,1,0:T(8,128)(2,1)S(1)} collective-permute-done((bf16[2,48,1536]{2,1,0:T(8,128)(2,1)S(1)}, bf16[2,48,1536]{2,1,0:T(8,128)(2,1)S(1)}, u32[]{:S(2)}, u32[]{:S(2)}) %collective-permute-start.15) | collective-permute-done | bytes 294944 | tf_op jit(solution)/shard_map/ppermute | solution.py:177
  276.1 6.3 %all-gather.11.cloned.1.call-done = bf16[1024,768]{1,0:T(8,128)(2,1)} async-done(((bf16[512,768]{1,0:T(8,128)(2,1)}), bf16[1024,768]{1,0:T(8,128)(2,1)}) %all-gather.11.cloned.1.call-update) | async-done | bytes 1572880 | tf_op jit(solution)/shard_map/all_gather | solution.py:397
  290.7 32.8 %while.35 = (s32[]{:T(128)}, bf16[2,512,6,64]{1,3,2,0:T(8,128)(2,1)}, bf16[2,512,6,64]{1,3,2,0:T(8,128)(2,1)}, bf16[2,512,6,64]{1,3,2,0:T(8,128)(2,1)}, bf16[2,5...) while((s32[]{:T(128)}, ...), condition=%wide.region_28.29_spmd, body=%wide.region_26.28_spmd.sunk | while | flops 1279964160 | bytes 101724096 | solution.py:417
  345.1 3.5 convolution_bitcast_fusion.1
  365.2 3.5 collective-permute-done.6
  391.5 21.9 %collective-permute-done.10 = f32[2,120,128]{2,1,0:T(8,128)S(1)} collective-permute-done((f32[2,120,128]{2,1,0:T(8,128)S(1)}, f32[2,120,128]{2,1,0:T(8,128)S(1)}, u32[]{:S(2)}, u32[]{:S(2)}) %collective-permute-start.10) | collective-permute-done | bytes 122912 | tf_op jit(solution)/shard_map/ppermute | solution.py:177
  415.1 4.7 collective-permute-done.11
  427.5 7.5 %collective-permute-done.12 = f32[2,2,2,120,128]{4,3,2,1,0:T(8,128)} collective-permute-done((f32[2,2,2,120,128]{4,3,2,1,0:T(8,128)}, f32[2,2,2,120,128]{4,3,2,1,0:T(8,128)}, u32[]{:S(2)}, u32[]{:S(2)}) %collective-permute-start.12) | collective-permute-done | bytes 491552 | tf_op jit(solution)/shard_map/ppermute | solution.py:177
  437.2 6.1 %collective-permute-done.1 = bf16[2,2,48,4,384]{4,2,0,1,3:T(8,128)(2,1)} collective-permute-done((bf16[2,2,48,4,384]{4,2,0,1,3:T(8,128)(2,1)}, bf16[2,2,48,4,384]{4,2,0,1,3:T(8,128)(2,1)}, u32[]{:S(2)}, u32[]{:S(2)}) %collective-permute-start.1) | collective-permute-done | bytes 589856 | tf_op jit(solution)/shard_map/ppermute | solution.py:177
  459.6 6.2 %collective-permute-done.3 = bf16[48,4,384]{2,0,1:T(8,128)(2,1)S(1)} collective-permute-done((bf16[48,4,384]{2,0,1:T(8,128)(2,1)S(1)}, bf16[48,4,384]{2,0,1:T(8,128)(2,1)S(1)}, u32[]{:S(2)}, u32[]{:S(2)}) %collective-permute-start.3) | collective-permute-done | bytes 147488 | tf_op jit(solution)/shard_map/ppermute | solution.py:177
  (617 shorter events, 310.6 us)
Async XLA Ops:
  7.2 14.9 %all-gather.5.cloned.1.call-start = ((), (), s32[]{:S(2)}) async-start(), calls=%async_computation.8 | async-start | bytes 2359296 | tf_op jit(solution)/shard_map/all_gather | solution.py:286
  7.9 67.2 %reduce-scatter.13.cloned.1.call-start = ((), (), s32[]{:S(2)}) async-start(), calls=%async_computation.12 | async-start | bytes 589824 | tf_op jit(solution)/shard_map/reduce_scatter | solution.py:311
  66.0 29.1 %reduce-scatter.15.cloned.1.call-start = ((), (), s32[]{:S(2)}) async-start(), calls=%async_computation.13 | async-start | bytes 589824 | tf_op jit(solution)/shard_map/reduce_scatter | solution.py:345
  85.9 21.4 %reduce-scatter.9.cloned.1.call-start = ((), (), s32[]{:S(2)}) async-start(), calls=%async_computation.9 | async-start | bytes 2359296 | tf_op jit(solution)/shard_map/reduce_scatter | solution.py:308
  91.8 31.6 %all-gather.7.cloned.1.call-start = ((), (), s32[]{:S(2)}) async-start(), calls=%async_computation.10 | async-start | bytes 2359296 | tf_op jit(solution)/shard_map/all_gather | solution.py:332
  112.2 32.2 %reduce-scatter.19.cloned.1.call-start = ((), (), s32[]{:S(2)}) async-start(), calls=%async_computation.17 | async-start | bytes 589824 | tf_op jit(solution)/shard_map/reduce_scatter | solution.py:384
  122.3 25.5 %reduce-scatter.11.cloned.1.call-start = ((), (), s32[]{:S(2)}) async-start(), calls=%async_computation.11 | async-start | bytes 2359296 | tf_op jit(solution)/shard_map/reduce_scatter | solution.py:342
  135.9 47.7 %all-gather.9.cloned.1.call-start = ((), (), s32[]{:S(2)}) async-start(), calls=%async_computation.14 | async-start | bytes 2359296 | tf_op jit(solution)/shard_map/all_gather | solution.py:367
  157.0 109.3 %reduce-scatter.17.cloned.1.call-start = ((), (), s32[]{:S(2)}) async-start(), calls=%async_computation.15 | async-start | bytes 2359296 | tf_op jit(solution)/shard_map/reduce_scatter | solution.py:381
  192.2 28.5 %collective-permute-start.17 = (bf16[2,2,2,48,1536]{4,3,2,1,0:T(8,128)(2,1)}, bf16[2,2,2,48,1536]{4,3,2,1,0:T(8,128)(2,1)}, u32[]{:S(2)}, u32[]{:S(2)}) collective-permute-start(bf16[2,2,2,48,1536]{4,3,2,1,0:T(8,128)(2,1)} %fusion.111), channel_id=1, source_target_pairs={{0,4},{2,6},{4,0},{6,2},{8,12},{10,14},{12,8},{14,10},{16,20},{18,... | collective-permute-start | bytes 3538952 | tf_op jit(solution)/shard_map/ppermute | solution.py:177
  208.3 28.2 %collective-permute-start.13 = (bf16[2,2,2,48,1536]{4,3,2,1,0:T(8,128)(2,1)}, bf16[2,2,2,48,1536]{4,3,2,1,0:T(8,128)(2,1)}, u32[]{:S(2)}, u32[]{:S(2)}) collective-permute-start(bf16[2,2,2,48,1536]{4,3,2,1,0:T(8,128)(2,1)} %fusion.110), channel_id=1, source_target_pairs={{0,2},{2,0},{4,6},{6,4},{8,10},{10,8},{12,14},{14,12},{16,18},{18,... | collective-permute-start | bytes 3538952 | tf_op jit(solution)/shard_map/ppermute | solution.py:177
  213.5 68.8 %all-gather.11.cloned.1.call-start = ((), (), s32[]{:S(2)}) async-start(), calls=%async_computation.16 | async-start | bytes 2359296 | tf_op jit(solution)/shard_map/all_gather | solution.py:397
  223.4 15.2 %collective-permute-start.18 = (bf16[2,2,48,1536]{3,2,1,0:T(8,128)(2,1)S(1)}, bf16[2,2,48,1536]{3,2,1,0:T(8,128)(2,1)S(1)}, u32[]{:S(2)}, u32[]{:S(2)}) collective-permute-start(bf16[2,2,48,1536]{3,2,1,0:T(8,128)(2,1)S(1)} %fusion.116), channel_id=1, source_target_pairs={{0,8},{2,10},{4,12},{6,14},{8,0},{10,2},{12,4},{14,6},{16,24},{18,... | collective-permute-start | bytes 1769480 | tf_op jit(solution)/shard_map/ppermute | solution.py:177
  238.2 14.5 %collective-permute-start.14 = (bf16[2,2,48,1536]{3,2,1,0:T(8,128)(2,1)S(1)}, bf16[2,2,48,1536]{3,2,1,0:T(8,128)(2,1)S(1)}, u32[]{:S(2)}, u32[]{:S(2)}) collective-permute-start(bf16[2,2,48,1536]{3,2,1,0:T(8,128)(2,1)S(1)} %fusion.115), channel_id=1, source_target_pairs={{0,4},{2,6},{4,0},{6,2},{8,12},{10,14},{12,8},{14,10},{16,20},{18,... | collective-permute-start | bytes 1769480 | tf_op jit(solution)/shard_map/ppermute | solution.py:177
  238.8 15.6 %collective-permute-start.19 = (bf16[2,48,1536]{2,1,0:T(8,128)(2,1)S(1)}, bf16[2,48,1536]{2,1,0:T(8,128)(2,1)S(1)}, u32[]{:S(2)}, u32[]{:S(2)}) collective-permute-start(bf16[2,48,1536]{2,1,0:T(8,128)(2,1)S(1)} %fusion.137), channel_id=1, source_target_pairs={{0,2},{2,0},{4,6},{6,4},{8,10},{10,8},{12,14},{14,12},{16,18},{18,... | collective-permute-start | bytes 884744 | tf_op jit(solution)/shard_map/ppermute | solution.py:177
  254.5 11.0 %collective-permute-start.20 = (bf16[48,1536]{1,0:T(8,128)(2,1)S(1)}, bf16[48,1536]{1,0:T(8,128)(2,1)S(1)}, u32[]{:S(2)}, u32[]{:S(2)}) collective-permute-start(bf16[48,1536]{1,0:T(8,128)(2,1)S(1)} %fusion.142), channel_id=1, source_target_pairs={{0,16},{2,18},{4,20},{6,22},{8,24},{10,26},{12,28},{14,30},{16,0},... | collective-permute-start | bytes 442376 | tf_op jit(solution)/shard_map/ppermute | solution.py:177
  273.2 152.6 %reduce-scatter.23.cloned.1.call-start = ((), (), s32[]{:S(2)}) async-start(), calls=%async_computation.19 | async-start | bytes 589824 | tf_op jit(solution)/shard_map/reduce_scatter | solution.py:439
  340.7 21.7 %collective-permute-start.5 = (bf16[2,2,2,120,128]{4,3,0,1,2:T(8,128)(2,1)}, bf16[2,2,2,120,128]{4,3,0,1,2:T(8,128)(2,1)}, u32[]{:S(2)}, u32[]{:S(2)}) collective-permute-start(bf16[2,2,2,120,128]{4,3,0,1,2:T(8,128)(2,1)} %fusion.139), channel_id=1, source_target_pairs={{0,2},{2,0},{4,6},{6,4},{8,10},{10,8},{12,14},{14,12},{16,18},{18,... | collective-permute-start | bytes 737288 | tf_op jit(solution)/shard_map/ppermute | solution.py:177
  375.6 91.6 %reduce-scatter.21.cloned.1.call-start = ((), (), s32[]{:S(2)}) async-start(), calls=%async_computation.18 | async-start | bytes 2359296 | tf_op jit(solution)/shard_map/reduce_scatter | solution.py:436
  384.3 36.8 %collective-permute-start = (bf16[2,2,2,48,4,384]{5,3,0,1,2,4:T(8,128)(2,1)S(1)}, bf16[2,2,2,48,4,384]{5,3,0,1,2,4:T(8,128)(2,1)}, u32[]{:S(2)}, u32[]{:S(2)}) collective-permute-start(bf16[2,2,2,48,4,384]{5,3,0,1,2,4:T(8,128)(2,1)S(1)} %fusion.109), channel_id=1, source_target_pairs={{0,8},{2,10},{4,12},{6,14},{8,0},{10,2},{12,4},{14,6},{16,24},{18,... | collective-permute-start | bytes 3538952 | tf_op jit(solution)/shard_map/ppermute | solution.py:177
  387.8 25.6 %collective-permute-start.10 = (f32[2,120,128]{2,1,0:T(8,128)S(1)}, f32[2,120,128]{2,1,0:T(8,128)S(1)}, u32[]{:S(2)}, u32[]{:S(2)}) collective-permute-start(f32[2,120,128]{2,1,0:T(8,128)S(1)} %maximum_select_fusion.6), channel_id=1, source_target_pairs={{0,8},{2,10},{4,12},{6,14},{8,0},{10,2},{12,4},{14,6},{16,24},{18,... | collective-permute-start | bytes 368648 | tf_op jit(solution)/shard_map/ppermute | solution.py:177
  420.6 14.4 %collective-permute-start.12 = (f32[2,2,2,120,128]{4,3,2,1,0:T(8,128)}, f32[2,2,2,120,128]{4,3,2,1,0:T(8,128)}, u32[]{:S(2)}, u32[]{:S(2)}) collective-permute-start(f32[2,2,2,120,128]{4,3,2,1,0:T(8,128)} %maximum_select_fusion.2), channel_id=1, source_target_pairs={{0,2},{2,0},{4,6},{6,4},{8,10},{10,8},{12,14},{14,12},{16,18},{18,... | collective-permute-start | bytes 1474568 | tf_op jit(solution)/shard_map/ppermute | solution.py:177
  424.3 19.0 %collective-permute-start.1 = (bf16[2,2,48,4,384]{4,2,0,1,3:T(8,128)(2,1)}, bf16[2,2,48,4,384]{4,2,0,1,3:T(8,128)(2,1)}, u32[]{:S(2)}, u32[]{:S(2)}) collective-permute-start(bf16[2,2,48,4,384]{4,2,0,1,3:T(8,128)(2,1)} %fusion.114), channel_id=1, source_target_pairs={{0,2},{2,0},{4,6},{6,4},{8,10},{10,8},{12,14},{14,12},{16,18},{18,... | collective-permute-start | bytes 1769480 | tf_op jit(solution)/shard_map/ppermute | solution.py:177
  446.3 11.4 %collective-permute-start.2 = (bf16[2,48,4,384]{3,1,0,2:T(8,128)(2,1)}, bf16[2,48,4,384]{3,1,0,2:T(8,128)(2,1)}, u32[]{:S(2)}, u32[]{:S(2)}) collective-permute-start(bf16[2,48,4,384]{3,1,0,2:T(8,128)(2,1)} %fusion.135), channel_id=1, source_target_pairs={{0,4},{2,6},{4,0},{6,2},{8,12},{10,14},{12,8},{14,10},{16,20},{18,... | collective-permute-start | bytes 884744 | tf_op jit(solution)/shard_map/ppermute | solution.py:177
  (142 other events, 607.5 us)
Sparse Core Ops, SparseCore 0:
  9.6 12.5 all-gather.4
  66.1 8.9 reduce-scatter.12
  86.0 8.9 reduce-scatter.14
  97.1 10.1 reduce-scatter.8
  112.3 11.0 all-gather.6
  125.5 8.9 reduce-scatter.18
  136.7 10.1 reduce-scatter.10
  157.2 10.9 all-gather.8
  213.6 8.1 reduce-scatter.16
  273.3 8.9 all-gather.10
  375.8 6.8 reduce-scatter.22
  391.6 9.0 reduce-scatter.20

commit v5 on v4

--- a/solution.py
+++ b/solution.py
@@ -127,20 +127,25 @@
     return (active_low, gelu_back, jnp.dot(active_low, w_down, preferred_element_type=jnp.float32))
 
 
-def feed_back(full_rows, active_low, gelu_back, full_grad, w_up, w_down, down_spec="rf,rd->fd"):
-    grad_down = jnp.einsum(down_spec, active_low, full_grad, preferred_element_type=jnp.float32)
+def feed_back(
+    full_rows, active_low, gelu_back, full_grad, w_up, w_down, down_spec="rf,rd->fd", up_rows=None, down_rows=None
+):
+    up_rows = full_rows if up_rows is None else up_rows
+    down_rows = full_grad if down_rows is None else down_rows
+    grad_down = jnp.einsum(down_spec, active_low, down_rows, preferred_element_type=jnp.float32)
     active_grad = jnp.einsum("rd,fd->rf", full_grad, w_down, preferred_element_type=jnp.float32)
     hidden_grad = gelu_back(active_grad)[0].astype(jnp.bfloat16)
-    grad_up = jnp.einsum("rd,rf->df", full_rows, hidden_grad, preferred_element_type=jnp.float32)
+    grad_up = jnp.einsum("rd,rf->df", up_rows, hidden_grad, preferred_element_type=jnp.float32)
     grad_bias = jnp.sum(hidden_grad, axis=0, dtype=jnp.float32)
     normed_part = jnp.einsum("rf,df->rd", hidden_grad, w_up, preferred_element_type=jnp.float32)
     return (grad_up, grad_bias, grad_down, normed_part)
 
 
-def input_back(rows, weight_qkv, query_grad, key_grad, value_grad, stack_axis=0):
+def input_back(rows, weight_qkv, query_grad, key_grad, value_grad, stack_axis=0, grad_rows=None):
+    grad_rows = rows if grad_rows is None else grad_rows
     grad_qkv = jnp.stack(
         [
-            jnp.einsum("rd,re->de", rows, piece, preferred_element_type=jnp.float32)
+            jnp.einsum("rd,re->de", grad_rows, piece, preferred_element_type=jnp.float32)
             for piece in (query_grad, key_grad, value_grad)
         ],
         axis=stack_axis,
@@ -218,21 +223,41 @@
     return jnp.transpose(shaped, [canonical.index(bit) for bit in order] + rest)
 
 
-def reduce_scattered(pieces, colours_of, size, wire):
+def chain_orders(size, colours):
+    bits = size.bit_length() - 1
+    return bit_orders(bits, colours)[:colours]
+
+
+def permute_columns(values, orders, size):
+    bits = size.bit_length() - 1
+    colours = len(orders)
+    lead = values.shape[:-1]
+    n = len(lead)
+    per = values.shape[-1] // size
+    shaped = values.reshape(lead + (2,) * bits + (colours, per // colours))
+    canonical = list(range(bits - 1, -1, -1))
+    parts = []
+    for colour, order in enumerate(orders):
+        part = lax.index_in_dim(shaped, colour, axis=n + bits, keepdims=False)
+        axes = list(range(n)) + [n + canonical.index(bit) for bit in order] + [n + bits]
+        parts.append(jnp.transpose(part, axes))
+    return jnp.stack(parts, axis=n).reshape(values.shape)
+
+
+def reduce_permuted(grad, orders, size, wire):
     bits = size.bit_length() - 1
     me = lax.axis_index("dp")
-    orders = bit_orders(bits, 3)
-    out = []
-    for piece, colour in zip(pieces, colours_of):
-        chunk = ordered(piece, orders[colour], size, bits)
-        out.append(halve(chunk, orders[colour], me, size, wire))
-    return out
-
-
-def reduce_replicated(replicated, size, wire, lanes=128):
+    colours = len(orders)
+    per = grad.shape[0] // size
+    shaped = grad.reshape((colours,) + (2,) * bits + (per // colours,) + grad.shape[1:])
+    return jnp.concatenate(
+        [halve(shaped[colour], orders[colour], me, size, wire) for colour in range(colours)]
+    )
+
+
+def reduce_replicated(replicated, size, wire, order, lanes=128):
     bits = size.bit_length() - 1
     me = lax.axis_index("dp")
-    order = bit_orders(bits, 3)[0]
     blocks = []
     for piece in replicated:
         flat = piece.reshape(-1)
@@ -367,16 +392,43 @@
         lax.all_gather(text_branch_grad, "mp", axis=0, tiled=True),
         lax.all_gather(layout_branch_grad, "mp", axis=0, tiled=True),
     )
+    n_dp = lax.axis_size("dp")
+    n_mp = lax.axis_size("mp")
+    per_dest = D // n_dp
+    ffn_orders = chain_orders(n_dp, 2)
+    tail_orders = chain_orders(n_dp, 3 if per_dest % 3 == 0 else 1)
     text_wup_grad, text_upbias_grad, text_wdown_grad_t, text_normed_part = feed_back(
-        text_full, text_active, text_gelu_back, text_full_grad, text_wup, text_wdown, "rf,rd->df"
-    )
-    n_dp = lax.axis_size("dp")
-    wup_share, wdown_share_t = reduce_scattered(
-        (text_wup_grad, text_wdown_grad_t), (0, 1), n_dp, jnp.bfloat16
-    )
+        text_full,
+        text_active,
+        text_gelu_back,
+        text_full_grad,
+        text_wup,
+        text_wdown,
+        "rf,rd->df",
+        up_rows=permute_columns(text_full, ffn_orders[:1], n_dp),
+        down_rows=permute_columns(text_full_grad, ffn_orders[1:], n_dp),
+    )
+    wup_share = reduce_permuted(text_wup_grad, ffn_orders[:1], n_dp, jnp.bfloat16)
+    wdown_share_t = reduce_permuted(text_wdown_grad_t, ffn_orders[1:], n_dp, jnp.bfloat16)
     layout_wup_grad, layout_upbias_grad, layout_wdown_grad, layout_normed_part = feed_back(
         layout_full, layout_active, layout_gelu_back, layout_full_grad, layout_wup, layout_wdown
     )
+    small_early = xor_sum(
+        jnp.concatenate(
+            [
+                jnp.sum(text_branch_grad, axis=0, dtype=jnp.float32),
+                text_gain_second,
+                text_shift_second,
+                jnp.sum(layout_branch_grad, axis=0, dtype=jnp.float32),
+                layout_gain_second,
+                layout_shift_second,
+            ]
+        ),
+        "mp",
+        n_mp,
+    )
+    early = (text_upbias_grad, layout_wup_grad, layout_upbias_grad, layout_wdown_grad, small_early)
+    early_out = reduce_replicated(early, n_dp, jnp.bfloat16, ffn_orders[0])
     text_normed_grad, layout_normed_grad = (
         lax.psum_scatter(
             text_normed_part.astype(jnp.bfloat16), "mp", scatter_dimension=0, tiled=True
@@ -397,18 +449,21 @@
         lax.all_gather(text_mixed_low, "mp", axis=0, tiled=True),
         lax.all_gather(layout_mixed_low, "mp", axis=0, tiled=True),
     )
+    text_context_grad = jnp.einsum(
+        "rd,ed->re", text_wide_grad, text_wout, preferred_element_type=jnp.float32
+    ).astype(jnp.bfloat16)
+    layout_context_grad = jnp.einsum(
+        "rd,ed->re", layout_wide_grad, layout_wout, preferred_element_type=jnp.float32
+    ).astype(jnp.bfloat16)
     text_wout_grad_t = jnp.einsum(
-        "re,rd->de", text_context, text_wide_grad, preferred_element_type=jnp.float32
+        "re,rd->de",
+        text_context,
+        permute_columns(text_wide_grad, tail_orders, n_dp),
+        preferred_element_type=jnp.float32,
     )
     layout_wout_grad = jnp.einsum(
         "re,rd->ed", layout_context, layout_wide_grad, preferred_element_type=jnp.float32
     )
-    text_context_grad = jnp.einsum(
-        "rd,ed->re", text_wide_grad, text_wout, preferred_element_type=jnp.float32
-    ).astype(jnp.bfloat16)
-    layout_context_grad = jnp.einsum(
-        "rd,ed->re", layout_wide_grad, layout_wout, preferred_element_type=jnp.float32
-    ).astype(jnp.bfloat16)
     back_blocks = blocks + (
         log_totals,
         blocked(text_context_grad, text_head),
@@ -424,6 +479,7 @@
         unblocked(text_kgrad),
         unblocked(text_vgrad),
         stack_axis=1,
+        grad_rows=permute_columns(text_rows, tail_orders, n_dp),
     )
     layout_qkv_grad, layout_qvbias_grad, layout_input_part = input_back(
         layout_rows,
@@ -442,56 +498,46 @@
     )
     text_dinput = (text_mixed_grad + text_input_sum).astype(jnp.bfloat16)
     layout_dinput = (layout_mixed_grad + layout_input_sum).astype(jnp.bfloat16)
-    n_mp = lax.axis_size("mp")
-    small = jnp.concatenate(
-        [
-            part.reshape(-1)
-            for part in (
-                jnp.stack(
-                    [
-                        jnp.sum(text_mixed_low, axis=0, dtype=jnp.float32),
-                        jnp.sum(text_branch_grad, axis=0, dtype=jnp.float32),
-                    ]
-                ),
-                jnp.stack([text_gain_first, text_gain_second]),
-                jnp.stack([text_shift_first, text_shift_second]),
-                jnp.stack(
-                    [
-                        jnp.sum(layout_mixed_low, axis=0, dtype=jnp.float32),
-                        jnp.sum(layout_branch_grad, axis=0, dtype=jnp.float32),
-                    ]
-                ),
-                jnp.stack([layout_gain_first, layout_gain_second]),
-                jnp.stack([layout_shift_first, layout_shift_second]),
-            )
-        ]
-    )
-    small = xor_sum(small, "mp", n_mp)
-    scattered = (jnp.concatenate([text_qkv_grad_t, text_wout_grad_t[:, None, :]], axis=1),)
-    replicated = (
-        text_qvbias_grad,
-        text_upbias_grad,
-        layout_qkv_grad,
-        layout_qvbias_grad,
-        layout_wout_grad,
-        layout_wup_grad,
-        layout_upbias_grad,
-        layout_wdown_grad,
-        small,
-    )
-    scattered_out = reduce_scattered(scattered, (2,), n_dp, jnp.bfloat16)
-    replicated_out = reduce_replicated(replicated, n_dp, jnp.bfloat16)
-    qkv_share = jnp.transpose(scattered_out[0][:, :3], (1, 0, 2))
-    wout_share = scattered_out[0][:, 3].T
+    small_late = xor_sum(
+        jnp.concatenate(
+            [
+                jnp.sum(text_mixed_low, axis=0, dtype=jnp.float32),
+                text_gain_first,
+                text_shift_first,
+                jnp.sum(layout_mixed_low, axis=0, dtype=jnp.float32),
+                layout_gain_first,
+                layout_shift_first,
+            ]
+        ),
+        "mp",
+        n_mp,
+    )
+    late = (text_qvbias_grad, layout_qkv_grad, layout_qvbias_grad, layout_wout_grad, small_late)
+    stacked = jnp.concatenate([text_qkv_grad_t, text_wout_grad_t[:, None, :]], axis=1)
+    qkv_out = reduce_permuted(stacked, tail_orders, n_dp, jnp.bfloat16)
+    late_out = reduce_replicated(late, n_dp, jnp.bfloat16, tail_orders[-1])
+    qkv_share = jnp.transpose(qkv_out[:, :3], (1, 0, 2))
+    wout_share = qkv_out[:, 3].T
     wdown_share = wdown_share_t.T
-    summed = replicated_out[:8]
-    small_sum = replicated_out[8]
-    sizes = (2 * D, 2 * D, 2 * D, 2 * DL, 2 * DL, 2 * DL)
-    shared = []
-    offset = 0
-    for size in sizes:
-        shared.append(small_sum[offset : offset + size].reshape(2, -1))
-        offset += size
+    summed = (
+        late_out[0],
+        early_out[0],
+        late_out[1],
+        late_out[2],
+        late_out[3],
+        early_out[1],
+        early_out[2],
+        early_out[3],
+    )
+
+    def pair(first, second, width, at):
+        return jnp.stack([first[at * width : (at + 1) * width], second[at * width : (at + 1) * width]])
+
+    text_small = (late_out[4][: 3 * D], early_out[4][: 3 * D])
+    layout_small = (late_out[4][3 * D :], early_out[4][3 * D :])
+    shared = [pair(*text_small, D, at) for at in range(3)] + [
+        pair(*layout_small, DL, at) for at in range(3)
+    ]
     return (
         text_final.astype(jnp.bfloat16),
         layout_final.astype(jnp.bfloat16),

time: 483 us -> 466 us (0.965)
  waiting for transfers between devices: 116 us -> 74.5 us
  starting transfers between devices: 29.9 us -> 41.8 us
  local copies, waits for them, and re-layouts: 112 us -> 123 us
  other arithmetic: 81.2 us -> 88.9 us
  matrix products: 113 us -> 106 us
    ppermute x20 -> x36, waiting for transfers between devices: 90.3 us -> 68.2 us  [xor_exchange(): return lax.ppermute(values, 'dp', [(i, i ^ step) for i in range(size)])]
    ppermute x20 -> x36, starting transfers between devices: 28.2 us -> 40 us  [xor_exchange(): return lax.ppermute(values, 'dp', [(i, i ^ step) for i in range(size)])]
    reshape x16 -> x0, local copies, waits for them, and re-layouts: 10.4 us -> none  [the longest x6 4.09 us: layer_body(): part.reshape(-1)]
    all_gather x0 -> x4, local copies, waits for them, and re-layouts: none -> 9.55 us  [the longest x1 2.65 us: layer_body(): lax.all_gather(text_input, 'mp', axis=0, tiled=True)]
    reduce_scatter x1, waiting for transfers between devices: 7.83 us -> 0.01 us  [layer_body(): lax.psum_scatter(text_mixed_part.astype(jnp.bfloat16), 'mp', scatter_dime...]
    dot_general x4 -> x0, local copies, waits for them, and re-layouts: 6.29 us -> none  [the longest x3 3.63 us: input_back(): jnp.einsum('rd,re->de', rows, piece, preferred_element_type=jnp.float32)]
    all_gather x1, waiting for transfers between devices: 6.26 us -> 0.02 us  [layer_body(): lax.all_gather(text_mixed_low, 'mp', axis=0, tiled=True)]
    convert_element_type x16 -> x28, local copies, waits for them, and re-layouts: 6.58 us -> 9.83 us  [halve(): received = xor_exchange(send.astype(wire), 1 << bit, size)]
  transfers between devices with their start and end apart: 33 -> 50, of which waited for: 17 -> 19; matrix products, arithmetic and copies ran while one was open for 32% -> 38% of each run, Pallas kernels for 0% -> 0%
where the time goes in v5:
time: 466 us; the launch traced here: 460 us
  local copies, waits for them, and re-layouts  123 us (26%)
  matrix products  106 us (23%)
  other arithmetic  88.9 us (19%)
  waiting for transfers between devices  74.5 us (16%)
  starting transfers between devices  41.8 us (9%)
  between operations  16.1 us (3%)
  blocking collectives  8.78 us (2%)
    ppermute x36, waiting for transfers between devices, xor_exchange(): return lax.ppermute(values, 'dp', [(i, i ^ step) for i in range(size)])  68.2 us
    ppermute x36, starting transfers between devices, xor_exchange(): return lax.ppermute(values, 'dp', [(i, i ^ step) for i in range(size)])  40 us
    unnamed x211, local copies, waits for them, and re-layouts  23.7 us
    add x27, other arithmetic, halve(): chunk = keep + received.astype(chunk.dtype)  15.5 us
    reduce_sum x8, other arithmetic, layer_norm(): centered = values - jnp.mean(values, axis=-1, keepdims=True)  12.7 us
    dot_general x2, matrix products, feed_back(): jnp.einsum('rd,fd->rf', full_grad, w_down, preferred_element_type=jnp.flo...  10.9 us
    convert_element_type x28, local copies, waits for them, and re-layouts, halve(): received = xor_exchange(send.astype(wire), 1 << bit, size)  9.83 us
    dot_general x2, matrix products, feed_forward(): jnp.dot(full_rows, w_up, preferred_element_type=jnp.float32) + up_bias  9.64 us
  transfers between devices with their start and end apart: 50, of which 19 were waited for; matrix products, arithmetic and copies ran while one was open for 38% of the time, Pallas kernels for 0%

profile of v5, /device:TPU:0, one launch (start us, length us, event | category | flops | bytes accessed | tf_op | source)
XLA Modules:
  0.0 459.5 jit_solution(17562034539555136986)
XLA Ops:
  22.1 4.0 convolution_bitcast_fusion
  28.1 3.9 squeeze.248
  34.7 3.4 squeeze.247
  38.1 3.6 fusion.109
  43.4 18.0 %while.34 = (s32[]{:T(128)}, bf16[2,512,6,64]{1,3,2,0:T(8,128)(2,1)}, bf16[2,512,6,16]{1,3,2,0:T(8,128)(2,1)}, f32[2,6,512,1]{2,1,3,0:T(8,128)}, bf16[2,512,6,64...) while((s32[]{:T(128)}, ...), condition=%wide.region_3.4_spmd, body=%wide.region_0.3_spmd.sunk | while | flops 519287808 | bytes 54970212 | solution.py:327
  102.4 7.2 %multiply_convert_fusion.1 = (bf16[1024,1536]{1,0:T(8,128)(2,1)S(1)}, f32[1024,1536]{1,0:T(8,128)}) fusion(f32[1536]{0:T(1024)} %convert_element_type.538, bf16[1024,768]{1,0:T(8,128)(2,1)} %all-gather.7.cloned.1.call-done, bf16[768,1536]{1,0:T(8,128)(2,1)S(1)} %copy-done), kind=kOutput, calls=%fused_computation.103 | convolution fusion | flops 2425356288 | bytes 13375488 | tf_op jit(solution)/shard_map/dot_general | solution.py:124
  111.3 3.7 convolution_convert_fusion.4
  162.6 9.4 %convert_reduce_fusion = (f32[1536]{0:T(1024)}, bf16[1024,1536]{1,0:T(8,128)(2,1)}) fusion(f32[1024,1536]{1,0:T(8,128)} %get-tuple-element.451, f32[1536]{0:T(1024)} %convert_element_type.538, bf16[1024,768]{1,0:T(8,128)(2,1)} %all-gather.9.cloned.1.call-done, bf16[1536,768]{1,0:T(8,128)(2,1)} %param.38), kind=kOutput, calls=%fused_computation.101 | convolution fusion | flops 2441083392 | bytes 13381632 | tf_op jit(solution)/shard_map/rd,fd->rf/dot_general | solution.py:136
  172.0 7.4 %concatenate.179 = f32[1190,128]{1,0:T(8,128)} concatenate(f32[12,128]{1,0:T(8,128)} %bitcast.748, f32[576,128]{1,0:T(8,128)} %reshape.1019, f32[3,128]{1,0:T(4,128)} %bitcast.758, f32[576,128]{1,0:T(8,128)} %reshape.1021, f32[23,128]{1,0:T(8,128)} %pad_bitcast_fusion), dimensions={0} | concatenate | bytes 1218560 | tf_op jit(solution)/shard_map/concatenate | solution.py:266
  196.0 5.1 %fusion.96 = f32[2,2,2,2,48,1536]{5,4,3,2,1,0:T(8,128)S(1)} fusion(bf16[1024,1536]{1,0:T(8,128)(2,1)} %copy-done.115, bf16[1024,2,2,2,2,48]{0,5,3,1,2,4:T(8,128)(2,1)} %bitcast.701), kind=kOutput, calls=%fused_computation.106 | convolution fusion | flops 2415919104 | bytes 9437184 | tf_op jit(solution)/shard_map/rf,rd->df/dot_general | solution.py:135
  207.8 4.2 fusion.98
  213.2 3.7 convolution_convert_fusion.3
  224.9 10.0 %collective-permute-done.28 = f32[2,2,80,128]{3,2,1,0:T(8,128)S(1)} collective-permute-done((f32[2,2,80,128]{3,2,1,0:T(8,128)S(1)}, f32[2,2,80,128]{3,2,1,0:T(8,128)S(1)}, u32[]{:S(2)}, u32[]{:S(2)}) %collective-permute-start.28) | collective-permute-done | bytes 163872 | tf_op jit(solution)/shard_map/ppermute | solution.py:182
  235.6 2.8 fusion.115
  239.9 5.7 %collective-permute-done.29 = f32[2,2,2,80,128]{4,3,2,1,0:T(8,128)S(1)} collective-permute-done((f32[2,2,2,80,128]{4,3,2,1,0:T(8,128)S(1)}, f32[2,2,2,80,128]{4,3,2,1,0:T(8,128)S(1)}, u32[]{:S(2)}, u32[]{:S(2)}) %collective-permute-start.29) | collective-permute-done | bytes 327712 | tf_op jit(solution)/shard_map/ppermute | solution.py:182
  254.2 14.3 %collective-permute-done.30 = bf16[2,2,2,48,1536]{4,3,2,1,0:T(8,128)(2,1)} collective-permute-done((bf16[2,2,2,48,1536]{4,3,2,1,0:T(8,128)(2,1)}, bf16[2,2,2,48,1536]{4,3,2,1,0:T(8,128)(2,1)}, u32[]{:S(2)}, u32[]{:S(2)}) %collective-permute-start.30) | collective-permute-done | bytes 1179680 | tf_op jit(solution)/shard_map/ppermute | solution.py:182
  272.3 11.6 %collective-permute-done.31 = bf16[2,2,48,1536]{3,2,1,0:T(8,128)(2,1)S(1)} collective-permute-done((bf16[2,2,48,1536]{3,2,1,0:T(8,128)(2,1)S(1)}, bf16[2,2,48,1536]{3,2,1,0:T(8,128)(2,1)S(1)}, u32[]{:S(2)}, u32[]{:S(2)}) %collective-permute-start.31) | collective-permute-done | bytes 589856 | tf_op jit(solution)/shard_map/ppermute | solution.py:182
  289.7 3.4 multiply_reduce_fusion.1
  302.2 4.7 %collective-permute-done.33 = bf16[48,1536]{1,0:T(8,128)(2,1)S(1)} collective-permute-done((bf16[48,1536]{1,0:T(8,128)(2,1)S(1)}, bf16[48,1536]{1,0:T(8,128)(2,1)S(1)}, u32[]{:S(2)}, u32[]{:S(2)}) %collective-permute-start.33) | collective-permute-done | bytes 147488 | tf_op jit(solution)/shard_map/ppermute | solution.py:182
  316.3 32.9 %while.35 = (s32[]{:T(128)}, bf16[2,512,6,64]{1,3,2,0:T(8,128)(2,1)}, bf16[2,512,6,64]{1,3,2,0:T(8,128)(2,1)}, bf16[2,512,6,64]{1,3,2,0:T(8,128)(2,1)}, bf16[2,5...) while((s32[]{:T(128)}, ...), condition=%wide.region_28.29_spmd, body=%wide.region_26.28_spmd.sunk | while | flops 1279964160 | bytes 114307136 | solution.py:472
  352.7 2.8 copy.160
  385.9 3.4 collective-permute-done.14
  410.6 3.8 collective-permute-done.19
  449.6 2.8 add_convert_fusion.2
  (700 shorter events, 321.8 us)
Async XLA Ops:
  7.2 14.9 %all-gather.5.cloned.1.call-start = ((), (), s32[]{:S(2)}) async-start(), calls=%async_computation.8 | async-start | bytes 2359296 | tf_op jit(solution)/shard_map/all_gather | solution.py:311
  7.9 75.0 %reduce-scatter.9.cloned.1.call-start = ((), (), s32[]{:S(2)}) async-start(), calls=%async_computation.9 | async-start | bytes 2359296 | tf_op jit(solution)/shard_map/reduce_scatter | solution.py:333
  66.6 22.8 %reduce-scatter.13.cloned.1.call-start = ((), (), s32[]{:S(2)}) async-start(), calls=%async_computation.12 | async-start | bytes 589824 | tf_op jit(solution)/shard_map/reduce_scatter | solution.py:336
  80.3 22.1 %all-gather.7.cloned.1.call-start = ((), (), s32[]{:S(2)}) async-start(), calls=%async_computation.10 | async-start | bytes 2359296 | tf_op jit(solution)/shard_map/all_gather | solution.py:357
  87.8 30.3 %reduce-scatter.15.cloned.1.call-start = ((), (), s32[]{:S(2)}) async-start(), calls=%async_computation.13 | async-start | bytes 589824 | tf_op jit(solution)/shard_map/reduce_scatter | solution.py:370
  100.4 31.7 %reduce-scatter.11.cloned.1.call-start = ((), (), s32[]{:S(2)}) async-start(), calls=%async_computation.11 | async-start | bytes 2359296 | tf_op jit(solution)/shard_map/reduce_scatter | solution.py:367
  115.0 32.8 %reduce-scatter.19.cloned.1.call-start = ((), (), s32[]{:S(2)}) async-start(), calls=%async_computation.17 | async-start | bytes 589824 | tf_op jit(solution)/shard_map/reduce_scatter | solution.py:436
  132.1 30.5 %all-gather.9.cloned.1.call-start = ((), (), s32[]{:S(2)}) async-start(), calls=%async_computation.14 | async-start | bytes 2359296 | tf_op jit(solution)/shard_map/all_gather | solution.py:392
  141.4 148.2 %reduce-scatter.17.cloned.1.call-start = ((), (), s32[]{:S(2)}) async-start(), calls=%async_computation.15 | async-start | bytes 2359296 | tf_op jit(solution)/shard_map/reduce_scatter | solution.py:433
  203.9 47.2 %collective-permute-start.34 = (bf16[2,2,2,48,1536]{4,3,2,1,0:T(8,128)(2,1)}, bf16[2,2,2,48,1536]{4,3,2,1,0:T(8,128)(2,1)}, u32[]{:S(2)}, u32[]{:S(2)}) collective-permute-start(bf16[2,2,2,48,1536]{4,3,2,1,0:T(8,128)(2,1)} %fusion.116), channel_id=1, source_target_pairs={{0,4},{2,6},{4,0},{6,2},{8,12},{10,14},{12,8},{14,10},{16,20},{18,... | collective-permute-start | bytes 3538952 | tf_op jit(solution)/shard_map/ppermute | solution.py:182
  216.9 90.8 %all-gather.11.cloned.1.call-start = ((), (), s32[]{:S(2)}) async-start(), calls=%async_computation.16 | async-start | bytes 2359296 | tf_op jit(solution)/shard_map/all_gather | solution.py:449
  238.4 30.1 %collective-permute-start.30 = (bf16[2,2,2,48,1536]{4,3,2,1,0:T(8,128)(2,1)}, bf16[2,2,2,48,1536]{4,3,2,1,0:T(8,128)(2,1)}, u32[]{:S(2)}, u32[]{:S(2)}) collective-permute-start(bf16[2,2,2,48,1536]{4,3,2,1,0:T(8,128)(2,1)} %fusion.115), channel_id=1, source_target_pairs={{0,2},{2,0},{4,6},{6,4},{8,10},{10,8},{12,14},{14,12},{16,18},{18,... | collective-permute-start | bytes 3538952 | tf_op jit(solution)/shard_map/ppermute | solution.py:182
  253.6 18.0 %collective-permute-start.35 = (bf16[2,2,48,1536]{3,2,1,0:T(8,128)(2,1)S(1)}, bf16[2,2,48,1536]{3,2,1,0:T(8,128)(2,1)S(1)}, u32[]{:S(2)}, u32[]{:S(2)}) collective-permute-start(bf16[2,2,48,1536]{3,2,1,0:T(8,128)(2,1)S(1)} %fusion.119), channel_id=1, source_target_pairs={{0,8},{2,10},{4,12},{6,14},{8,0},{10,2},{12,4},{14,6},{16,24},{18,... | collective-permute-start | bytes 1769480 | tf_op jit(solution)/shard_map/ppermute | solution.py:182
  270.9 13.0 %collective-permute-start.31 = (bf16[2,2,48,1536]{3,2,1,0:T(8,128)(2,1)S(1)}, bf16[2,2,48,1536]{3,2,1,0:T(8,128)(2,1)S(1)}, u32[]{:S(2)}, u32[]{:S(2)}) collective-permute-start(bf16[2,2,48,1536]{3,2,1,0:T(8,128)(2,1)S(1)} %fusion.118), channel_id=1, source_target_pairs={{0,4},{2,6},{4,0},{6,2},{8,12},{10,14},{12,8},{14,10},{16,20},{18,... | collective-permute-start | bytes 1769480 | tf_op jit(solution)/shard_map/ppermute | solution.py:182
  271.8 14.6 %collective-permute-start.36 = (bf16[2,48,1536]{2,1,0:T(8,128)(2,1)S(1)}, bf16[2,48,1536]{2,1,0:T(8,128)(2,1)S(1)}, u32[]{:S(2)}, u32[]{:S(2)}) collective-permute-start(bf16[2,48,1536]{2,1,0:T(8,128)(2,1)S(1)} %fusion.143), channel_id=1, source_target_pairs={{0,2},{2,0},{4,6},{6,4},{8,10},{10,8},{12,14},{14,12},{16,18},{18,... | collective-permute-start | bytes 884744 | tf_op jit(solution)/shard_map/ppermute | solution.py:182
  285.8 12.1 %collective-permute-start.32 = (bf16[2,48,1536]{2,1,0:T(8,128)(2,1)}, bf16[2,48,1536]{2,1,0:T(8,128)(2,1)}, u32[]{:S(2)}, u32[]{:S(2)}) collective-permute-start(bf16[2,48,1536]{2,1,0:T(8,128)(2,1)} %fusion.142), channel_id=1, source_target_pairs={{0,8},{2,10},{4,12},{6,14},{8,0},{10,2},{12,4},{14,6},{16,24},{18,... | collective-permute-start | bytes 884744 | tf_op jit(solution)/shard_map/ppermute | solution.py:182
  287.2 12.6 %collective-permute-start.37 = (bf16[48,1536]{1,0:T(8,128)(2,1)}, bf16[48,1536]{1,0:T(8,128)(2,1)}, u32[]{:S(2)}, u32[]{:S(2)}) collective-permute-start(bf16[48,1536]{1,0:T(8,128)(2,1)} %fusion.150), channel_id=1, source_target_pairs={{0,16},{2,18},{4,20},{6,22},{8,24},{10,26},{12,28},{14,30},{16,0},... | collective-permute-start | bytes 442376 | tf_op jit(solution)/shard_map/ppermute | solution.py:182
  297.7 150.0 %reduce-scatter.23.cloned.1.call-start = ((), (), s32[]{:S(2)}) async-start(), calls=%async_computation.19 | async-start | bytes 589824 | tf_op jit(solution)/shard_map/reduce_scatter | solution.py:495
  369.0 15.2 %collective-permute-start.13 = (bf16[2,2,2,40,128]{4,3,0,1,2:T(8,128)(2,1)S(1)}, bf16[2,2,2,40,128]{4,3,0,1,2:T(8,128)(2,1)}, u32[]{:S(2)}, u32[]{:S(2)}) collective-permute-start(bf16[2,2,2,40,128]{4,3,0,1,2:T(8,128)(2,1)S(1)} %fusion.154), channel_id=1, source_target_pairs={{0,8},{2,10},{4,12},{6,14},{8,0},{10,2},{12,4},{14,6},{16,24},{18,... | collective-permute-start | bytes 245768 | tf_op jit(solution)/shard_map/ppermute | solution.py:182
  375.0 74.6 %reduce-scatter.21.cloned.1.call-start = ((), (), s32[]{:S(2)}) async-start(), calls=%async_computation.18 | async-start | bytes 2359296 | tf_op jit(solution)/shard_map/reduce_scatter | solution.py:492
  396.1 20.8 %collective-permute-start.4 = (bf16[2,2,2,16,4,384]{5,3,4,2,1,0:T(8,128)(2,1)}, bf16[2,2,2,16,4,384]{5,3,4,2,1,0:T(8,128)(2,1)}, u32[]{:S(2)}, u32[]{:S(2)}) collective-permute-start(bf16[2,2,2,16,4,384]{5,3,4,2,1,0:T(8,128)(2,1)} %fusion.133), channel_id=1, source_target_pairs={{0,4},{2,6},{4,0},{6,2},{8,12},{10,14},{12,8},{14,10},{16,20},{18,... | collective-permute-start | bytes 1179656 | tf_op jit(solution)/shard_map/ppermute | solution.py:182
  397.0 22.0 %collective-permute-start = (bf16[2,2,2,16,4,384]{5,3,4,2,1,0:T(8,128)(2,1)}, bf16[2,2,2,16,4,384]{5,3,4,2,1,0:T(8,128)(2,1)}, u32[]{:S(2)}, u32[]{:S(2)}) collective-permute-start(bf16[2,2,2,16,4,384]{5,3,4,2,1,0:T(8,128)(2,1)} %fusion.132), channel_id=1, source_target_pairs={{0,2},{2,0},{4,6},{6,4},{8,10},{10,8},{12,14},{14,12},{16,18},{18,... | collective-permute-start | bytes 1179656 | tf_op jit(solution)/shard_map/ppermute | solution.py:182
  398.4 23.0 %collective-permute-start.8 = (bf16[2,2,2,16,4,384]{5,3,4,2,1,0:T(8,128)(2,1)S(1)}, bf16[2,2,2,16,4,384]{5,3,4,2,1,0:T(8,128)(2,1)}, u32[]{:S(2)}, u32[]{:S(2)}) collective-permute-start(bf16[2,2,2,16,4,384]{5,3,4,2,1,0:T(8,128)(2,1)S(1)} %fusion.134), channel_id=1, source_target_pairs={{0,8},{2,10},{4,12},{6,14},{8,0},{10,2},{12,4},{14,6},{16,24},{18,... | collective-permute-start | bytes 1179656 | tf_op jit(solution)/shard_map/ppermute | solution.py:182
  422.7 12.7 %collective-permute-start.9 = (bf16[2,2,16,4,384]{4,2,3,1,0:T(8,128)(2,1)S(1)}, bf16[2,2,16,4,384]{4,2,3,1,0:T(8,128)(2,1)S(1)}, u32[]{:S(2)}, u32[]{:S(2)}) collective-permute-start(bf16[2,2,16,4,384]{4,2,3,1,0:T(8,128)(2,1)S(1)} %fusion.147), channel_id=1, source_target_pairs={{0,2},{2,0},{4,6},{6,4},{8,10},{10,8},{12,14},{14,12},{16,18},{18,... | collective-permute-start | bytes 589832 | tf_op jit(solution)/shard_map/ppermute | solution.py:182
  (164 other events, 674.9 us)
Sparse Core Ops, SparseCore 0:
  9.6 12.5 all-gather.4
  66.8 10.2 reduce-scatter.8
  80.4 8.9 reduce-scatter.12
  91.4 10.8 all-gather.6
  104.4 8.9 reduce-scatter.14
  115.6 10.1 reduce-scatter.10
  132.2 8.9 reduce-scatter.18
  143.3 10.9 all-gather.8
  217.0 8.1 reduce-scatter.16
  297.9 7.0 all-gather.10
  375.1 6.7 reduce-scatter.22
  403.1 8.1 reduce-scatter.20

commit v6 on v3

--- a/solution.py
+++ b/solution.py
@@ -126,20 +126,25 @@
     return (active_low, gelu_back, jnp.dot(active_low, w_down, preferred_element_type=jnp.float32))
 
 
-def feed_back(full_rows, active_low, gelu_back, full_grad, w_up, w_down, down_spec="rf,rd->fd"):
-    grad_down = jnp.einsum(down_spec, active_low, full_grad, preferred_element_type=jnp.float32)
+def feed_back(
+    full_rows, active_low, gelu_back, full_grad, w_up, w_down, down_spec="rf,rd->fd", up_rows=None, down_rows=None
+):
+    up_rows = full_rows if up_rows is None else up_rows
+    down_rows = full_grad if down_rows is None else down_rows
+    grad_down = jnp.einsum(down_spec, active_low, down_rows, preferred_element_type=jnp.float32)
     active_grad = jnp.einsum("rd,fd->rf", full_grad, w_down, preferred_element_type=jnp.float32)
     hidden_grad = gelu_back(active_grad)[0].astype(jnp.bfloat16)
-    grad_up = jnp.einsum("rd,rf->df", full_rows, hidden_grad, preferred_element_type=jnp.float32)
+    grad_up = jnp.einsum("rd,rf->df", up_rows, hidden_grad, preferred_element_type=jnp.float32)
     grad_bias = jnp.sum(hidden_grad, axis=0, dtype=jnp.float32)
     normed_part = jnp.einsum("rf,df->rd", hidden_grad, w_up, preferred_element_type=jnp.float32)
     return (grad_up, grad_bias, grad_down, normed_part)
 
 
-def input_back(rows, weight_qkv, query_grad, key_grad, value_grad, stack_axis=0):
+def input_back(rows, weight_qkv, query_grad, key_grad, value_grad, stack_axis=0, grad_rows=None):
+    grad_rows = rows if grad_rows is None else grad_rows
     grad_qkv = jnp.stack(
         [
-            jnp.einsum("rd,re->de", rows, piece, preferred_element_type=jnp.float32)
+            jnp.einsum("rd,re->de", grad_rows, piece, preferred_element_type=jnp.float32)
             for piece in (query_grad, key_grad, value_grad)
         ],
         axis=stack_axis,
@@ -216,14 +221,45 @@
     return jnp.transpose(shaped, [canonical.index(bit) for bit in order] + rest)
 
 
+def chain_orders(size, colours):
+    bits = size.bit_length() - 1
+    return bit_orders(bits, colours)[:colours]
+
+
+def permute_columns(values, orders, size):
+    bits = size.bit_length() - 1
+    colours = len(orders)
+    lead = values.shape[:-1]
+    n = len(lead)
+    per = values.shape[-1] // size
+    shaped = values.reshape(lead + (2,) * bits + (colours, per // colours))
+    canonical = list(range(bits - 1, -1, -1))
+    parts = []
+    for colour, order in enumerate(orders):
+        part = lax.index_in_dim(shaped, colour, axis=n + bits, keepdims=False)
+        axes = list(range(n)) + [n + canonical.index(bit) for bit in order] + [n + bits]
+        parts.append(jnp.transpose(part, axes))
+    return jnp.stack(parts, axis=n).reshape(values.shape)
+
+
+def reduce_permuted(grad, orders, size, wire):
+    bits = size.bit_length() - 1
+    me = lax.axis_index("dp")
+    colours = len(orders)
+    per = grad.shape[0] // size
+    shaped = grad.reshape((colours,) + (2,) * bits + (per // colours,) + grad.shape[1:])
+    return jnp.concatenate(
+        [halve(shaped[colour], orders[colour], me, size, wire) for colour in range(colours)]
+    )
+
+
 def dp_reduce(scattered, colours_of, replicated, size, wire, lanes=128):
     bits = size.bit_length() - 1
     me = lax.axis_index("dp")
     orders = bit_orders(bits, 3)
     scattered_out = []
     for piece, colour in zip(scattered, colours_of):
-        chunk = ordered(piece, orders[colour], size, bits)
-        scattered_out.append(halve(chunk, orders[colour], me, size, wire))
+        scattered_out.append(reduce_permuted(piece, [orders[colour]], size, wire))
     blocks = []
     for piece in replicated:
         flat = piece.reshape(-1)
@@ -359,8 +395,18 @@
         lax.all_gather(text_branch_grad, "mp", axis=0, tiled=True),
         lax.all_gather(layout_branch_grad, "mp", axis=0, tiled=True),
     )
+    n_dp = lax.axis_size("dp")
+    orders = chain_orders(n_dp, 3)
     text_wup_grad, text_upbias_grad, text_wdown_grad_t, text_normed_part = feed_back(
-        text_full, text_active, text_gelu_back, text_full_grad, text_wup, text_wdown, "rf,rd->df"
+        text_full,
+        text_active,
+        text_gelu_back,
+        text_full_grad,
+        text_wup,
+        text_wdown,
+        "rf,rd->df",
+        up_rows=permute_columns(text_full, [orders[0]], n_dp),
+        down_rows=permute_columns(text_full_grad, [orders[1]], n_dp),
     )
     layout_wup_grad, layout_upbias_grad, layout_wdown_grad, layout_normed_part = feed_back(
         layout_full, layout_active, layout_gelu_back, layout_full_grad, layout_wup, layout_wdown
@@ -386,7 +432,10 @@
         lax.all_gather(layout_mixed_low, "mp", axis=0, tiled=True),
     )
     text_wout_grad_t = jnp.einsum(
-        "re,rd->de", text_context, text_wide_grad, preferred_element_type=jnp.float32
+        "re,rd->de",
+        text_context,
+        permute_columns(text_wide_grad, [orders[2]], n_dp),
+        preferred_element_type=jnp.float32,
     )
     layout_wout_grad = jnp.einsum(
         "re,rd->ed", layout_context, layout_wide_grad, preferred_element_type=jnp.float32
@@ -412,6 +461,7 @@
         unblocked(text_kgrad),
         unblocked(text_vgrad),
         stack_axis=1,
+        grad_rows=permute_columns(text_rows, [orders[2]], n_dp),
     )
     layout_qkv_grad, layout_qvbias_grad, layout_input_part = input_back(
         layout_rows,
@@ -430,7 +480,6 @@
     )
     text_dinput = (text_mixed_grad + text_input_sum).astype(jnp.bfloat16)
     layout_dinput = (layout_mixed_grad + layout_input_sum).astype(jnp.bfloat16)
-    n_dp = lax.axis_size("dp")
     n_mp = lax.axis_size("mp")
     small = jnp.concatenate(
         [

time: 411 us -> 419 us (1.019)
  local copies, waits for them, and re-layouts: 108 us -> 123 us
  waiting for transfers between devices: 61.6 us -> 56 us
    all_gather x0 -> x4, local copies, waits for them, and re-layouts: none -> 7.72 us  [the longest x1 2.58 us: body(): lax.all_gather(text_input, 'mp', axis=0, tiled=True)]
    reduce_scatter x1, waiting for transfers between devices: 6.9 us -> 1.53 us  [body(): lax.psum_scatter(text_branch_part.astype(jnp.bfloat16), 'mp', scatter_dim...]
    transpose x0 -> x4, local copies, waits for them, and re-layouts: none -> 4.29 us  [permute_columns(): parts.append(jnp.transpose(part, axes))]
    unnamed x236 -> x240, local copies, waits for them, and re-layouts: 21.1 us -> 23.2 us
  transfers between devices with their start and end apart: 33 -> 33, of which waited for: 14 -> 14; matrix products, arithmetic and copies ran while one was open for 39% -> 40% of each run, Pallas kernels for 0% -> 0%
where the time goes in v6:
time: 419 us; the launch traced here: 414 us
  local copies, waits for them, and re-layouts  123 us (29%)
  matrix products  108 us (26%)
  other arithmetic  72 us (17%)
  waiting for transfers between devices  56 us (13%)
  starting transfers between devices  28.9 us (7%)
  between operations  16.2 us (4%)
  blocking collectives  8.64 us (2%)
    ppermute x20, waiting for transfers between devices, xor_exchange(): return lax.ppermute(values, 'dp', [(i, i ^ step) for i in range(size)])  39.9 us
    ppermute x20, starting transfers between devices, xor_exchange(): return lax.ppermute(values, 'dp', [(i, i ^ step) for i in range(size)])  27.4 us
    unnamed x240, local copies, waits for them, and re-layouts  23.2 us
    reduce_sum x8, other arithmetic, layer_norm(): centered = values - jnp.mean(values, axis=-1, keepdims=True)  12.6 us
    add x15, other arithmetic, halve(): keep + xor_exchange(send.astype(wire), 1 << bit, size).astype(chunk.dtype)  11.6 us
    convert_element_type x16, local copies, waits for them, and re-layouts, halve(): send.astype(wire)  10.5 us
    dot_general x2, matrix products, feed_forward(): jnp.dot(full_rows, w_up, preferred_element_type=jnp.float32) + up_bias  9.72 us
    dot_general x2, matrix products, feed_back(): jnp.einsum('rd,fd->rf', full_grad, w_down, preferred_element_type=jnp.flo...  9.71 us
  transfers between devices with their start and end apart: 33, of which 14 were waited for; matrix products, arithmetic and copies ran while one was open for 40% of the time, Pallas kernels for 0%

profile of v6, /device:TPU:0, one launch (start us, length us, event | category | flops | bytes accessed | tf_op | source)
XLA Modules:
  0.0 413.6 jit_solution(3340438251637342887)
XLA Ops:
  22.1 4.0 convolution_bitcast_fusion
  28.2 3.7 squeeze.169
  34.5 3.4 squeeze.168
  38.0 3.7 fusion.101
  43.3 18.1 %while.34 = (s32[]{:T(128)}, bf16[2,512,6,64]{1,3,2,0:T(8,128)(2,1)}, bf16[2,512,6,16]{1,3,2,0:T(8,128)(2,1)}, f32[2,6,512,1]{2,1,3,0:T(8,128)}, bf16[2,512,6,64...) while((s32[]{:T(128)}, ...), condition=%wide.region_3.4_spmd, body=%wide.region_0.3_spmd.sunk | while | flops 519287808 | bytes 54970212 | solution.py:330
  83.6 5.3 %reduce-scatter.13.cloned.1.call-done = bf16[512,192]{0,1:T(8,128)(2,1)} async-done(((bf16[1024,192]{0,1:T(8,128)(2,1)}), bf16[512,192]{0,1:T(8,128)(2,1)}) %reduce-scatter.13.cloned.1.call-update) | async-done | bytes 196624 | tf_op jit(solution)/shard_map/reduce_scatter | solution.py:339
  101.8 7.2 %multiply_convert_fusion.1 = (bf16[1024,1536]{1,0:T(8,128)(2,1)S(1)}, f32[1024,1536]{1,0:T(8,128)}) fusion(f32[1536]{0:T(1024)} %convert_element_type.422, bf16[1024,768]{1,0:T(8,128)(2,1)} %all-gather.7.cloned.1.call-done, bf16[768,1536]{1,0:T(8,128)(2,1)S(1)} %copy-done), kind=kOutput, calls=%fused_computation.103 | convolution fusion | flops 2425356288 | bytes 13375488 | tf_op jit(solution)/shard_map/dot_general | solution.py:123
  110.7 3.7 convolution_convert_fusion.4
  146.3 8.2 %convert_reduce_fusion = (f32[1536]{0:T(1024)}, bf16[1024,1536]{1,0:T(8,128)(2,1)S(1)}) fusion(f32[1024,1536]{1,0:T(8,128)} %get-tuple-element.411, f32[1536]{0:T(1024)} %convert_element_type.422, bf16[1024,768]{1,0:T(8,128)(2,1)} %all-gather.9.cloned.1.call-done, bf16[1536,768]{1,0:T(8,128)(2,1)} %param.38), kind=kOutput, calls=%fused_computation.101 | convolution fusion | flops 2441083392 | bytes 13381632 | tf_op jit(solution)/shard_map/rd,fd->rf/dot_general | solution.py:135
  156.2 3.8 convolution_convert_fusion.3
  181.6 4.3 %fusion.171 = f32[768,1536]{1,0:T(8,128)} fusion(bf16[1024,768]{0,1:T(8,128)(2,1)S(1)} %bitcast.541, bf16[1024,1536]{1,0:T(8,128)(2,1)S(1)} %copy-done.130), kind=kOutput, calls=%fused_computation.343 | convolution fusion | flops 2415919104 | bytes 9437184 | tf_op jit(solution)/shard_map/rf,rd->df/dot_general | solution.py:134
  186.0 3.4 multiply_reduce_fusion.1
  194.0 6.2 %fusion.170 = f32[768,1536]{1,0:T(8,128)} fusion(bf16[1024,768]{0,1:T(8,128)(2,1)S(1)} %bitcast.540, bf16[1024,1536]{1,0:T(8,128)(2,1)} %copy-done.131), kind=kOutput, calls=%fused_computation.342 | convolution fusion | flops 2415919104 | bytes 9437184 | tf_op jit(solution)/shard_map/rd,rf->df/dot_general | solution.py:137
  200.8 3.7 all-gather.11.cloned.1.call-done
  212.9 33.3 %while.35 = (s32[]{:T(128)}, bf16[2,512,6,64]{1,3,2,0:T(8,128)(2,1)}, bf16[2,512,6,64]{1,3,2,0:T(8,128)(2,1)}, bf16[2,512,6,64]{1,3,2,0:T(8,128)(2,1)}, bf16[2,5...) while((s32[]{:T(128)}, ...), condition=%wide.region_28.29_spmd, body=%wide.region_26.28_spmd.sunk | while | flops 1279964160 | bytes 114307136 | solution.py:454
  266.7 3.9 fusion.115
  283.4 3.8 fusion.117
  299.6 6.1 %copy.109 = f32[768,4,384]{2,0,1:T(8,128)} copy(f32[768,4,384]{0,2,1:T(8,128)} %pad_maximum_fusion) | data formatting | bytes 9437184 | tf_op jit(solution)/shard_map/optimization_barrier | solution.py:524
  315.1 5.2 %add_convert_fusion.1 = bf16[1024,768]{1,0:T(8,128)(2,1)} fusion(f32[1024,768]{1,0:T(8,128)} %fusion.117, f32[1024,768]{1,0:T(8,128)} %fusion.115, bf16[1024,384]{0,1:T(8,128)(2,1)S(1)} %bitcast.514, bf16[3,768,384]{2,1,0:T(8,128)(2,1)} %param.32), kind=kOutput, calls=%fused_computation.106 | convolution fusion | flops 606339072 | bytes 9240576 | tf_op jit(solution)/shard_map/re,de->rd/dot_general | solution.py:158
  320.4 19.6 %collective-permute-done.9 = f32[120,128]{1,0:T(8,128)S(1)} collective-permute-done((f32[120,128]{1,0:T(8,128)S(1)}, f32[120,128]{1,0:T(8,128)S(1)}, u32[]{:S(2)}, u32[]{:S(2)}) %collective-permute-start.9) | collective-permute-done | bytes 61472 | tf_op jit(solution)/shard_map/ppermute | solution.py:181
  341.6 3.3 collective-permute-done.10
  347.3 3.9 collective-permute-done.11
  390.6 3.3 collective-permute-start.4
  394.3 6.5 %collective-permute-done.4 = bf16[48,4,384]{2,0,1:T(8,128)(2,1)S(1)} collective-permute-done((bf16[48,4,384]{2,0,1:T(8,128)(2,1)S(1)}, bf16[48,4,384]{2,0,1:T(8,128)(2,1)S(1)}, u32[]{:S(2)}, u32[]{:S(2)}) %collective-permute-start.4) | collective-permute-done | bytes 147488 | tf_op jit(solution)/shard_map/ppermute | solution.py:181
  (668 shorter events, 280.4 us)
Async XLA Ops:
  7.2 14.9 %all-gather.5.cloned.1.call-start = ((), (), s32[]{:S(2)}) async-start(), calls=%async_computation.8 | async-start | bytes 2359296 | tf_op jit(solution)/shard_map/all_gather | solution.py:314
  7.9 70.7 %reduce-scatter.9.cloned.1.call-start = ((), (), s32[]{:S(2)}) async-start(), calls=%async_computation.9 | async-start | bytes 2359296 | tf_op jit(solution)/shard_map/reduce_scatter | solution.py:336
  66.6 22.3 %reduce-scatter.13.cloned.1.call-start = ((), (), s32[]{:S(2)}) async-start(), calls=%async_computation.12 | async-start | bytes 589824 | tf_op jit(solution)/shard_map/reduce_scatter | solution.py:339
  78.6 23.2 %all-gather.7.cloned.1.call-start = ((), (), s32[]{:S(2)}) async-start(), calls=%async_computation.10 | async-start | bytes 2359296 | tf_op jit(solution)/shard_map/all_gather | solution.py:360
  83.5 36.3 %reduce-scatter.15.cloned.1.call-start = ((), (), s32[]{:S(2)}) async-start(), calls=%async_computation.13 | async-start | bytes 589824 | tf_op jit(solution)/shard_map/reduce_scatter | solution.py:373
  100.0 25.8 %reduce-scatter.11.cloned.1.call-start = ((), (), s32[]{:S(2)}) async-start(), calls=%async_computation.11 | async-start | bytes 2359296 | tf_op jit(solution)/shard_map/reduce_scatter | solution.py:370
  114.4 31.9 %all-gather.9.cloned.1.call-start = ((), (), s32[]{:S(2)}) async-start(), calls=%async_computation.14 | async-start | bytes 2359296 | tf_op jit(solution)/shard_map/all_gather | solution.py:395
  135.1 29.4 %reduce-scatter.19.cloned.1.call-start = ((), (), s32[]{:S(2)}) async-start(), calls=%async_computation.17 | async-start | bytes 589824 | tf_op jit(solution)/shard_map/reduce_scatter | solution.py:418
  145.1 40.8 %reduce-scatter.17.cloned.1.call-start = ((), (), s32[]{:S(2)}) async-start(), calls=%async_computation.15 | async-start | bytes 2359296 | tf_op jit(solution)/shard_map/reduce_scatter | solution.py:415
  160.1 44.4 %all-gather.11.cloned.1.call-start = ((), (), s32[]{:S(2)}) async-start(), calls=%async_computation.16 | async-start | bytes 2359296 | tf_op jit(solution)/shard_map/all_gather | solution.py:431
  193.3 152.3 %reduce-scatter.23.cloned.1.call-start = ((), (), s32[]{:S(2)}) async-start(), calls=%async_computation.19 | async-start | bytes 589824 | tf_op jit(solution)/shard_map/reduce_scatter | solution.py:477
  266.7 137.0 %reduce-scatter.21.cloned.1.call-start = ((), (), s32[]{:S(2)}) async-start(), calls=%async_computation.18 | async-start | bytes 2359296 | tf_op jit(solution)/shard_map/reduce_scatter | solution.py:474
  294.9 10.8 %collective-permute-start.7 = (bf16[2,120,128]{2,1,0:T(8,128)(2,1)S(1)}, bf16[2,120,128]{2,1,0:T(8,128)(2,1)S(1)}, u32[]{:S(2)}, u32[]{:S(2)}) collective-permute-start(bf16[2,120,128]{2,1,0:T(8,128)(2,1)S(1)} %fusion.141), channel_id=1, source_target_pairs={{0,8},{2,10},{4,12},{6,14},{8,0},{10,2},{12,4},{14,6},{16,24},{18,... | collective-permute-start | bytes 184328 | tf_op jit(solution)/shard_map/ppermute | solution.py:181
  311.0 40.9 %collective-permute-start.17 = (bf16[2,2,2,48,1536]{4,3,2,1,0:T(8,128)(2,1)}, bf16[2,2,2,48,1536]{4,3,2,1,0:T(8,128)(2,1)}, u32[]{:S(2)}, u32[]{:S(2)}) collective-permute-start(bf16[2,2,2,48,1536]{4,3,2,1,0:T(8,128)(2,1)} %fusion.109), channel_id=1, source_target_pairs={{0,4},{2,6},{4,0},{6,2},{8,12},{10,14},{12,8},{14,10},{16,20},{18,... | collective-permute-start | bytes 3538952 | tf_op jit(solution)/shard_map/ppermute | solution.py:181
  312.5 44.4 %collective-permute-start.13 = (bf16[2,2,2,48,1536]{4,3,2,1,0:T(8,128)(2,1)S(1)}, bf16[2,2,2,48,1536]{4,3,2,1,0:T(8,128)(2,1)}, u32[]{:S(2)}, u32[]{:S(2)}) collective-permute-start(bf16[2,2,2,48,1536]{4,3,2,1,0:T(8,128)(2,1)S(1)} %fusion.108), channel_id=1, source_target_pairs={{0,2},{2,0},{4,6},{6,4},{8,10},{10,8},{12,14},{14,12},{16,18},{18,... | collective-permute-start | bytes 3538952 | tf_op jit(solution)/shard_map/ppermute | solution.py:181
  314.0 47.0 %collective-permute-start.1 = (bf16[2,2,2,48,4,384]{5,3,2,1,0,4:T(8,128)(2,1)}, bf16[2,2,2,48,4,384]{5,3,2,1,0,4:T(8,128)(2,1)}, u32[]{:S(2)}, u32[]{:S(2)}) collective-permute-start(bf16[2,2,2,48,4,384]{5,3,2,1,0,4:T(8,128)(2,1)} %fusion.107), channel_id=1, source_target_pairs={{0,8},{2,10},{4,12},{6,14},{8,0},{10,2},{12,4},{14,6},{16,24},{18,... | collective-permute-start | bytes 3538952 | tf_op jit(solution)/shard_map/ppermute | solution.py:181
  314.5 25.4 %collective-permute-start.9 = (f32[120,128]{1,0:T(8,128)S(1)}, f32[120,128]{1,0:T(8,128)S(1)}, u32[]{:S(2)}, u32[]{:S(2)}) collective-permute-start(f32[120,128]{1,0:T(8,128)S(1)} %bitcast_add_fusion.15), channel_id=1, source_target_pairs={{0,16},{2,18},{4,20},{6,22},{8,24},{10,26},{12,28},{14,30},{16,0},... | collective-permute-start | bytes 184328 | tf_op jit(solution)/shard_map/ppermute | solution.py:181
  351.2 13.6 %collective-permute-start.12 = (f32[2,2,2,120,128]{4,3,2,1,0:T(8,128)S(1)}, f32[2,2,2,120,128]{4,3,2,1,0:T(8,128)S(1)}, u32[]{:S(2)}, u32[]{:S(2)}) collective-permute-start(f32[2,2,2,120,128]{4,3,2,1,0:T(8,128)S(1)} %maximum_select_fusion.2), channel_id=1, source_target_pairs={{0,2},{2,0},{4,6},{6,4},{8,10},{10,8},{12,14},{14,12},{16,18},{18,... | collective-permute-start | bytes 1474568 | tf_op jit(solution)/shard_map/ppermute | solution.py:181
  355.4 22.7 %collective-permute-start.18 = (bf16[2,2,48,1536]{3,2,1,0:T(8,128)(2,1)}, bf16[2,2,48,1536]{3,2,1,0:T(8,128)(2,1)}, u32[]{:S(2)}, u32[]{:S(2)}) collective-permute-start(bf16[2,2,48,1536]{3,2,1,0:T(8,128)(2,1)} %fusion.113), channel_id=1, source_target_pairs={{0,8},{2,10},{4,12},{6,14},{8,0},{10,2},{12,4},{14,6},{16,24},{18,... | collective-permute-start | bytes 1769480 | tf_op jit(solution)/shard_map/ppermute | solution.py:181
  360.3 20.2 %collective-permute-start.14 = (bf16[2,2,48,1536]{3,2,1,0:T(8,128)(2,1)}, bf16[2,2,48,1536]{3,2,1,0:T(8,128)(2,1)}, u32[]{:S(2)}, u32[]{:S(2)}) collective-permute-start(bf16[2,2,48,1536]{3,2,1,0:T(8,128)(2,1)} %fusion.112), channel_id=1, source_target_pairs={{0,4},{2,6},{4,0},{6,2},{8,12},{10,14},{12,8},{14,10},{16,20},{18,... | collective-permute-start | bytes 1769480 | tf_op jit(solution)/shard_map/ppermute | solution.py:181
  363.4 19.1 %collective-permute-start.2 = (bf16[2,2,48,4,384]{4,2,1,0,3:T(8,128)(2,1)}, bf16[2,2,48,4,384]{4,2,1,0,3:T(8,128)(2,1)}, u32[]{:S(2)}, u32[]{:S(2)}) collective-permute-start(bf16[2,2,48,4,384]{4,2,1,0,3:T(8,128)(2,1)} %fusion.111), channel_id=1, source_target_pairs={{0,2},{2,0},{4,6},{6,4},{8,10},{10,8},{12,14},{14,12},{16,18},{18,... | collective-permute-start | bytes 1769480 | tf_op jit(solution)/shard_map/ppermute | solution.py:181
  381.7 12.1 %collective-permute-start.15 = (bf16[2,48,1536]{2,1,0:T(8,128)(2,1)S(1)}, bf16[2,48,1536]{2,1,0:T(8,128)(2,1)S(1)}, u32[]{:S(2)}, u32[]{:S(2)}) collective-permute-start(bf16[2,48,1536]{2,1,0:T(8,128)(2,1)S(1)} %fusion.133), channel_id=1, source_target_pairs={{0,8},{2,10},{4,12},{6,14},{8,0},{10,2},{12,4},{14,6},{16,24},{18,... | collective-permute-start | bytes 884744 | tf_op jit(solution)/shard_map/ppermute | solution.py:181
  386.8 14.8 %collective-permute-start.20 = (bf16[48,1536]{1,0:T(8,128)(2,1)S(1)}, bf16[48,1536]{1,0:T(8,128)(2,1)S(1)}, u32[]{:S(2)}, u32[]{:S(2)}) collective-permute-start(bf16[48,1536]{1,0:T(8,128)(2,1)S(1)} %fusion.139), channel_id=1, source_target_pairs={{0,16},{2,18},{4,20},{6,22},{8,24},{10,26},{12,28},{14,30},{16,0},... | collective-permute-start | bytes 442376 | tf_op jit(solution)/shard_map/ppermute | solution.py:181
  390.6 10.2 %collective-permute-start.4 = (bf16[48,4,384]{2,0,1:T(8,128)(2,1)S(1)}, bf16[48,4,384]{2,0,1:T(8,128)(2,1)S(1)}, u32[]{:S(2)}, u32[]{:S(2)}) collective-permute-start(bf16[48,4,384]{2,0,1:T(8,128)(2,1)S(1)} %fusion.137), channel_id=1, source_target_pairs={{0,16},{2,18},{4,20},{6,22},{8,24},{10,26},{12,28},{14,30},{16,0},... | collective-permute-start | bytes 442376 | tf_op jit(solution)/shard_map/ppermute | solution.py:181
  (164 other events, 571.4 us)
Sparse Core Ops, SparseCore 0:
  9.6 12.5 all-gather.4
  66.7 10.2 reduce-scatter.8
  79.8 9.0 reduce-scatter.12
  90.9 10.8 all-gather.6
  104.5 8.9 reduce-scatter.14
  115.6 10.1 reduce-scatter.10
  135.2 11.0 all-gather.8
  148.6 8.9 reduce-scatter.18
  160.2 10.2 reduce-scatter.16
  193.5 10.9 all-gather.10
  266.8 8.9 reduce-scatter.22
  320.5 8.1 reduce-scatter.20

commit v7 on v3

--- a/solution.py
+++ b/solution.py
@@ -291,7 +291,7 @@
         blocked(layout_values, layout_head),
         usable_group,
     )
-    text_context, layout_context, log_totals = lax.map(attend_window, blocks)
+    text_context, layout_context, log_totals = jax.vmap(attend_window)(blocks)
     text_context = unblocked(text_context)
     layout_context = unblocked(layout_context)
     text_mixed_part = jnp.dot(text_context, text_wout, preferred_element_type=jnp.float32)
@@ -402,8 +402,8 @@
         blocked(text_context_grad, text_head),
         blocked(layout_context_grad, layout_head),
     )
-    text_qgrad, text_kgrad, text_vgrad, layout_qgrad, layout_kgrad, layout_vgrad = lax.map(
-        attend_back, back_blocks
+    text_qgrad, text_kgrad, text_vgrad, layout_qgrad, layout_kgrad, layout_vgrad = jax.vmap(attend_back)(
+        back_blocks
     )
     text_qkv_grad_t, text_qvbias_grad, text_input_part = input_back(
         text_rows,

time: 411 us -> 416 us (1.012)
  matrix products: 110 us -> 138 us
  local copies, waits for them, and re-layouts: 108 us -> 90.7 us
  other arithmetic: 71.9 us -> 67.4 us
    while x96 -> x0, local copies, waits for them, and re-layouts: 19.7 us -> none
    all_gather x1, waiting for transfers between devices: 0.63 us -> 7.65 us  [body(): lax.all_gather(text_branch_grad, 'mp', axis=0, tiled=True)]
    reduce_scatter x1, waiting for transfers between devices: 6.9 us -> 0.02 us  [body(): lax.psum_scatter(text_branch_part.astype(jnp.bfloat16), 'mp', scatter_dim...]
    dot_general x2 -> x1, matrix products: 2.43 us -> 9.16 us  [attend_back(): jnp.einsum('qhd,khd->hqk', layout_cgrad, layout_values, preferred_element...]
    another operation x8 -> x0, local copies, waits for them, and re-layouts: 6.67 us -> none
    dot_general x2 -> x1, matrix products: 2.14 us -> 7.67 us  [attend_back(): jnp.einsum('hqk,qhd->khd', probs_low, text_cgrad, preferred_element_type=...]
    convert_element_type x2 -> x0, other arithmetic: 5.5 us -> none  [the longest x1 3.59 us: project_path(): queries = (joined[0] + biases[0]).astype(jnp.bfloat16)]
    dot_general x2 -> x1, matrix products: 1.84 us -> 7.29 us  [attend_back(): jnp.einsum('hqk,qhd->khd', probs_low, layout_cgrad, preferred_element_typ...]
  transfers between devices with their start and end apart: 33 -> 33, of which waited for: 14 -> 13; matrix products, arithmetic and copies ran while one was open for 39% -> 40% of each run, Pallas kernels for 0% -> 0%
where the time goes in v7:
time: 416 us; the launch traced here: 411 us
  matrix products  138 us (33%)
  local copies, waits for them, and re-layouts  90.7 us (22%)
  other arithmetic  67.4 us (16%)
  waiting for transfers between devices  60.6 us (15%)
  starting transfers between devices  28.6 us (7%)
  between operations  16.5 us (4%)
  blocking collectives  8.9 us (2%)
    ppermute x20, waiting for transfers between devices, xor_exchange(): return lax.ppermute(values, 'dp', [(i, i ^ step) for i in range(size)])  39.1 us
    ppermute x20, starting transfers between devices, xor_exchange(): return lax.ppermute(values, 'dp', [(i, i ^ step) for i in range(size)])  27.2 us
    unnamed x302, local copies, waits for them, and re-layouts  22.9 us
    add x15, other arithmetic, halve(): keep + xor_exchange(send.astype(wire), 1 << bit, size).astype(chunk.dtype)  11.7 us
    convert_element_type x16, local copies, waits for them, and re-layouts, halve(): send.astype(wire)  10.5 us
    reduce_sum x8, other arithmetic, layer_norm(): centered = values - jnp.mean(values, axis=-1, keepdims=True)  10.1 us
    dot_general x2, matrix products, feed_back(): jnp.einsum('rd,fd->rf', full_grad, w_down, preferred_element_type=jnp.flo...  9.77 us
    dot_general x2, matrix products, feed_back(): jnp.einsum(down_spec, active_low, full_grad, preferred_element_type=jnp.f...  9.71 us
  transfers between devices with their start and end apart: 33, of which 13 were waited for; matrix products, arithmetic and copies ran while one was open for 40% of the time, Pallas kernels for 0%

profile of v7, /device:TPU:0, one launch (start us, length us, event | category | flops | bytes accessed | tf_op | source)
XLA Modules:
  0.0 411.0 jit_solution(15439107132622629733)
XLA Ops:
  22.1 4.0 convolution_bitcast_fusion
  32.1 3.8 squeeze.119
  39.4 7.9 %fusion.47 = f32[2,6,512,512]{2,3,1,0:T(8,128)} fusion(bf16[2,512,6,64]{1,0,3,2:T(2,128)(2,1)S(1)} %convert_element_type.422, f32[2,512,6,64]{1,0,3,2:T(2,128)} %squeeze.120, f32[6,64]{1,0:T(8,128)S(1)} %reshape.745), kind=kOutput, calls=%fused_computation.117 | convolution fusion | flops 403439616 | bytes 14943744 | tf_op jit(solution)/shard_map/vmap(qhd,khd->hqk)/dot_general | solution.py:43
  47.3 6.7 %fusion.119 = (f32[2,6,512]{2,1,0:T(8,128)S(1)}, f32[2,6,512,512]{2,3,1,0:T(8,128)S(1)}) fusion(bf16[2,512,6,16]{1,0,3,2:T(2,128)(2,1)S(1)} %copy-done.39, f32[2,512,6,16]{1,0,3,2:T(2,128)S(1)} %copy-done.27, f32[6,16]{1,0:T(8,128)S(1)} %reshape.746, f32[2,6,512,512]{2,3,1,0:T(8,128)} %fusion.47, pred[2,512]{1,0:T(4,128)(4,1)S(1)} %broadcast_in_dim.36), kind=kOutput, calls=%fused_computation.286 | convolution fusion | flops 116582400 | bytes 25781632 | tf_op jit(solution)/shard_map/vmap(qhd,khd->hqk)/dot_general | solution.py:46
  78.1 3.8 fusion.36
  88.6 4.5 %reduce-scatter.13.cloned.1.call-done = bf16[512,192]{0,1:T(8,128)(2,1)} async-done(((bf16[1024,192]{0,1:T(8,128)(2,1)}), bf16[512,192]{0,1:T(8,128)(2,1)}) %reduce-scatter.13.cloned.1.call-update) | async-done | bytes 196624 | tf_op jit(solution)/shard_map/reduce_scatter | solution.py:303
  106.0 7.1 %multiply_convert_fusion.1 = (bf16[1024,1536]{1,0:T(8,128)(2,1)S(1)}, f32[1024,1536]{1,0:T(8,128)}) fusion(f32[1536]{0:T(1024)} %convert_element_type.433, bf16[1024,768]{1,0:T(8,128)(2,1)} %all-gather.7.cloned.1.call-done, bf16[768,1536]{1,0:T(8,128)(2,1)S(1)} %copy-done), kind=kOutput, calls=%fused_computation.10 | convolution fusion | flops 2425356288 | bytes 13375488 | tf_op jit(solution)/shard_map/dot_general | solution.py:123
  146.7 7.7 %all-gather.9.cloned.1.call-done = bf16[1024,768]{1,0:T(8,128)(2,1)} async-done(((bf16[512,768]{1,0:T(8,128)(2,1)}), bf16[1024,768]{1,0:T(8,128)(2,1)}) %all-gather.9.cloned.1.call-update) | async-done | bytes 1572880 | tf_op jit(solution)/shard_map/all_gather | solution.py:359
  154.4 8.2 %convert_reduce_fusion = (f32[1536]{0:T(1024)}, bf16[1024,1536]{1,0:T(8,128)(2,1)S(1)}) fusion(f32[1024,1536]{1,0:T(8,128)} %get-tuple-element.137, f32[1536]{0:T(1024)} %convert_element_type.433, bf16[1024,768]{1,0:T(8,128)(2,1)} %all-gather.9.cloned.1.call-done, bf16[1536,768]{1,0:T(8,128)(2,1)} %param.34), kind=kOutput, calls=%fused_computation.8 | convolution fusion | flops 2441083392 | bytes 13381632 | tf_op jit(solution)/shard_map/rd,fd->rf/dot_general | solution.py:131
  164.3 3.7 convolution_convert_fusion.1
  173.9 7.3 %convert_reduce_fusion.10 = (f32[6,16]{1,0:T(8,128)S(1)}, bf16[2,512,6,16]{1,3,2,0:T(8,128)(2,1)S(1)}) fusion(f32[2,6,512,512]{2,3,1,0:T(8,128)} %copy-done.2, f32[2,6,512]{2,1,0:T(8,128)S(1)} %copy-done.56, bf16[2,512,6,16]{1,0,3,2:T(2,128)(2,1)S(1)} %reshape.698), kind=kOutput, calls=%fused_computation.158 | convolution fusion | flops 107249568 | bytes 13001088 | tf_op jit(solution)/shard_map/vmap(hqk,qhd->khd)/dot_general | solution.py:100
  185.7 7.4 %fusion.121 = f32[768,1536]{1,0:T(8,128)} fusion(bf16[1024,768]{1,0:T(8,128)(2,1)} %all-gather.9.cloned.1.call-done, bf16[1024,1536]{1,0:T(8,128)(2,1)} %copy-done.34), kind=kOutput, calls=%fused_computation.288 | convolution fusion | flops 2415919104 | bytes 9437184 | tf_op jit(solution)/shard_map/rf,rd->df/dot_general | solution.py:130
  201.1 6.1 %fusion.120 = f32[768,1536]{1,0:T(8,128)} fusion(bf16[1024,768]{1,0:T(8,128)(2,1)S(1)} %copy-done.47, bf16[1024,1536]{1,0:T(8,128)(2,1)} %copy-done.35), kind=kOutput, calls=%fused_computation.287 | convolution fusion | flops 2415919104 | bytes 9437184 | tf_op jit(solution)/shard_map/rd,rf->df/dot_general | solution.py:133
  214.4 7.7 %convert_reduce_fusion.5 = (f32[6,64]{1,0:T(8,128)S(1)}, bf16[2,512,6,64]{1,3,2,0:T(8,128)(2,1)}) fusion(f32[2,6,512,512]{2,3,1,0:T(8,128)} %copy-done.2, f32[2,6,512]{2,1,0:T(8,128)} %log_add_fusion, bf16[2,512,6,64]{1,0,3,2:T(2,128)(2,1)S(1)} %reshape.697), kind=kOutput, calls=%fused_computation.48 | convolution fusion | flops 410123904 | bytes 14181888 | tf_op jit(solution)/shard_map/vmap(hqk,qhd->khd)/dot_general | solution.py:97
  222.1 6.7 %fusion.44 = f32[2,6,512,512]{2,3,1,0:T(8,128)} fusion(bf16[2,512,6,64]{1,0,3,2:T(2,128)(2,1)S(1)} %reshape.697, f32[2,512,6,64]{1,0,3,2:T(2,128)S(1)} %copy-done.11, f32[6,64]{1,0:T(8,128)S(1)} %reshape.744), kind=kOutput, calls=%fused_computation.114 | convolution fusion | flops 403439616 | bytes 14943744 | tf_op jit(solution)/shard_map/vmap(qhd,khd->hqk)/dot_general | solution.py:88
  228.8 9.2 %multiply_reduce_fusion = (f32[2,6,512]{2,1,0:T(8,128)S(1)}, f32[2,6,512,512]{2,3,1,0:T(8,128)}) fusion(f32[2,6,512,512]{2,3,1,0:T(8,128)S(1)} %bitcast.331, f32[2,6,512]{2,1,0:T(8,128)S(1)} %copy-done.57, f32[2,6,512,512]{2,3,1,0:T(8,128)} %fusion.44, f32[2,512,6,16]{1,0,3,2:T(2,128)S(1)} %copy-done.24, f32[6,16]{1,0:T(8,128)S(1)} %copy-done.77, ...), kind=kOutput, calls=%fused_computation.1 | convolution fusion | flops 113436672 | bytes 38388096 | tf_op jit(solution)/shard_map/vmap(qhd,khd->hqk)/dot_general | solution.py:91
  238.0 7.1 %multiply_convert_fusion = bf16[2,6,512,512]{2,3,1,0:T(8,128)(2,1)S(1)} fusion(f32[2,6,512,512]{2,3,1,0:T(8,128)} %get-tuple-element.141, f32[2,6,512,512]{2,3,1,0:T(8,128)S(1)} %bitcast.331, f32[2,6,512]{2,1,0:T(8,128)S(1)} %get-tuple-element.140, f32[2,6,512]{2,1,0:T(8,128)S(1)} %copy-done.57), kind=kLoop, calls=%fused_computation | loop fusion | flops 12582912 | bytes 31506432 | tf_op jit(solution)/shard_map/vmap()/convert_element_type | solution.py:96
  264.4 4.0 fusion.53
  281.9 3.7 fusion.55
  297.1 6.1 %copy.109 = f32[768,4,384]{2,0,1:T(8,128)} copy(f32[768,4,384]{0,2,1:T(8,128)} %pad_maximum_fusion) | data formatting | bytes 9437184 | tf_op jit(solution)/shard_map/optimization_barrier | solution.py:475
  312.5 5.2 %add_convert_fusion.1 = bf16[1024,768]{1,0:T(8,128)(2,1)} fusion(f32[1024,768]{1,0:T(8,128)} %fusion.55, f32[1024,768]{1,0:T(8,128)} %fusion.53, bf16[1024,384]{0,1:T(8,128)(2,1)S(1)} %bitcast.348, bf16[3,768,384]{2,1,0:T(8,128)(2,1)} %param.28), kind=kOutput, calls=%fused_computation.14 | convolution fusion | flops 606339072 | bytes 9240576 | tf_op jit(solution)/shard_map/re,de->rd/dot_general | solution.py:153
  317.8 19.6 %collective-permute-done.9 = f32[120,128]{1,0:T(8,128)S(1)} collective-permute-done((f32[120,128]{1,0:T(8,128)S(1)}, f32[120,128]{1,0:T(8,128)S(1)}, u32[]{:S(2)}, u32[]{:S(2)}) %collective-permute-start.9) | collective-permute-done | bytes 61472 | tf_op jit(solution)/shard_map/ppermute | solution.py:176
  344.7 3.9 collective-permute-done.11
  391.6 6.7 %collective-permute-done.4 = bf16[48,4,384]{2,0,1:T(8,128)(2,1)S(1)} collective-permute-done((bf16[48,4,384]{2,0,1:T(8,128)(2,1)S(1)}, bf16[48,4,384]{2,0,1:T(8,128)(2,1)S(1)}, u32[]{:S(2)}, u32[]{:S(2)}) %collective-permute-start.4) | collective-permute-done | bytes 147488 | tf_op jit(solution)/shard_map/ppermute | solution.py:176
  (592 shorter events, 236.7 us)
Async XLA Ops:
  7.2 14.9 %all-gather.5.cloned.1.call-start = ((), (), s32[]{:S(2)}) async-start(), calls=%async_computation.8 | async-start | bytes 2359296 | tf_op jit(solution)/shard_map/all_gather | solution.py:278
  7.9 76.0 %reduce-scatter.9.cloned.1.call-start = ((), (), s32[]{:S(2)}) async-start(), calls=%async_computation.9 | async-start | bytes 2359296 | tf_op jit(solution)/shard_map/reduce_scatter | solution.py:300
  67.9 25.2 %reduce-scatter.13.cloned.1.call-start = ((), (), s32[]{:S(2)}) async-start(), calls=%async_computation.12 | async-start | bytes 589824 | tf_op jit(solution)/shard_map/reduce_scatter | solution.py:303
  83.9 22.1 %all-gather.7.cloned.1.call-start = ((), (), s32[]{:S(2)}) async-start(), calls=%async_computation.10 | async-start | bytes 2359296 | tf_op jit(solution)/shard_map/all_gather | solution.py:324
  88.5 30.0 %reduce-scatter.15.cloned.1.call-start = ((), (), s32[]{:S(2)}) async-start(), calls=%async_computation.13 | async-start | bytes 589824 | tf_op jit(solution)/shard_map/reduce_scatter | solution.py:337
  103.4 27.1 %reduce-scatter.11.cloned.1.call-start = ((), (), s32[]{:S(2)}) async-start(), calls=%async_computation.11 | async-start | bytes 2359296 | tf_op jit(solution)/shard_map/reduce_scatter | solution.py:334
  118.4 26.1 %reduce-scatter.19.cloned.1.call-start = ((), (), s32[]{:S(2)}) async-start(), calls=%async_computation.17 | async-start | bytes 589824 | tf_op jit(solution)/shard_map/reduce_scatter | solution.py:372
  130.2 24.2 %all-gather.9.cloned.1.call-start = ((), (), s32[]{:S(2)}) async-start(), calls=%async_computation.14 | async-start | bytes 2359296 | tf_op jit(solution)/shard_map/all_gather | solution.py:359
  139.5 53.6 %reduce-scatter.17.cloned.1.call-start = ((), (), s32[]{:S(2)}) async-start(), calls=%async_computation.15 | async-start | bytes 2359296 | tf_op jit(solution)/shard_map/reduce_scatter | solution.py:369
  168.2 42.9 %all-gather.11.cloned.1.call-start = ((), (), s32[]{:S(2)}) async-start(), calls=%async_computation.16 | async-start | bytes 2359296 | tf_op jit(solution)/shard_map/all_gather | solution.py:385
  200.0 143.1 %reduce-scatter.23.cloned.1.call-start = ((), (), s32[]{:S(2)}) async-start(), calls=%async_computation.19 | async-start | bytes 589824 | tf_op jit(solution)/shard_map/reduce_scatter | solution.py:427
  263.2 137.9 %reduce-scatter.21.cloned.1.call-start = ((), (), s32[]{:S(2)}) async-start(), calls=%async_computation.18 | async-start | bytes 2359296 | tf_op jit(solution)/shard_map/reduce_scatter | solution.py:424
  293.4 9.7 %collective-permute-start.7 = (bf16[2,120,128]{2,1,0:T(8,128)(2,1)S(1)}, bf16[2,120,128]{2,1,0:T(8,128)(2,1)S(1)}, u32[]{:S(2)}, u32[]{:S(2)}) collective-permute-start(bf16[2,120,128]{2,1,0:T(8,128)(2,1)S(1)} %fusion.87), channel_id=1, source_target_pairs={{0,8},{2,10},{4,12},{6,14},{8,0},{10,2},{12,4},{14,6},{16,24},{18,... | collective-permute-start | bytes 184328 | tf_op jit(solution)/shard_map/ppermute | solution.py:176
  308.5 40.9 %collective-permute-start.17 = (bf16[2,2,2,48,1536]{4,3,2,1,0:T(8,128)(2,1)S(1)}, bf16[2,2,2,48,1536]{4,3,2,1,0:T(8,128)(2,1)}, u32[]{:S(2)}, u32[]{:S(2)}) collective-permute-start(bf16[2,2,2,48,1536]{4,3,2,1,0:T(8,128)(2,1)S(1)} %fusion.30), channel_id=1, source_target_pairs={{0,4},{2,6},{4,0},{6,2},{8,12},{10,14},{12,8},{14,10},{16,20},{18,... | collective-permute-start | bytes 3538952 | tf_op jit(solution)/shard_map/ppermute | solution.py:176
  309.9 44.4 %collective-permute-start.13 = (bf16[2,2,2,48,1536]{4,3,2,1,0:T(8,128)(2,1)}, bf16[2,2,2,48,1536]{4,3,2,1,0:T(8,128)(2,1)}, u32[]{:S(2)}, u32[]{:S(2)}) collective-permute-start(bf16[2,2,2,48,1536]{4,3,2,1,0:T(8,128)(2,1)} %fusion.29), channel_id=1, source_target_pairs={{0,2},{2,0},{4,6},{6,4},{8,10},{10,8},{12,14},{14,12},{16,18},{18,... | collective-permute-start | bytes 3538952 | tf_op jit(solution)/shard_map/ppermute | solution.py:176
  311.4 47.0 %collective-permute-start.1 = (bf16[2,2,2,48,4,384]{5,3,0,1,2,4:T(8,128)(2,1)}, bf16[2,2,2,48,4,384]{5,3,0,1,2,4:T(8,128)(2,1)}, u32[]{:S(2)}, u32[]{:S(2)}) collective-permute-start(bf16[2,2,2,48,4,384]{5,3,0,1,2,4:T(8,128)(2,1)} %fusion.28), channel_id=1, source_target_pairs={{0,8},{2,10},{4,12},{6,14},{8,0},{10,2},{12,4},{14,6},{16,24},{18,... | collective-permute-start | bytes 3538952 | tf_op jit(solution)/shard_map/ppermute | solution.py:176
  312.0 25.4 %collective-permute-start.9 = (f32[120,128]{1,0:T(8,128)S(1)}, f32[120,128]{1,0:T(8,128)S(1)}, u32[]{:S(2)}, u32[]{:S(2)}) collective-permute-start(f32[120,128]{1,0:T(8,128)S(1)} %bitcast_add_fusion.13), channel_id=1, source_target_pairs={{0,16},{2,18},{4,20},{6,22},{8,24},{10,26},{12,28},{14,30},{16,0},... | collective-permute-start | bytes 184328 | tf_op jit(solution)/shard_map/ppermute | solution.py:176
  348.7 13.6 %collective-permute-start.12 = (f32[2,2,2,120,128]{4,3,2,1,0:T(8,128)S(1)}, f32[2,2,2,120,128]{4,3,2,1,0:T(8,128)S(1)}, u32[]{:S(2)}, u32[]{:S(2)}) collective-permute-start(f32[2,2,2,120,128]{4,3,2,1,0:T(8,128)S(1)} %maximum_select_fusion.2), channel_id=1, source_target_pairs={{0,2},{2,0},{4,6},{6,4},{8,10},{10,8},{12,14},{14,12},{16,18},{18,... | collective-permute-start | bytes 1474568 | tf_op jit(solution)/shard_map/ppermute | solution.py:176
  352.8 22.7 %collective-permute-start.18 = (bf16[2,2,48,1536]{3,2,1,0:T(8,128)(2,1)}, bf16[2,2,48,1536]{3,2,1,0:T(8,128)(2,1)}, u32[]{:S(2)}, u32[]{:S(2)}) collective-permute-start(bf16[2,2,48,1536]{3,2,1,0:T(8,128)(2,1)} %fusion.51), channel_id=1, source_target_pairs={{0,8},{2,10},{4,12},{6,14},{8,0},{10,2},{12,4},{14,6},{16,24},{18,... | collective-permute-start | bytes 1769480 | tf_op jit(solution)/shard_map/ppermute | solution.py:176
  357.7 20.2 %collective-permute-start.14 = (bf16[2,2,48,1536]{3,2,1,0:T(8,128)(2,1)}, bf16[2,2,48,1536]{3,2,1,0:T(8,128)(2,1)}, u32[]{:S(2)}, u32[]{:S(2)}) collective-permute-start(bf16[2,2,48,1536]{3,2,1,0:T(8,128)(2,1)} %fusion.50), channel_id=1, source_target_pairs={{0,4},{2,6},{4,0},{6,2},{8,12},{10,14},{12,8},{14,10},{16,20},{18,... | collective-permute-start | bytes 1769480 | tf_op jit(solution)/shard_map/ppermute | solution.py:176
  360.8 19.1 %collective-permute-start.2 = (bf16[2,2,48,4,384]{4,2,0,1,3:T(8,128)(2,1)}, bf16[2,2,48,4,384]{4,2,0,1,3:T(8,128)(2,1)}, u32[]{:S(2)}, u32[]{:S(2)}) collective-permute-start(bf16[2,2,48,4,384]{4,2,0,1,3:T(8,128)(2,1)} %fusion.49), channel_id=1, source_target_pairs={{0,2},{2,0},{4,6},{6,4},{8,10},{10,8},{12,14},{14,12},{16,18},{18,... | collective-permute-start | bytes 1769480 | tf_op jit(solution)/shard_map/ppermute | solution.py:176
  379.2 12.1 %collective-permute-start.15 = (bf16[2,48,1536]{2,1,0:T(8,128)(2,1)S(1)}, bf16[2,48,1536]{2,1,0:T(8,128)(2,1)S(1)}, u32[]{:S(2)}, u32[]{:S(2)}) collective-permute-start(bf16[2,48,1536]{2,1,0:T(8,128)(2,1)S(1)} %fusion.71), channel_id=1, source_target_pairs={{0,8},{2,10},{4,12},{6,14},{8,0},{10,2},{12,4},{14,6},{16,24},{18,... | collective-permute-start | bytes 884744 | tf_op jit(solution)/shard_map/ppermute | solution.py:176
  384.2 14.8 %collective-permute-start.20 = (bf16[48,1536]{1,0:T(8,128)(2,1)S(1)}, bf16[48,1536]{1,0:T(8,128)(2,1)S(1)}, u32[]{:S(2)}, u32[]{:S(2)}) collective-permute-start(bf16[48,1536]{1,0:T(8,128)(2,1)S(1)} %fusion.85), channel_id=1, source_target_pairs={{0,16},{2,18},{4,20},{6,22},{8,24},{10,26},{12,28},{14,30},{16,0},... | collective-permute-start | bytes 442376 | tf_op jit(solution)/shard_map/ppermute | solution.py:176
  388.1 10.2 %collective-permute-start.4 = (bf16[48,4,384]{2,0,1:T(8,128)(2,1)S(1)}, bf16[48,4,384]{2,0,1:T(8,128)(2,1)S(1)}, u32[]{:S(2)}, u32[]{:S(2)}) collective-permute-start(bf16[48,4,384]{2,0,1:T(8,128)(2,1)S(1)} %fusion.83), channel_id=1, source_target_pairs={{0,16},{2,18},{4,20},{6,22},{8,24},{10,26},{12,28},{14,30},{16,0},... | collective-permute-start | bytes 442376 | tf_op jit(solution)/shard_map/ppermute | solution.py:176
  (153 other events, 691.7 us)
Sparse Core Ops, SparseCore 0:
  9.6 12.5 all-gather.4
  68.0 10.2 reduce-scatter.8
  84.0 8.9 reduce-scatter.12
  95.0 10.9 all-gather.6
  108.6 8.9 reduce-scatter.14
  119.7 10.1 reduce-scatter.10
  132.2 9.0 reduce-scatter.18
  143.4 10.9 all-gather.8
  168.3 10.2 reduce-scatter.16
  200.1 10.9 all-gather.10
  263.3 8.9 reduce-scatter.22
  317.9 8.1 reduce-scatter.20

commit v8 on v3

--- a/solution.py
+++ b/solution.py
@@ -224,6 +224,8 @@
     for piece, colour in zip(scattered, colours_of):
         chunk = ordered(piece, orders[colour], size, bits)
         scattered_out.append(halve(chunk, orders[colour], me, size, wire))
+    if not replicated:
+        return scattered_out, []
     blocks = []
     for piece in replicated:
         flat = piece.reshape(-1)
@@ -405,6 +407,15 @@
     text_qgrad, text_kgrad, text_vgrad, layout_qgrad, layout_kgrad, layout_vgrad = lax.map(
         attend_back, back_blocks
     )
+    (text_wup_grad, text_wdown_grad_t), attended = lax.optimization_barrier(
+        (
+            (text_wup_grad, text_wdown_grad_t),
+            (text_qgrad, text_kgrad, text_vgrad, layout_qgrad, layout_kgrad, layout_vgrad),
+        )
+    )
+    text_qgrad, text_kgrad, text_vgrad, layout_qgrad, layout_kgrad, layout_vgrad = attended
+    n_dp = lax.axis_size("dp")
+    ffn_out, _ = dp_reduce((text_wup_grad, text_wdown_grad_t), (0, 1), (), n_dp, jnp.bfloat16)
     text_qkv_grad_t, text_qvbias_grad, text_input_part = input_back(
         text_rows,
         text_qkv,
@@ -430,7 +441,6 @@
     )
     text_dinput = (text_mixed_grad + text_input_sum).astype(jnp.bfloat16)
     layout_dinput = (layout_mixed_grad + layout_input_sum).astype(jnp.bfloat16)
-    n_dp = lax.axis_size("dp")
     n_mp = lax.axis_size("mp")
     small = jnp.concatenate(
         [
@@ -456,11 +466,7 @@
         ]
     )
     small = xor_sum(small, "mp", n_mp)
-    scattered = (
-        jnp.concatenate([text_qkv_grad_t, text_wout_grad_t[:, None, :]], axis=1),
-        text_wup_grad,
-        text_wdown_grad_t,
-    )
+    scattered = (jnp.concatenate([text_qkv_grad_t, text_wout_grad_t[:, None, :]], axis=1),)
     replicated = (
         text_qvbias_grad,
         text_upbias_grad,
@@ -474,12 +480,12 @@
     )
     scattered, replicated = lax.optimization_barrier((scattered, replicated))
     scattered_out, replicated_out = dp_reduce(
-        scattered, (2, 0, 1), replicated, n_dp, jnp.bfloat16
+        scattered, (2,), replicated, n_dp, jnp.bfloat16
     )
     qkv_share = jnp.transpose(scattered_out[0][:, :3], (1, 0, 2))
     wout_share = scattered_out[0][:, 3].T
-    wup_share = scattered_out[1]
-    wdown_share = scattered_out[2].T
+    wup_share = ffn_out[0]
+    wdown_share = ffn_out[1].T
     summed = replicated_out[:8]
     small_sum = replicated_out[8]
     sizes = (2 * D, 2 * D, 2 * D, 2 * DL, 2 * DL, 2 * DL)

time: 411 us -> 409 us (level)
    while x8 -> x2, local copies, waits for them, and re-layouts: 6.81 us -> 0.8 us  [body(): lax.map(attend_back, back_blocks)]
    optimization_barrier x0 -> x6, local copies, waits for them, and re-layouts: none -> 5.09 us  [body(): lax.optimization_barrier(((text_wup_grad, text_wdown_grad_t), (text_qgrad...]
    unnamed x236 -> x238, local copies, waits for them, and re-layouts: 21.1 us -> 20.9 us
where the time goes in v8:
time: 409 us; the launch traced here: 404 us
  matrix products  110 us (27%)
  local copies, waits for them, and re-layouts  107 us (26%)
  other arithmetic  71 us (17%)
  waiting for transfers between devices  61.7 us (15%)
  starting transfers between devices  28.6 us (7%)
  between operations  16.3 us (4%)
  blocking collectives  8.64 us (2%)
    ppermute x20, waiting for transfers between devices, xor_exchange(): return lax.ppermute(values, 'dp', [(i, i ^ step) for i in range(size)])  40.3 us
    ppermute x20, starting transfers between devices, xor_exchange(): return lax.ppermute(values, 'dp', [(i, i ^ step) for i in range(size)])  27.1 us
    unnamed x238, local copies, waits for them, and re-layouts  20.9 us
    reduce_sum x8, other arithmetic, layer_norm(): centered = values - jnp.mean(values, axis=-1, keepdims=True)  12.6 us
    add x15, other arithmetic, halve(): keep + xor_exchange(send.astype(wire), 1 << bit, size).astype(chunk.dtype)  11.6 us
    convert_element_type x16, local copies, waits for them, and re-layouts, halve(): send.astype(wire)  10.5 us
    dot_general x2, matrix products, feed_back(): jnp.einsum('rd,fd->rf', full_grad, w_down, preferred_element_type=jnp.flo...  9.7 us
    dot_general x2, matrix products, feed_forward(): jnp.dot(full_rows, w_up, preferred_element_type=jnp.float32) + up_bias  9.58 us
  transfers between devices with their start and end apart: 33, of which 14 were waited for; matrix products, arithmetic and copies ran while one was open for 39% of the time, Pallas kernels for 0%

profile of v8, /device:TPU:0, one launch (start us, length us, event | category | flops | bytes accessed | tf_op | source)
XLA Modules:
  0.0 403.6 jit_solution(12185242190543136725)
XLA Ops:
  22.1 4.0 convolution_bitcast_fusion
  28.2 3.6 squeeze.169
  34.4 3.4 squeeze.168
  37.8 3.6 fusion.103
  43.1 18.1 %while.34 = (s32[]{:T(128)}, bf16[2,512,6,64]{1,3,2,0:T(8,128)(2,1)}, bf16[2,512,6,16]{1,3,2,0:T(8,128)(2,1)}, f32[2,6,512,1]{2,1,3,0:T(8,128)}, bf16[2,512,6,64...) while((s32[]{:T(128)}, ...), condition=%wide.region_3.4_spmd, body=%wide.region_0.3_spmd.sunk | while | flops 519287808 | bytes 54970212 | solution.py:296
  83.1 5.6 %reduce-scatter.13.cloned.1.call-done = bf16[512,192]{0,1:T(8,128)(2,1)} async-done(((bf16[1024,192]{0,1:T(8,128)(2,1)}), bf16[512,192]{0,1:T(8,128)(2,1)}) %reduce-scatter.13.cloned.1.call-update) | async-done | bytes 196624 | tf_op jit(solution)/shard_map/reduce_scatter | solution.py:305
  101.7 7.1 %multiply_convert_fusion.1 = (bf16[1024,1536]{1,0:T(8,128)(2,1)S(1)}, f32[1024,1536]{1,0:T(8,128)}) fusion(f32[1536]{0:T(1024)} %convert_element_type.431, bf16[1024,768]{1,0:T(8,128)(2,1)} %all-gather.7.cloned.1.call-done, bf16[768,1536]{1,0:T(8,128)(2,1)S(1)} %copy-done), kind=kOutput, calls=%fused_computation.103 | convolution fusion | flops 2425356288 | bytes 13375488 | tf_op jit(solution)/shard_map/dot_general | solution.py:123
  110.5 3.7 convolution_convert_fusion.4
  118.8 6.8 %reduce-scatter.11.cloned.1.call-done = bf16[512,768]{1,0:T(8,128)(2,1)} async-done(((bf16[1024,768]{1,0:T(8,128)(2,1)}), bf16[512,768]{1,0:T(8,128)(2,1)}) %reduce-scatter.11.cloned.1.call-update) | async-done | bytes 786448 | tf_op jit(solution)/shard_map/reduce_scatter | solution.py:336
  146.1 8.2 %convert_reduce_fusion = (f32[1536]{0:T(1024)}, bf16[1024,1536]{1,0:T(8,128)(2,1)S(1)}) fusion(f32[1024,1536]{1,0:T(8,128)} %get-tuple-element.423, f32[1536]{0:T(1024)} %convert_element_type.431, bf16[1024,768]{1,0:T(8,128)(2,1)} %all-gather.9.cloned.1.call-done, bf16[1536,768]{1,0:T(8,128)(2,1)} %param.38), kind=kOutput, calls=%fused_computation.101 | convolution fusion | flops 2441083392 | bytes 13381632 | tf_op jit(solution)/shard_map/rd,fd->rf/dot_general | solution.py:131
  156.1 3.8 convolution_convert_fusion.3
  174.9 7.3 %fusion.173 = f32[768,1536]{1,0:T(8,128)} fusion(bf16[1024,768]{1,0:T(8,128)(2,1)} %all-gather.9.cloned.1.call-done, bf16[1024,1536]{1,0:T(8,128)(2,1)} %copy-done.43), kind=kOutput, calls=%fused_computation.349 | convolution fusion | flops 2415919104 | bytes 9437184 | tf_op jit(solution)/shard_map/rf,rd->df/dot_general | solution.py:130
  182.3 3.4 multiply_reduce_fusion.1
  190.5 6.2 %fusion.172 = f32[768,1536]{1,0:T(8,128)} fusion(bf16[1024,768]{1,0:T(8,128)(2,1)S(1)} %copy-done.56, bf16[1024,1536]{1,0:T(8,128)(2,1)} %copy-done.44), kind=kOutput, calls=%fused_computation.348 | convolution fusion | flops 2415919104 | bytes 9437184 | tf_op jit(solution)/shard_map/rd,rf->df/dot_general | solution.py:133
  197.3 3.5 all-gather.11.cloned.1.call-done
  209.2 33.0 %while.35 = (s32[]{:T(128)}, bf16[2,512,6,64]{1,3,2,0:T(8,128)(2,1)}, bf16[2,512,6,64]{1,3,2,0:T(8,128)(2,1)}, bf16[2,512,6,64]{1,3,2,0:T(8,128)(2,1)}, bf16[2,5...) while((s32[]{:T(128)}, ...), condition=%wide.region_28.29_spmd, body=%wide.region_26.28_spmd.sunk | while | flops 1279964160 | bytes 114307136 | solution.py:407
  255.4 3.9 fusion.117
  273.2 3.8 fusion.119
  289.4 6.1 %copy.105 = f32[768,4,384]{2,0,1:T(8,128)} copy(f32[768,4,384]{0,2,1:T(8,128)} %pad_maximum_fusion) | data formatting | bytes 9437184 | tf_op jit(solution)/shard_map/optimization_barrier | solution.py:481
  304.9 5.2 %add_convert_fusion.1 = bf16[1024,768]{1,0:T(8,128)(2,1)} fusion(f32[1024,768]{1,0:T(8,128)} %fusion.119, f32[1024,768]{1,0:T(8,128)} %fusion.117, bf16[1024,384]{0,1:T(8,128)(2,1)S(1)} %bitcast.516, bf16[3,768,384]{2,1,0:T(8,128)(2,1)} %param.32), kind=kOutput, calls=%fused_computation.106 | convolution fusion | flops 606339072 | bytes 9240576 | tf_op jit(solution)/shard_map/re,de->rd/dot_general | solution.py:153
  310.2 19.6 %collective-permute-done.9 = f32[120,128]{1,0:T(8,128)S(1)} collective-permute-done((f32[120,128]{1,0:T(8,128)S(1)}, f32[120,128]{1,0:T(8,128)S(1)}, u32[]{:S(2)}, u32[]{:S(2)}) %collective-permute-start.9) | collective-permute-done | bytes 61472 | tf_op jit(solution)/shard_map/ppermute | solution.py:176
  331.3 3.5 collective-permute-done.10
  337.1 4.0 collective-permute-done.11
  384.0 6.7 %collective-permute-done.4 = bf16[48,4,384]{2,0,1:T(8,128)(2,1)S(1)} collective-permute-done((bf16[48,4,384]{2,0,1:T(8,128)(2,1)S(1)}, bf16[48,4,384]{2,0,1:T(8,128)(2,1)S(1)}, u32[]{:S(2)}, u32[]{:S(2)}) %collective-permute-start.4) | collective-permute-done | bytes 147488 | tf_op jit(solution)/shard_map/ppermute | solution.py:176
  (658 shorter events, 263.7 us)
Async XLA Ops:
  7.2 14.9 %all-gather.5.cloned.1.call-start = ((), (), s32[]{:S(2)}) async-start(), calls=%async_computation.8 | async-start | bytes 2359296 | tf_op jit(solution)/shard_map/all_gather | solution.py:280
  7.9 70.2 %reduce-scatter.9.cloned.1.call-start = ((), (), s32[]{:S(2)}) async-start(), calls=%async_computation.9 | async-start | bytes 2359296 | tf_op jit(solution)/shard_map/reduce_scatter | solution.py:302
  66.4 22.3 %reduce-scatter.13.cloned.1.call-start = ((), (), s32[]{:S(2)}) async-start(), calls=%async_computation.12 | async-start | bytes 589824 | tf_op jit(solution)/shard_map/reduce_scatter | solution.py:305
  78.1 23.6 %all-gather.7.cloned.1.call-start = ((), (), s32[]{:S(2)}) async-start(), calls=%async_computation.10 | async-start | bytes 2359296 | tf_op jit(solution)/shard_map/all_gather | solution.py:326
  83.0 31.3 %reduce-scatter.15.cloned.1.call-start = ((), (), s32[]{:S(2)}) async-start(), calls=%async_computation.13 | async-start | bytes 589824 | tf_op jit(solution)/shard_map/reduce_scatter | solution.py:339
  99.8 25.9 %reduce-scatter.11.cloned.1.call-start = ((), (), s32[]{:S(2)}) async-start(), calls=%async_computation.11 | async-start | bytes 2359296 | tf_op jit(solution)/shard_map/reduce_scatter | solution.py:336
  114.2 31.9 %all-gather.9.cloned.1.call-start = ((), (), s32[]{:S(2)}) async-start(), calls=%async_computation.14 | async-start | bytes 2359296 | tf_op jit(solution)/shard_map/all_gather | solution.py:361
  134.9 29.4 %reduce-scatter.19.cloned.1.call-start = ((), (), s32[]{:S(2)}) async-start(), calls=%async_computation.17 | async-start | bytes 589824 | tf_op jit(solution)/shard_map/reduce_scatter | solution.py:374
  145.0 37.2 %reduce-scatter.17.cloned.1.call-start = ((), (), s32[]{:S(2)}) async-start(), calls=%async_computation.15 | async-start | bytes 2359296 | tf_op jit(solution)/shard_map/reduce_scatter | solution.py:371
  159.9 40.9 %all-gather.11.cloned.1.call-start = ((), (), s32[]{:S(2)}) async-start(), calls=%async_computation.16 | async-start | bytes 2359296 | tf_op jit(solution)/shard_map/all_gather | solution.py:387
  189.6 145.8 %reduce-scatter.23.cloned.1.call-start = ((), (), s32[]{:S(2)}) async-start(), calls=%async_computation.19 | async-start | bytes 589824 | tf_op jit(solution)/shard_map/reduce_scatter | solution.py:438
  255.3 138.3 %reduce-scatter.21.cloned.1.call-start = ((), (), s32[]{:S(2)}) async-start(), calls=%async_computation.18 | async-start | bytes 2359296 | tf_op jit(solution)/shard_map/reduce_scatter | solution.py:435
  284.7 10.8 %collective-permute-start.7 = (bf16[2,120,128]{2,1,0:T(8,128)(2,1)S(1)}, bf16[2,120,128]{2,1,0:T(8,128)(2,1)S(1)}, u32[]{:S(2)}, u32[]{:S(2)}) collective-permute-start(bf16[2,120,128]{2,1,0:T(8,128)(2,1)S(1)} %fusion.143), channel_id=1, source_target_pairs={{0,8},{2,10},{4,12},{6,14},{8,0},{10,2},{12,4},{14,6},{16,24},{18,... | collective-permute-start | bytes 184328 | tf_op jit(solution)/shard_map/ppermute | solution.py:176
  300.8 40.9 %collective-permute-start.17 = (bf16[2,2,2,48,1536]{4,3,2,1,0:T(8,128)(2,1)}, bf16[2,2,2,48,1536]{4,3,2,1,0:T(8,128)(2,1)}, u32[]{:S(2)}, u32[]{:S(2)}) collective-permute-start(bf16[2,2,2,48,1536]{4,3,2,1,0:T(8,128)(2,1)} %fusion.111), channel_id=1, source_target_pairs={{0,4},{2,6},{4,0},{6,2},{8,12},{10,14},{12,8},{14,10},{16,20},{18,... | collective-permute-start | bytes 3538952 | tf_op jit(solution)/shard_map/ppermute | solution.py:176
  302.3 44.4 %collective-permute-start.13 = (bf16[2,2,2,48,1536]{4,3,2,1,0:T(8,128)(2,1)S(1)}, bf16[2,2,2,48,1536]{4,3,2,1,0:T(8,128)(2,1)}, u32[]{:S(2)}, u32[]{:S(2)}) collective-permute-start(bf16[2,2,2,48,1536]{4,3,2,1,0:T(8,128)(2,1)S(1)} %fusion.110), channel_id=1, source_target_pairs={{0,2},{2,0},{4,6},{6,4},{8,10},{10,8},{12,14},{14,12},{16,18},{18,... | collective-permute-start | bytes 3538952 | tf_op jit(solution)/shard_map/ppermute | solution.py:176
  303.8 47.0 %collective-permute-start.1 = (bf16[2,2,2,48,4,384]{5,3,0,1,2,4:T(8,128)(2,1)}, bf16[2,2,2,48,4,384]{5,3,0,1,2,4:T(8,128)(2,1)}, u32[]{:S(2)}, u32[]{:S(2)}) collective-permute-start(bf16[2,2,2,48,4,384]{5,3,0,1,2,4:T(8,128)(2,1)} %fusion.109), channel_id=1, source_target_pairs={{0,8},{2,10},{4,12},{6,14},{8,0},{10,2},{12,4},{14,6},{16,24},{18,... | collective-permute-start | bytes 3538952 | tf_op jit(solution)/shard_map/ppermute | solution.py:176
  304.3 25.5 %collective-permute-start.9 = (f32[120,128]{1,0:T(8,128)S(1)}, f32[120,128]{1,0:T(8,128)S(1)}, u32[]{:S(2)}, u32[]{:S(2)}) collective-permute-start(f32[120,128]{1,0:T(8,128)S(1)} %bitcast_add_fusion.13), channel_id=1, source_target_pairs={{0,16},{2,18},{4,20},{6,22},{8,24},{10,26},{12,28},{14,30},{16,0},... | collective-permute-start | bytes 184328 | tf_op jit(solution)/shard_map/ppermute | solution.py:176
  341.1 13.5 %collective-permute-start.12 = (f32[2,2,2,120,128]{4,3,2,1,0:T(8,128)S(1)}, f32[2,2,2,120,128]{4,3,2,1,0:T(8,128)S(1)}, u32[]{:S(2)}, u32[]{:S(2)}) collective-permute-start(f32[2,2,2,120,128]{4,3,2,1,0:T(8,128)S(1)} %maximum_select_fusion.2), channel_id=1, source_target_pairs={{0,2},{2,0},{4,6},{6,4},{8,10},{10,8},{12,14},{14,12},{16,18},{18,... | collective-permute-start | bytes 1474568 | tf_op jit(solution)/shard_map/ppermute | solution.py:176
  345.2 22.6 %collective-permute-start.18 = (bf16[2,2,48,1536]{3,2,1,0:T(8,128)(2,1)}, bf16[2,2,48,1536]{3,2,1,0:T(8,128)(2,1)}, u32[]{:S(2)}, u32[]{:S(2)}) collective-permute-start(bf16[2,2,48,1536]{3,2,1,0:T(8,128)(2,1)} %fusion.115), channel_id=1, source_target_pairs={{0,8},{2,10},{4,12},{6,14},{8,0},{10,2},{12,4},{14,6},{16,24},{18,... | collective-permute-start | bytes 1769480 | tf_op jit(solution)/shard_map/ppermute | solution.py:176
  350.1 20.2 %collective-permute-start.14 = (bf16[2,2,48,1536]{3,2,1,0:T(8,128)(2,1)}, bf16[2,2,48,1536]{3,2,1,0:T(8,128)(2,1)}, u32[]{:S(2)}, u32[]{:S(2)}) collective-permute-start(bf16[2,2,48,1536]{3,2,1,0:T(8,128)(2,1)} %fusion.114), channel_id=1, source_target_pairs={{0,4},{2,6},{4,0},{6,2},{8,12},{10,14},{12,8},{14,10},{16,20},{18,... | collective-permute-start | bytes 1769480 | tf_op jit(solution)/shard_map/ppermute | solution.py:176
  353.2 19.1 %collective-permute-start.2 = (bf16[2,2,48,4,384]{4,2,0,1,3:T(8,128)(2,1)}, bf16[2,2,48,4,384]{4,2,0,1,3:T(8,128)(2,1)}, u32[]{:S(2)}, u32[]{:S(2)}) collective-permute-start(bf16[2,2,48,4,384]{4,2,0,1,3:T(8,128)(2,1)} %fusion.113), channel_id=1, source_target_pairs={{0,2},{2,0},{4,6},{6,4},{8,10},{10,8},{12,14},{14,12},{16,18},{18,... | collective-permute-start | bytes 1769480 | tf_op jit(solution)/shard_map/ppermute | solution.py:176
  371.5 12.2 %collective-permute-start.15 = (bf16[2,48,1536]{2,1,0:T(8,128)(2,1)S(1)}, bf16[2,48,1536]{2,1,0:T(8,128)(2,1)S(1)}, u32[]{:S(2)}, u32[]{:S(2)}) collective-permute-start(bf16[2,48,1536]{2,1,0:T(8,128)(2,1)S(1)} %fusion.135), channel_id=1, source_target_pairs={{0,8},{2,10},{4,12},{6,14},{8,0},{10,2},{12,4},{14,6},{16,24},{18,... | collective-permute-start | bytes 884744 | tf_op jit(solution)/shard_map/ppermute | solution.py:176
  376.5 15.0 %collective-permute-start.20 = (bf16[48,1536]{1,0:T(8,128)(2,1)S(1)}, bf16[48,1536]{1,0:T(8,128)(2,1)S(1)}, u32[]{:S(2)}, u32[]{:S(2)}) collective-permute-start(bf16[48,1536]{1,0:T(8,128)(2,1)S(1)} %fusion.141), channel_id=1, source_target_pairs={{0,16},{2,18},{4,20},{6,22},{8,24},{10,26},{12,28},{14,30},{16,0},... | collective-permute-start | bytes 442376 | tf_op jit(solution)/shard_map/ppermute | solution.py:176
  380.4 10.3 %collective-permute-start.4 = (bf16[48,4,384]{2,0,1:T(8,128)(2,1)S(1)}, bf16[48,4,384]{2,0,1:T(8,128)(2,1)S(1)}, u32[]{:S(2)}, u32[]{:S(2)}) collective-permute-start(bf16[48,4,384]{2,0,1:T(8,128)(2,1)S(1)} %fusion.139), channel_id=1, source_target_pairs={{0,16},{2,18},{4,20},{6,22},{8,24},{10,26},{12,28},{14,30},{16,0},... | collective-permute-start | bytes 442376 | tf_op jit(solution)/shard_map/ppermute | solution.py:176
  (163 other events, 588.7 us)
Sparse Core Ops, SparseCore 0:
  9.6 12.5 all-gather.4
  66.5 10.2 reduce-scatter.8
  79.6 9.0 reduce-scatter.12
  90.7 10.9 all-gather.6
  104.3 8.9 reduce-scatter.14
  115.4 10.1 reduce-scatter.10
  135.0 11.0 all-gather.8
  148.4 8.9 reduce-scatter.18
  160.0 10.2 reduce-scatter.16
  189.8 10.9 all-gather.10
  255.5 8.9 reduce-scatter.22
  310.3 8.1 reduce-scatter.20

commit v9 on v3

--- a/solution.py
+++ b/solution.py
@@ -216,14 +216,12 @@
     return jnp.transpose(shaped, [canonical.index(bit) for bit in order] + rest)
 
 
-def dp_reduce(scattered, colours_of, replicated, size, wire, lanes=128):
+def dp_reduce(scattered, colours_of, replicated, size, wire, rider=1):
     bits = size.bit_length() - 1
     me = lax.axis_index("dp")
     orders = bit_orders(bits, 3)
-    scattered_out = []
-    for piece, colour in zip(scattered, colours_of):
-        chunk = ordered(piece, orders[colour], size, bits)
-        scattered_out.append(halve(chunk, orders[colour], me, size, wire))
+    host = scattered[rider]
+    lanes = host.shape[-1]
     blocks = []
     for piece in replicated:
         flat = piece.reshape(-1)
@@ -231,10 +229,21 @@
         blocks.append(flat.reshape(-1, lanes))
     joined = jnp.concatenate(blocks)
     rows = joined.shape[0]
-    joined = jnp.pad(joined, ((0, (-rows) % (size * 8)), (0, 0)))
-    chunk = ordered(joined, orders[0], size, bits)
-    block = halve(chunk, orders[0], me, size, wire)
-    full = double(block, orders[0], me, size, bits)
+    joined = jnp.pad(joined, ((0, (-rows) % size), (0, 0)))
+    extra = joined.shape[0] // size
+    own = host.shape[0] // size
+    carried = jnp.concatenate(
+        [host.reshape(size, own, lanes), joined.reshape(size, extra, lanes)], axis=1
+    ).reshape(size * (own + extra), lanes)
+    pieces = list(scattered)
+    pieces[rider] = carried
+    scattered_out = []
+    for piece, colour in zip(pieces, colours_of):
+        chunk = ordered(piece, orders[colour], size, bits)
+        scattered_out.append(halve(chunk, orders[colour], me, size, wire))
+    block = scattered_out[rider][own:]
+    scattered_out[rider] = scattered_out[rider][:own]
+    full = double(block, orders[colours_of[rider]], me, size, bits).reshape(-1, lanes)
     replicated_out = []
     offset = 0
     for piece in replicated:
@@ -244,6 +253,7 @@
         )
         offset += count
     return scattered_out, replicated_out
+
 
 def body(
     text_input,

time: 411 us -> 466 us (1.13)
  waiting for transfers between devices: 61.6 us -> 101 us
  local copies, waits for them, and re-layouts: 108 us -> 138 us
  starting transfers between devices: 28.7 us -> 20.8 us
  matrix products: 110 us -> 104 us
    ppermute x20 -> x16, waiting for transfers between devices: 40.2 us -> 80.1 us  [xor_exchange(): return lax.ppermute(values, 'dp', [(i, i ^ step) for i in range(size)])]
    concatenate x1, local copies, waits for them, and re-layouts: 2.8 us -> 11.9 us  [dp_reduce(): joined = jnp.concatenate(blocks)]
    ppermute x20 -> x16, starting transfers between devices: 27.1 us -> 19.3 us  [xor_exchange(): return lax.ppermute(values, 'dp', [(i, i ^ step) for i in range(size)])]
    unnamed x236 -> x241, local copies, waits for them, and re-layouts: 21.1 us -> 28.1 us
    reshape x6 -> x9, local copies, waits for them, and re-layouts: 1.96 us -> 8.36 us  [dp_reduce(): blocks.append(flat.reshape(-1, lanes))]
    pad x1 -> x5, local copies, waits for them, and re-layouts: 0.07 us -> 4.97 us  [the longest x4 2.71 us: dp_reduce(): flat = jnp.pad(flat, (0, -flat.shape[0] % lanes))]
    add x15 -> x11, other arithmetic: 11.6 us -> 8.38 us  [halve(): keep + xor_exchange(send.astype(wire), 1 << bit, size).astype(chunk.dtype)]
    convert_element_type x16 -> x12, local copies, waits for them, and re-layouts: 10.6 us -> 8.72 us  [halve(): send.astype(wire)]
  transfers between devices with their start and end apart: 33 -> 29, of which waited for: 14 -> 18; matrix products, arithmetic and copies ran while one was open for 39% -> 37% of each run, Pallas kernels for 0% -> 0%
where the time goes in v9:
time: 466 us; the launch traced here: 460 us
  local copies, waits for them, and re-layouts  138 us (30%)
  matrix products  104 us (22%)
  waiting for transfers between devices  101 us (22%)
  other arithmetic  69.4 us (15%)
  starting transfers between devices  20.8 us (4%)
  between operations  16.3 us (3%)
  blocking collectives  8.64 us (2%)
    ppermute x16, waiting for transfers between devices, xor_exchange(): return lax.ppermute(values, 'dp', [(i, i ^ step) for i in range(size)])  80.1 us
    unnamed x241, local copies, waits for them, and re-layouts  28.1 us
    ppermute x16, starting transfers between devices, xor_exchange(): return lax.ppermute(values, 'dp', [(i, i ^ step) for i in range(size)])  19.3 us
    reduce_sum x8, other arithmetic, layer_norm(): centered = values - jnp.mean(values, axis=-1, keepdims=True)  12.6 us
    concatenate x1, local copies, waits for them, and re-layouts, dp_reduce(): joined = jnp.concatenate(blocks)  11.9 us
    dot_general x2, matrix products, feed_back(): jnp.einsum('rd,fd->rf', full_grad, w_down, preferred_element_type=jnp.flo...  9.75 us
    dot_general x2, matrix products, feed_forward(): jnp.dot(full_rows, w_up, preferred_element_type=jnp.float32) + up_bias  9.62 us
    dot_general x2, matrix products, feed_back(): jnp.einsum(down_spec, active_low, full_grad, preferred_element_type=jnp.f...  9.47 us
  transfers between devices with their start and end apart: 29, of which 18 were waited for; matrix products, arithmetic and copies ran while one was open for 37% of the time, Pallas kernels for 0%

profile of v9, /device:TPU:0, one launch (start us, length us, event | category | flops | bytes accessed | tf_op | source)
XLA Modules:
  0.0 459.5 jit_solution(16263952702746465285)
XLA Ops:
  22.1 4.0 convolution_bitcast_fusion
  43.5 18.1 %while.34 = (s32[]{:T(128)}, bf16[2,512,6,64]{1,3,2,0:T(8,128)(2,1)}, bf16[2,512,6,16]{1,3,2,0:T(8,128)(2,1)}, f32[2,6,512,1]{2,1,3,0:T(8,128)}, bf16[2,512,6,64...) while((s32[]{:T(128)}, ...), condition=%wide.region_3.4_spmd, body=%wide.region_0.3_spmd.sunk | while | flops 519287808 | bytes 54970212 | solution.py:304
  83.4 5.7 %reduce-scatter.13.cloned.1.call-done = bf16[512,192]{0,1:T(8,128)(2,1)} async-done(((bf16[1024,192]{0,1:T(8,128)(2,1)}), bf16[512,192]{0,1:T(8,128)(2,1)}) %reduce-scatter.13.cloned.1.call-update) | async-done | bytes 196624 | tf_op jit(solution)/shard_map/reduce_scatter | solution.py:313
  102.0 7.2 %multiply_convert_fusion.1 = (bf16[1024,1536]{1,0:T(8,128)(2,1)S(1)}, f32[1024,1536]{1,0:T(8,128)}) fusion(f32[1536]{0:T(1024)} %convert_element_type.398, bf16[1024,768]{1,0:T(8,128)(2,1)} %all-gather.7.cloned.1.call-done, bf16[768,1536]{1,0:T(8,128)(2,1)S(1)} %copy-done), kind=kOutput, calls=%fused_computation.103 | convolution fusion | flops 2425356288 | bytes 13375488 | tf_op jit(solution)/shard_map/dot_general | solution.py:123
  119.2 6.8 %reduce-scatter.11.cloned.1.call-done = bf16[512,768]{1,0:T(8,128)(2,1)} async-done(((bf16[1024,768]{1,0:T(8,128)(2,1)}), bf16[512,768]{1,0:T(8,128)(2,1)}) %reduce-scatter.11.cloned.1.call-update) | async-done | bytes 786448 | tf_op jit(solution)/shard_map/reduce_scatter | solution.py:344
  146.5 8.2 %convert_reduce_fusion = (f32[1536]{0:T(1024)}, bf16[1024,1536]{1,0:T(8,128)(2,1)S(1)}) fusion(f32[1024,1536]{1,0:T(8,128)} %get-tuple-element.513, f32[1536]{0:T(1024)} %convert_element_type.398, bf16[1024,768]{1,0:T(8,128)(2,1)} %all-gather.9.cloned.1.call-done, bf16[1536,768]{1,0:T(8,128)(2,1)} %param.38), kind=kOutput, calls=%fused_computation.101 | convolution fusion | flops 2441083392 | bytes 13381632 | tf_op jit(solution)/shard_map/rd,fd->rf/dot_general | solution.py:131
  175.2 7.3 %fusion.167 = f32[768,1536]{1,0:T(8,128)} fusion(bf16[1024,768]{1,0:T(8,128)(2,1)} %all-gather.9.cloned.1.call-done, bf16[1024,1536]{1,0:T(8,128)(2,1)} %copy-done.46), kind=kOutput, calls=%fused_computation.342 | convolution fusion | flops 2415919104 | bytes 9437184 | tf_op jit(solution)/shard_map/rf,rd->df/dot_general | solution.py:130
  191.0 6.2 %fusion.166 = f32[768,1536]{1,0:T(8,128)} fusion(bf16[1024,768]{1,0:T(8,128)(2,1)S(1)} %copy-done.61, bf16[1024,1536]{1,0:T(8,128)(2,1)} %copy-done.47), kind=kOutput, calls=%fused_computation.341 | convolution fusion | flops 2415919104 | bytes 9437184 | tf_op jit(solution)/shard_map/rd,rf->df/dot_general | solution.py:133
  209.5 32.9 %while.35 = (s32[]{:T(128)}, bf16[2,512,6,64]{1,3,2,0:T(8,128)(2,1)}, bf16[2,512,6,64]{1,3,2,0:T(8,128)(2,1)}, bf16[2,512,6,64]{1,3,2,0:T(8,128)(2,1)}, bf16[2,5...) while((s32[]{:T(128)}, ...), condition=%wide.region_28.29_spmd, body=%wide.region_26.28_spmd.sunk | while | flops 1279964160 | bytes 114307136 | solution.py:415
  267.4 6.1 %copy.184 = f32[768,4,384]{2,0,1:T(8,128)} copy(f32[768,4,384]{0,2,1:T(8,128)} %pad_maximum_fusion) | data formatting | bytes 9437184 | tf_op jit(solution)/shard_map/optimization_barrier | solution.py:485
  287.3 11.9 %concatenate.98 = f32[152,1536]{1,0:T(8,128)} concatenate(f32[1,1536]{1,0:T(1,128)S(1)} %reshape.734, f32[1,1536]{1,0:T(1,128)S(1)} %reshape.735, f32[36,1536]{1,0:T(8,128)} %reshape.736, f32[1,1536]{1,0:T(1,128)} %reshape.738, f32[12,1536]{1,0:T(8,128)} %reshape.739, f32[48,1536]{1,0:T(8,128)} %reshape.740, f32[1,1536]{1,0:T(1,128)} %reshape.741, f32[48,1536]{1,0:T(8,128)} %reshape.742, ...), dimensions={0} | concatenate | bytes 1867776 | tf_op jit(solution)/shard_map/concatenate | solution.py:230
  303.9 6.0 %copy_dynamic-update-slice_fusion = f32[2,2,2,2,58,1536]{5,0,4,1,2,3:T(2,128)S(1)} fusion(f32[2,2,2,2,48,1536]{5,4,3,2,1,0:T(8,128)} %bitcast.466), kind=kLoop, calls=%fused_computation.106 | loop fusion | bytes 9437184
  329.5 11.8 %collective-permute-done.13 = bf16[2,2,2,48,1536]{4,3,2,1,0:T(8,128)(2,1)} collective-permute-done((bf16[2,2,2,48,1536]{4,3,2,1,0:T(8,128)(2,1)}, bf16[2,2,2,48,1536]{4,3,2,1,0:T(8,128)(2,1)}, u32[]{:S(2)}, u32[]{:S(2)}) %collective-permute-start.13) | collective-permute-done | bytes 1179680 | tf_op jit(solution)/shard_map/ppermute | solution.py:176
  349.5 6.8 %collective-permute-done.5 = bf16[2,2,2,58,1536]{4,2,3,1,0:T(2,128)(2,1)} collective-permute-done((bf16[2,2,2,58,1536]{4,2,3,1,0:T(2,128)(2,1)}, bf16[2,2,2,58,1536]{4,2,3,1,0:T(2,128)(2,1)}, u32[]{:S(2)}, u32[]{:S(2)}) %collective-permute-start.5) | collective-permute-done | bytes 1425440 | tf_op jit(solution)/shard_map/ppermute | solution.py:176
  362.2 6.7 %collective-permute-done.2 = bf16[2,2,48,4,384]{4,2,0,1,3:T(8,128)(2,1)S(1)} collective-permute-done((bf16[2,2,48,4,384]{4,2,0,1,3:T(8,128)(2,1)S(1)}, bf16[2,2,48,4,384]{4,2,0,1,3:T(8,128)(2,1)S(1)}, u32[]{:S(2)}, u32[]{:S(2)}) %collective-permute-start.2) | collective-permute-done | bytes 589856 | tf_op jit(solution)/shard_map/ppermute | solution.py:176
  369.6 4.3 collective-permute-done.15
  376.5 5.1 %collective-permute-done.3 = bf16[2,48,4,384]{3,1,0,2:T(8,128)(2,1)S(1)} collective-permute-done((bf16[2,48,4,384]{3,1,0,2:T(8,128)(2,1)S(1)}, bf16[2,48,4,384]{3,1,0,2:T(8,128)(2,1)S(1)}, u32[]{:S(2)}, u32[]{:S(2)}) %collective-permute-start.3) | collective-permute-done | bytes 294944 | tf_op jit(solution)/shard_map/ppermute | solution.py:176
  385.2 4.2 collective-permute-done.4
  390.2 5.7 %collective-permute-done.7 = bf16[2,58,1536]{2,1,0:T(8,128)(2,1)S(1)} collective-permute-done((bf16[2,58,1536]{2,1,0:T(8,128)(2,1)S(1)}, bf16[2,58,1536]{2,1,0:T(8,128)(2,1)S(1)}, u32[]{:S(2)}, u32[]{:S(2)}) %collective-permute-start.7) | collective-permute-done | bytes 356384 | tf_op jit(solution)/shard_map/ppermute | solution.py:176
  396.8 9.0 %collective-permute-done.8 = bf16[58,1536]{1,0:T(8,128)(2,1)S(1)} collective-permute-done((bf16[58,1536]{1,0:T(8,128)(2,1)S(1)}, bf16[58,1536]{1,0:T(8,128)(2,1)S(1)}, u32[]{:S(2)}, u32[]{:S(2)}) %collective-permute-start.8) | collective-permute-done | bytes 178208 | tf_op jit(solution)/shard_map/ppermute | solution.py:176
  407.3 4.6 %collective-permute-done.9 = f32[10,1536]{1,0:T(8,128)S(1)} collective-permute-done((f32[10,1536]{1,0:T(8,128)S(1)}, f32[10,1536]{1,0:T(8,128)S(1)}, u32[]{:S(2)}, u32[]{:S(2)}) %collective-permute-start.9) | collective-permute-done | bytes 61472 | tf_op jit(solution)/shard_map/ppermute | solution.py:176
  412.0 6.3 %collective-permute-done.10 = f32[2,10,1536]{2,1,0:T(8,128)S(1)} collective-permute-done((f32[2,10,1536]{2,1,0:T(8,128)S(1)}, f32[2,10,1536]{2,1,0:T(8,128)S(1)}, u32[]{:S(2)}, u32[]{:S(2)}) %collective-permute-start.10) | collective-permute-done | bytes 122912 | tf_op jit(solution)/shard_map/ppermute | solution.py:176
  420.1 8.4 %collective-permute-done.11 = f32[2,2,10,1536]{3,2,1,0:T(8,128)S(1)} collective-permute-done((f32[2,2,10,1536]{3,2,1,0:T(8,128)S(1)}, f32[2,2,10,1536]{3,2,1,0:T(8,128)S(1)}, u32[]{:S(2)}, u32[]{:S(2)}) %collective-permute-start.11) | collective-permute-done | bytes 245792 | tf_op jit(solution)/shard_map/ppermute | solution.py:176
  434.1 7.2 %collective-permute-done.12 = f32[2,2,2,10,1536]{4,2,3,1,0:T(2,128)S(1)} collective-permute-done((f32[2,2,2,10,1536]{4,2,3,1,0:T(2,128)}, f32[2,2,2,10,1536]{4,2,3,1,0:T(2,128)S(1)}, u32[]{:S(2)}, u32[]{:S(2)}) %collective-permute-start.12) | collective-permute-done | bytes 491552 | tf_op jit(solution)/shard_map/ppermute | solution.py:176
  (661 shorter events, 293.2 us)
Async XLA Ops:
  7.2 14.9 %all-gather.5.cloned.1.call-start = ((), (), s32[]{:S(2)}) async-start(), calls=%async_computation.8 | async-start | bytes 2359296 | tf_op jit(solution)/shard_map/all_gather | solution.py:288
  7.9 70.6 %reduce-scatter.9.cloned.1.call-start = ((), (), s32[]{:S(2)}) async-start(), calls=%async_computation.9 | async-start | bytes 2359296 | tf_op jit(solution)/shard_map/reduce_scatter | solution.py:310
  66.8 22.3 %reduce-scatter.13.cloned.1.call-start = ((), (), s32[]{:S(2)}) async-start(), calls=%async_computation.12 | async-start | bytes 589824 | tf_op jit(solution)/shard_map/reduce_scatter | solution.py:313
  78.4 23.6 %all-gather.7.cloned.1.call-start = ((), (), s32[]{:S(2)}) async-start(), calls=%async_computation.10 | async-start | bytes 2359296 | tf_op jit(solution)/shard_map/all_gather | solution.py:334
  83.3 31.4 %reduce-scatter.15.cloned.1.call-start = ((), (), s32[]{:S(2)}) async-start(), calls=%async_computation.13 | async-start | bytes 589824 | tf_op jit(solution)/shard_map/reduce_scatter | solution.py:347
  100.2 25.8 %reduce-scatter.11.cloned.1.call-start = ((), (), s32[]{:S(2)}) async-start(), calls=%async_computation.11 | async-start | bytes 2359296 | tf_op jit(solution)/shard_map/reduce_scatter | solution.py:344
  114.7 31.8 %all-gather.9.cloned.1.call-start = ((), (), s32[]{:S(2)}) async-start(), calls=%async_computation.14 | async-start | bytes 2359296 | tf_op jit(solution)/shard_map/all_gather | solution.py:369
  135.3 29.3 %reduce-scatter.19.cloned.1.call-start = ((), (), s32[]{:S(2)}) async-start(), calls=%async_computation.17 | async-start | bytes 589824 | tf_op jit(solution)/shard_map/reduce_scatter | solution.py:382
  145.4 37.1 %reduce-scatter.17.cloned.1.call-start = ((), (), s32[]{:S(2)}) async-start(), calls=%async_computation.15 | async-start | bytes 2359296 | tf_op jit(solution)/shard_map/reduce_scatter | solution.py:379
  160.2 40.9 %all-gather.11.cloned.1.call-start = ((), (), s32[]{:S(2)}) async-start(), calls=%async_computation.16 | async-start | bytes 2359296 | tf_op jit(solution)/shard_map/all_gather | solution.py:395
  190.0 136.8 %reduce-scatter.23.cloned.1.call-start = ((), (), s32[]{:S(2)}) async-start(), calls=%async_computation.19 | async-start | bytes 589824 | tf_op jit(solution)/shard_map/reduce_scatter | solution.py:437
  257.7 174.1 %reduce-scatter.21.cloned.1.call-start = ((), (), s32[]{:S(2)}) async-start(), calls=%async_computation.18 | async-start | bytes 2359296 | tf_op jit(solution)/shard_map/reduce_scatter | solution.py:434
  312.8 28.5 %collective-permute-start.13 = (bf16[2,2,2,48,1536]{4,3,2,1,0:T(8,128)(2,1)}, bf16[2,2,2,48,1536]{4,3,2,1,0:T(8,128)(2,1)}, u32[]{:S(2)}, u32[]{:S(2)}) collective-permute-start(bf16[2,2,2,48,1536]{4,3,2,1,0:T(8,128)(2,1)} %fusion.111), channel_id=1, source_target_pairs={{0,4},{2,6},{4,0},{6,2},{8,12},{10,14},{12,8},{14,10},{16,20},{18,... | collective-permute-start | bytes 3538952 | tf_op jit(solution)/shard_map/ppermute | solution.py:176
  317.4 28.2 %collective-permute-start.1 = (bf16[2,2,2,48,4,384]{5,3,0,1,2,4:T(8,128)(2,1)}, bf16[2,2,2,48,4,384]{5,3,0,1,2,4:T(8,128)(2,1)}, u32[]{:S(2)}, u32[]{:S(2)}) collective-permute-start(bf16[2,2,2,48,4,384]{5,3,0,1,2,4:T(8,128)(2,1)} %fusion.110), channel_id=1, source_target_pairs={{0,8},{2,10},{4,12},{6,14},{8,0},{10,2},{12,4},{14,6},{16,24},{18,... | collective-permute-start | bytes 3538952 | tf_op jit(solution)/shard_map/ppermute | solution.py:176
  321.9 34.4 %collective-permute-start.5 = (bf16[2,2,2,58,1536]{4,2,3,1,0:T(2,128)(2,1)}, bf16[2,2,2,58,1536]{4,2,3,1,0:T(2,128)(2,1)}, u32[]{:S(2)}, u32[]{:S(2)}) collective-permute-start(bf16[2,2,2,58,1536]{4,2,3,1,0:T(2,128)(2,1)} %fusion.105), channel_id=1, source_target_pairs={{0,2},{2,0},{4,6},{6,4},{8,10},{10,8},{12,14},{14,12},{16,18},{18,... | collective-permute-start | bytes 4276232 | tf_op jit(solution)/shard_map/ppermute | solution.py:176
  343.8 16.7 %collective-permute-start.14 = (bf16[2,2,48,1536]{3,2,1,0:T(8,128)(2,1)S(1)}, bf16[2,2,48,1536]{3,2,1,0:T(8,128)(2,1)S(1)}, u32[]{:S(2)}, u32[]{:S(2)}) collective-permute-start(bf16[2,2,48,1536]{3,2,1,0:T(8,128)(2,1)S(1)} %fusion.114), channel_id=1, source_target_pairs={{0,8},{2,10},{4,12},{6,14},{8,0},{10,2},{12,4},{14,6},{16,24},{18,... | collective-permute-start | bytes 1769480 | tf_op jit(solution)/shard_map/ppermute | solution.py:176
  348.0 20.8 %collective-permute-start.2 = (bf16[2,2,48,4,384]{4,2,0,1,3:T(8,128)(2,1)S(1)}, bf16[2,2,48,4,384]{4,2,0,1,3:T(8,128)(2,1)S(1)}, u32[]{:S(2)}, u32[]{:S(2)}) collective-permute-start(bf16[2,2,48,4,384]{4,2,0,1,3:T(8,128)(2,1)S(1)} %fusion.113), channel_id=1, source_target_pairs={{0,2},{2,0},{4,6},{6,4},{8,10},{10,8},{12,14},{14,12},{16,18},{18,... | collective-permute-start | bytes 1769480 | tf_op jit(solution)/shard_map/ppermute | solution.py:176
  359.7 24.5 %collective-permute-start.6 = (bf16[2,2,58,1536]{3,1,2,0:T(2,128)(2,1)S(1)}, bf16[2,2,58,1536]{3,1,2,0:T(2,128)(2,1)S(1)}, u32[]{:S(2)}, u32[]{:S(2)}) collective-permute-start(bf16[2,2,58,1536]{3,1,2,0:T(2,128)(2,1)S(1)} %fusion.112), channel_id=1, source_target_pairs={{0,4},{2,6},{4,0},{6,2},{8,12},{10,14},{12,8},{14,10},{16,20},{18,... | collective-permute-start | bytes 2138120 | tf_op jit(solution)/shard_map/ppermute | solution.py:176
  360.6 13.3 %collective-permute-start.15 = (bf16[2,48,1536]{2,1,0:T(8,128)(2,1)S(1)}, bf16[2,48,1536]{2,1,0:T(8,128)(2,1)S(1)}, u32[]{:S(2)}, u32[]{:S(2)}) collective-permute-start(bf16[2,48,1536]{2,1,0:T(8,128)(2,1)S(1)} %fusion.135), channel_id=1, source_target_pairs={{0,2},{2,0},{4,6},{6,4},{8,10},{10,8},{12,14},{14,12},{16,18},{18,... | collective-permute-start | bytes 884744 | tf_op jit(solution)/shard_map/ppermute | solution.py:176
  369.0 12.6 %collective-permute-start.3 = (bf16[2,48,4,384]{3,1,0,2:T(8,128)(2,1)S(1)}, bf16[2,48,4,384]{3,1,0,2:T(8,128)(2,1)S(1)}, u32[]{:S(2)}, u32[]{:S(2)}) collective-permute-start(bf16[2,48,4,384]{3,1,0,2:T(8,128)(2,1)S(1)} %fusion.134), channel_id=1, source_target_pairs={{0,4},{2,6},{4,0},{6,2},{8,12},{10,14},{12,8},{14,10},{16,20},{18,... | collective-permute-start | bytes 884744 | tf_op jit(solution)/shard_map/ppermute | solution.py:176
  374.0 15.4 %collective-permute-start.16 = (bf16[48,1536]{1,0:T(8,128)(2,1)S(1)}, bf16[48,1536]{1,0:T(8,128)(2,1)S(1)}, u32[]{:S(2)}, u32[]{:S(2)}) collective-permute-start(bf16[48,1536]{1,0:T(8,128)(2,1)S(1)} %fusion.139), channel_id=1, source_target_pairs={{0,16},{2,18},{4,20},{6,22},{8,24},{10,26},{12,28},{14,30},{16,0},... | collective-permute-start | bytes 442376 | tf_op jit(solution)/shard_map/ppermute | solution.py:176
  384.6 11.3 %collective-permute-start.7 = (bf16[2,58,1536]{2,1,0:T(8,128)(2,1)S(1)}, bf16[2,58,1536]{2,1,0:T(8,128)(2,1)S(1)}, u32[]{:S(2)}, u32[]{:S(2)}) collective-permute-start(bf16[2,58,1536]{2,1,0:T(8,128)(2,1)S(1)} %fusion.127), channel_id=1, source_target_pairs={{0,8},{2,10},{4,12},{6,14},{8,0},{10,2},{12,4},{14,6},{16,24},{18,... | collective-permute-start | bytes 1069064 | tf_op jit(solution)/shard_map/ppermute | solution.py:176
  418.3 10.2 %collective-permute-start.11 = (f32[2,2,10,1536]{3,2,1,0:T(8,128)S(1)}, f32[2,2,10,1536]{3,2,1,0:T(8,128)S(1)}, u32[]{:S(2)}, u32[]{:S(2)}) collective-permute-start(f32[2,2,10,1536]{3,2,1,0:T(8,128)S(1)} %maximum_select_fusion.4), channel_id=1, source_target_pairs={{0,4},{2,6},{4,0},{6,2},{8,12},{10,14},{12,8},{14,10},{16,20},{18,... | collective-permute-start | bytes 737288 | tf_op jit(solution)/shard_map/ppermute | solution.py:176
  429.8 11.5 %collective-permute-start.12 = (f32[2,2,2,10,1536]{4,2,3,1,0:T(2,128)}, f32[2,2,2,10,1536]{4,2,3,1,0:T(2,128)S(1)}, u32[]{:S(2)}, u32[]{:S(2)}) collective-permute-start(f32[2,2,2,10,1536]{4,2,3,1,0:T(2,128)} %copy.192), channel_id=1, source_target_pairs={{0,2},{2,0},{4,6},{6,4},{8,10},{10,8},{12,14},{14,12},{16,18},{18,... | collective-permute-start | bytes 1474568 | tf_op jit(solution)/shard_map/ppermute | solution.py:176
  (160 other events, 570.9 us)
Sparse Core Ops, SparseCore 0:
  9.6 12.5 all-gather.4
  66.9 10.2 reduce-scatter.8
  80.0 9.0 reduce-scatter.12
  91.1 10.9 all-gather.6
  104.7 8.9 reduce-scatter.14
  115.8 10.1 reduce-scatter.10
  135.4 11.0 all-gather.8
  148.7 8.9 reduce-scatter.18
  160.2 10.2 reduce-scatter.16
  190.1 10.9 all-gather.10
  257.8 8.9 reduce-scatter.22
  326.9 8.1 reduce-scatter.20

commit v10 on v8

--- a/solution.py
+++ b/solution.py
@@ -2,6 +2,7 @@
 import jax.numpy as jnp
 from jax import lax
 from jax.sharding import PartitionSpec as P
+
 
 D = 768
 H = 12
@@ -192,7 +193,8 @@
         mine = (me >> bit) & 1
         keep = lax.dynamic_index_in_dim(chunk, mine, axis=0, keepdims=False)
         send = lax.dynamic_index_in_dim(chunk, 1 - mine, axis=0, keepdims=False)
-        chunk = keep + xor_exchange(send.astype(wire), 1 << bit, size).astype(chunk.dtype)
+        received = xor_exchange(send.astype(wire), 1 << bit, size)
+        chunk = keep + received.astype(chunk.dtype)
     return chunk
 
 
@@ -234,9 +236,9 @@
     joined = jnp.concatenate(blocks)
     rows = joined.shape[0]
     joined = jnp.pad(joined, ((0, (-rows) % (size * 8)), (0, 0)))
-    chunk = ordered(joined, orders[0], size, bits)
-    block = halve(chunk, orders[0], me, size, wire)
-    full = double(block, orders[0], me, size, bits)
+    chunk = ordered(joined, orders[2], size, bits)
+    block = halve(chunk, orders[2], me, size, wire)
+    full = double(block, orders[2], me, size, bits)
     replicated_out = []
     offset = 0
     for piece in replicated:
@@ -247,7 +249,8 @@
         offset += count
     return scattered_out, replicated_out
 
-def body(
+
+def layer_body(
     text_input,
     layout_input,
     repeated,
@@ -571,4 +574,4 @@
         P(),
         P(),
     )
-    return jax.shard_map(body, mesh=mesh, in_specs=in_specs, out_specs=out_specs, check_vma=False)
+    return jax.shard_map(layer_body, mesh=mesh, in_specs=in_specs, out_specs=out_specs, check_vma=False)

time: 409 us -> 408 us (level)
  transfers between devices with their start and end apart: 33 -> 33, of which waited for: 14 -> 16; matrix products, arithmetic and copies ran while one was open for 39% -> 39% of each run, Pallas kernels for 0% -> 0%
where the time goes in v10:
time: 408 us; the launch traced here: 402 us
  matrix products  110 us (27%)
  local copies, waits for them, and re-layouts  107 us (26%)
  other arithmetic  71 us (17%)
  waiting for transfers between devices  59.8 us (15%)
  starting transfers between devices  29.2 us (7%)
  between operations  16.3 us (4%)
  blocking collectives  8.64 us (2%)
    ppermute x20, waiting for transfers between devices, xor_exchange(): return lax.ppermute(values, 'dp', [(i, i ^ step) for i in range(size)])  38.5 us
    ppermute x20, starting transfers between devices, xor_exchange(): return lax.ppermute(values, 'dp', [(i, i ^ step) for i in range(size)])  27.6 us
    unnamed x238, local copies, waits for them, and re-layouts  21 us
    reduce_sum x8, other arithmetic, layer_norm(): centered = values - jnp.mean(values, axis=-1, keepdims=True)  12.6 us
    add x15, other arithmetic, halve(): chunk = keep + received.astype(chunk.dtype)  11.6 us
    convert_element_type x16, local copies, waits for them, and re-layouts, halve(): received = xor_exchange(send.astype(wire), 1 << bit, size)  10.5 us
    dot_general x2, matrix products, feed_back(): jnp.einsum('rd,fd->rf', full_grad, w_down, preferred_element_type=jnp.flo...  9.7 us
    dot_general x2, matrix products, feed_forward(): jnp.dot(full_rows, w_up, preferred_element_type=jnp.float32) + up_bias  9.58 us
  transfers between devices with their start and end apart: 33, of which 16 were waited for; matrix products, arithmetic and copies ran while one was open for 39% of the time, Pallas kernels for 0%

profile of v10, /device:TPU:0, one launch (start us, length us, event | category | flops | bytes accessed | tf_op | source)
XLA Modules:
  0.0 402.3 jit_solution(10373512609457628973)
XLA Ops:
  22.1 4.0 convolution_bitcast_fusion
  28.2 3.6 squeeze.169
  34.4 3.4 squeeze.168
  37.8 3.6 fusion.103
  43.1 18.1 %while.34 = (s32[]{:T(128)}, bf16[2,512,6,64]{1,3,2,0:T(8,128)(2,1)}, bf16[2,512,6,16]{1,3,2,0:T(8,128)(2,1)}, f32[2,6,512,1]{2,1,3,0:T(8,128)}, bf16[2,512,6,64...) while((s32[]{:T(128)}, ...), condition=%wide.region_3.4_spmd, body=%wide.region_0.3_spmd.sunk | while | flops 519287808 | bytes 54970212 | solution.py:299
  83.1 5.6 %reduce-scatter.13.cloned.1.call-done = bf16[512,192]{0,1:T(8,128)(2,1)} async-done(((bf16[1024,192]{0,1:T(8,128)(2,1)}), bf16[512,192]{0,1:T(8,128)(2,1)}) %reduce-scatter.13.cloned.1.call-update) | async-done | bytes 196624 | tf_op jit(solution)/shard_map/reduce_scatter | solution.py:308
  101.7 7.1 %multiply_convert_fusion.1 = (bf16[1024,1536]{1,0:T(8,128)(2,1)S(1)}, f32[1024,1536]{1,0:T(8,128)}) fusion(f32[1536]{0:T(1024)} %convert_element_type.431, bf16[1024,768]{1,0:T(8,128)(2,1)} %all-gather.7.cloned.1.call-done, bf16[768,1536]{1,0:T(8,128)(2,1)S(1)} %copy-done), kind=kOutput, calls=%fused_computation.103 | convolution fusion | flops 2425356288 | bytes 13375488 | tf_op jit(solution)/shard_map/dot_general | solution.py:124
  110.5 3.7 convolution_convert_fusion.4
  118.8 6.8 %reduce-scatter.11.cloned.1.call-done = bf16[512,768]{1,0:T(8,128)(2,1)} async-done(((bf16[1024,768]{1,0:T(8,128)(2,1)}), bf16[512,768]{1,0:T(8,128)(2,1)}) %reduce-scatter.11.cloned.1.call-update) | async-done | bytes 786448 | tf_op jit(solution)/shard_map/reduce_scatter | solution.py:339
  146.1 8.2 %convert_reduce_fusion = (f32[1536]{0:T(1024)}, bf16[1024,1536]{1,0:T(8,128)(2,1)S(1)}) fusion(f32[1024,1536]{1,0:T(8,128)} %get-tuple-element.423, f32[1536]{0:T(1024)} %convert_element_type.431, bf16[1024,768]{1,0:T(8,128)(2,1)} %all-gather.9.cloned.1.call-done, bf16[1536,768]{1,0:T(8,128)(2,1)} %param.38), kind=kOutput, calls=%fused_computation.101 | convolution fusion | flops 2441083392 | bytes 13381632 | tf_op jit(solution)/shard_map/rd,fd->rf/dot_general | solution.py:132
  156.1 3.8 convolution_convert_fusion.3
  174.9 7.3 %fusion.173 = f32[768,1536]{1,0:T(8,128)} fusion(bf16[1024,768]{1,0:T(8,128)(2,1)} %all-gather.9.cloned.1.call-done, bf16[1024,1536]{1,0:T(8,128)(2,1)} %copy-done.43), kind=kOutput, calls=%fused_computation.349 | convolution fusion | flops 2415919104 | bytes 9437184 | tf_op jit(solution)/shard_map/rf,rd->df/dot_general | solution.py:131
  182.3 3.4 multiply_reduce_fusion.1
  190.5 6.2 %fusion.172 = f32[768,1536]{1,0:T(8,128)} fusion(bf16[1024,768]{1,0:T(8,128)(2,1)S(1)} %copy-done.56, bf16[1024,1536]{1,0:T(8,128)(2,1)} %copy-done.44), kind=kOutput, calls=%fused_computation.348 | convolution fusion | flops 2415919104 | bytes 9437184 | tf_op jit(solution)/shard_map/rd,rf->df/dot_general | solution.py:134
  197.3 3.5 all-gather.11.cloned.1.call-done
  209.2 33.0 %while.35 = (s32[]{:T(128)}, bf16[2,512,6,64]{1,3,2,0:T(8,128)(2,1)}, bf16[2,512,6,64]{1,3,2,0:T(8,128)(2,1)}, bf16[2,512,6,64]{1,3,2,0:T(8,128)(2,1)}, bf16[2,5...) while((s32[]{:T(128)}, ...), condition=%wide.region_28.29_spmd, body=%wide.region_26.28_spmd.sunk | while | flops 1279964160 | bytes 114307136 | solution.py:410
  255.4 3.9 fusion.117
  273.2 3.8 fusion.119
  289.4 6.1 %copy.105 = f32[768,4,384]{2,0,1:T(8,128)} copy(f32[768,4,384]{0,2,1:T(8,128)} %pad_maximum_fusion) | data formatting | bytes 9437184 | tf_op jit(solution)/shard_map/optimization_barrier | solution.py:484
  304.9 5.2 %add_convert_fusion.1 = bf16[1024,768]{1,0:T(8,128)(2,1)} fusion(f32[1024,768]{1,0:T(8,128)} %fusion.119, f32[1024,768]{1,0:T(8,128)} %fusion.117, bf16[1024,384]{0,1:T(8,128)(2,1)S(1)} %bitcast.516, bf16[3,768,384]{2,1,0:T(8,128)(2,1)} %param.32), kind=kOutput, calls=%fused_computation.106 | convolution fusion | flops 606339072 | bytes 9240576 | tf_op jit(solution)/shard_map/re,de->rd/dot_general | solution.py:154
  310.2 18.3 %collective-permute-done.9 = f32[120,128]{1,0:T(8,128)S(1)} collective-permute-done((f32[120,128]{1,0:T(8,128)S(1)}, f32[120,128]{1,0:T(8,128)S(1)}, u32[]{:S(2)}, u32[]{:S(2)}) %collective-permute-start.9) | collective-permute-done | bytes 61472 | tf_op jit(solution)/shard_map/ppermute | solution.py:177
  330.0 3.4 collective-permute-done.10
  335.8 3.9 collective-permute-done.11
  383.9 4.5 %collective-permute-done.4 = bf16[48,4,384]{2,0,1:T(8,128)(2,1)S(1)} collective-permute-done((bf16[48,4,384]{2,0,1:T(8,128)(2,1)S(1)}, bf16[48,4,384]{2,0,1:T(8,128)(2,1)S(1)}, u32[]{:S(2)}, u32[]{:S(2)}) %collective-permute-start.4) | collective-permute-done | bytes 147488 | tf_op jit(solution)/shard_map/ppermute | solution.py:177
  (658 shorter events, 266.1 us)
Async XLA Ops:
  7.2 14.9 %all-gather.5.cloned.1.call-start = ((), (), s32[]{:S(2)}) async-start(), calls=%async_computation.8 | async-start | bytes 2359296 | tf_op jit(solution)/shard_map/all_gather | solution.py:283
  7.9 70.2 %reduce-scatter.9.cloned.1.call-start = ((), (), s32[]{:S(2)}) async-start(), calls=%async_computation.9 | async-start | bytes 2359296 | tf_op jit(solution)/shard_map/reduce_scatter | solution.py:305
  66.4 22.3 %reduce-scatter.13.cloned.1.call-start = ((), (), s32[]{:S(2)}) async-start(), calls=%async_computation.12 | async-start | bytes 589824 | tf_op jit(solution)/shard_map/reduce_scatter | solution.py:308
  78.1 23.6 %all-gather.7.cloned.1.call-start = ((), (), s32[]{:S(2)}) async-start(), calls=%async_computation.10 | async-start | bytes 2359296 | tf_op jit(solution)/shard_map/all_gather | solution.py:329
  83.0 31.3 %reduce-scatter.15.cloned.1.call-start = ((), (), s32[]{:S(2)}) async-start(), calls=%async_computation.13 | async-start | bytes 589824 | tf_op jit(solution)/shard_map/reduce_scatter | solution.py:342
  99.8 25.9 %reduce-scatter.11.cloned.1.call-start = ((), (), s32[]{:S(2)}) async-start(), calls=%async_computation.11 | async-start | bytes 2359296 | tf_op jit(solution)/shard_map/reduce_scatter | solution.py:339
  114.2 31.9 %all-gather.9.cloned.1.call-start = ((), (), s32[]{:S(2)}) async-start(), calls=%async_computation.14 | async-start | bytes 2359296 | tf_op jit(solution)/shard_map/all_gather | solution.py:364
  134.9 29.4 %reduce-scatter.19.cloned.1.call-start = ((), (), s32[]{:S(2)}) async-start(), calls=%async_computation.17 | async-start | bytes 589824 | tf_op jit(solution)/shard_map/reduce_scatter | solution.py:377
  145.0 37.2 %reduce-scatter.17.cloned.1.call-start = ((), (), s32[]{:S(2)}) async-start(), calls=%async_computation.15 | async-start | bytes 2359296 | tf_op jit(solution)/shard_map/reduce_scatter | solution.py:374
  159.9 40.9 %all-gather.11.cloned.1.call-start = ((), (), s32[]{:S(2)}) async-start(), calls=%async_computation.16 | async-start | bytes 2359296 | tf_op jit(solution)/shard_map/all_gather | solution.py:390
  189.6 144.5 %reduce-scatter.23.cloned.1.call-start = ((), (), s32[]{:S(2)}) async-start(), calls=%async_computation.19 | async-start | bytes 589824 | tf_op jit(solution)/shard_map/reduce_scatter | solution.py:441
  255.3 137.0 %reduce-scatter.21.cloned.1.call-start = ((), (), s32[]{:S(2)}) async-start(), calls=%async_computation.18 | async-start | bytes 2359296 | tf_op jit(solution)/shard_map/reduce_scatter | solution.py:438
  284.8 10.7 %collective-permute-start.7 = (bf16[2,120,128]{2,1,0:T(8,128)(2,1)S(1)}, bf16[2,120,128]{2,1,0:T(8,128)(2,1)S(1)}, u32[]{:S(2)}, u32[]{:S(2)}) collective-permute-start(bf16[2,120,128]{2,1,0:T(8,128)(2,1)S(1)} %fusion.143), channel_id=1, source_target_pairs={{0,4},{2,6},{4,0},{6,2},{8,12},{10,14},{12,8},{14,10},{16,20},{18,... | collective-permute-start | bytes 184328 | tf_op jit(solution)/shard_map/ppermute | solution.py:177
  295.5 8.8 %collective-permute-start.8 = (bf16[120,128]{1,0:T(8,128)(2,1)S(1)}, bf16[120,128]{1,0:T(8,128)(2,1)S(1)}, u32[]{:S(2)}, u32[]{:S(2)}) collective-permute-start(bf16[120,128]{1,0:T(8,128)(2,1)S(1)} %fusion.151), channel_id=1, source_target_pairs={{0,16},{2,18},{4,20},{6,22},{8,24},{10,26},{12,28},{14,30},{16,0},... | collective-permute-start | bytes 92168 | tf_op jit(solution)/shard_map/ppermute | solution.py:177
  300.8 40.5 %collective-permute-start.17 = (bf16[2,2,2,48,1536]{4,3,2,1,0:T(8,128)(2,1)}, bf16[2,2,2,48,1536]{4,3,2,1,0:T(8,128)(2,1)}, u32[]{:S(2)}, u32[]{:S(2)}) collective-permute-start(bf16[2,2,2,48,1536]{4,3,2,1,0:T(8,128)(2,1)} %fusion.111), channel_id=1, source_target_pairs={{0,4},{2,6},{4,0},{6,2},{8,12},{10,14},{12,8},{14,10},{16,20},{18,... | collective-permute-start | bytes 3538952 | tf_op jit(solution)/shard_map/ppermute | solution.py:177
  301.4 44.2 %collective-permute-start.13 = (bf16[2,2,2,48,1536]{4,3,2,1,0:T(8,128)(2,1)S(1)}, bf16[2,2,2,48,1536]{4,3,2,1,0:T(8,128)(2,1)}, u32[]{:S(2)}, u32[]{:S(2)}) collective-permute-start(bf16[2,2,2,48,1536]{4,3,2,1,0:T(8,128)(2,1)S(1)} %fusion.110), channel_id=1, source_target_pairs={{0,2},{2,0},{4,6},{6,4},{8,10},{10,8},{12,14},{14,12},{16,18},{18,... | collective-permute-start | bytes 3538952 | tf_op jit(solution)/shard_map/ppermute | solution.py:177
  302.8 47.6 %collective-permute-start.1 = (bf16[2,2,2,48,4,384]{5,3,0,1,2,4:T(8,128)(2,1)}, bf16[2,2,2,48,4,384]{5,3,0,1,2,4:T(8,128)(2,1)}, u32[]{:S(2)}, u32[]{:S(2)}) collective-permute-start(bf16[2,2,2,48,4,384]{5,3,0,1,2,4:T(8,128)(2,1)} %fusion.109), channel_id=1, source_target_pairs={{0,8},{2,10},{4,12},{6,14},{8,0},{10,2},{12,4},{14,6},{16,24},{18,... | collective-permute-start | bytes 3538952 | tf_op jit(solution)/shard_map/ppermute | solution.py:177
  304.3 24.1 %collective-permute-start.9 = (f32[120,128]{1,0:T(8,128)S(1)}, f32[120,128]{1,0:T(8,128)S(1)}, u32[]{:S(2)}, u32[]{:S(2)}) collective-permute-start(f32[120,128]{1,0:T(8,128)S(1)} %bitcast_add_fusion.13), channel_id=1, source_target_pairs={{0,16},{2,18},{4,20},{6,22},{8,24},{10,26},{12,28},{14,30},{16,0},... | collective-permute-start | bytes 184328 | tf_op jit(solution)/shard_map/ppermute | solution.py:177
  339.7 14.0 %collective-permute-start.12 = (f32[2,2,2,120,128]{4,3,2,1,0:T(8,128)S(1)}, f32[2,2,2,120,128]{4,3,2,1,0:T(8,128)S(1)}, u32[]{:S(2)}, u32[]{:S(2)}) collective-permute-start(f32[2,2,2,120,128]{4,3,2,1,0:T(8,128)S(1)} %maximum_select_fusion.2), channel_id=1, source_target_pairs={{0,8},{2,10},{4,12},{6,14},{8,0},{10,2},{12,4},{14,6},{16,24},{18,... | collective-permute-start | bytes 1474568 | tf_op jit(solution)/shard_map/ppermute | solution.py:177
  344.8 22.1 %collective-permute-start.18 = (bf16[2,2,48,1536]{3,2,1,0:T(8,128)(2,1)}, bf16[2,2,48,1536]{3,2,1,0:T(8,128)(2,1)}, u32[]{:S(2)}, u32[]{:S(2)}) collective-permute-start(bf16[2,2,48,1536]{3,2,1,0:T(8,128)(2,1)} %fusion.115), channel_id=1, source_target_pairs={{0,8},{2,10},{4,12},{6,14},{8,0},{10,2},{12,4},{14,6},{16,24},{18,... | collective-permute-start | bytes 1769480 | tf_op jit(solution)/shard_map/ppermute | solution.py:177
  348.9 21.1 %collective-permute-start.14 = (bf16[2,2,48,1536]{3,2,1,0:T(8,128)(2,1)}, bf16[2,2,48,1536]{3,2,1,0:T(8,128)(2,1)}, u32[]{:S(2)}, u32[]{:S(2)}) collective-permute-start(bf16[2,2,48,1536]{3,2,1,0:T(8,128)(2,1)} %fusion.114), channel_id=1, source_target_pairs={{0,4},{2,6},{4,0},{6,2},{8,12},{10,14},{12,8},{14,10},{16,20},{18,... | collective-permute-start | bytes 1769480 | tf_op jit(solution)/shard_map/ppermute | solution.py:177
  352.9 19.8 %collective-permute-start.2 = (bf16[2,2,48,4,384]{4,2,0,1,3:T(8,128)(2,1)}, bf16[2,2,48,4,384]{4,2,0,1,3:T(8,128)(2,1)}, u32[]{:S(2)}, u32[]{:S(2)}) collective-permute-start(bf16[2,2,48,4,384]{4,2,0,1,3:T(8,128)(2,1)} %fusion.113), channel_id=1, source_target_pairs={{0,2},{2,0},{4,6},{6,4},{8,10},{10,8},{12,14},{14,12},{16,18},{18,... | collective-permute-start | bytes 1769480 | tf_op jit(solution)/shard_map/ppermute | solution.py:177
  371.2 12.1 %collective-permute-start.15 = (bf16[2,48,1536]{2,1,0:T(8,128)(2,1)S(1)}, bf16[2,48,1536]{2,1,0:T(8,128)(2,1)S(1)}, u32[]{:S(2)}, u32[]{:S(2)}) collective-permute-start(bf16[2,48,1536]{2,1,0:T(8,128)(2,1)S(1)} %fusion.135), channel_id=1, source_target_pairs={{0,8},{2,10},{4,12},{6,14},{8,0},{10,2},{12,4},{14,6},{16,24},{18,... | collective-permute-start | bytes 884744 | tf_op jit(solution)/shard_map/ppermute | solution.py:177
  375.6 13.6 %collective-permute-start.20 = (bf16[48,1536]{1,0:T(8,128)(2,1)S(1)}, bf16[48,1536]{1,0:T(8,128)(2,1)S(1)}, u32[]{:S(2)}, u32[]{:S(2)}) collective-permute-start(bf16[48,1536]{1,0:T(8,128)(2,1)S(1)} %fusion.141), channel_id=1, source_target_pairs={{0,16},{2,18},{4,20},{6,22},{8,24},{10,26},{12,28},{14,30},{16,0},... | collective-permute-start | bytes 442376 | tf_op jit(solution)/shard_map/ppermute | solution.py:177
  (163 other events, 583.8 us)
Sparse Core Ops, SparseCore 0:
  9.6 12.5 all-gather.4
  66.5 10.2 reduce-scatter.8
  79.6 9.0 reduce-scatter.12
  90.7 10.9 all-gather.6
  104.3 8.9 reduce-scatter.14
  115.4 10.1 reduce-scatter.10
  135.0 11.0 all-gather.8
  148.4 8.9 reduce-scatter.18
  160.0 10.2 reduce-scatter.16
  189.8 10.9 all-gather.10
  255.5 8.9 reduce-scatter.22
  310.3 8.1 reduce-scatter.20

commit v11 on v8

--- a/solution.py
+++ b/solution.py
@@ -209,6 +209,51 @@
     return block.reshape((-1,) + block.shape[len(held) + 1 :])
 
 
+def group_masks(pair):
+    high, low = pair
+    return [(((t >> 1) & 1) << high) | ((t & 1) << low) for t in range(4)]
+
+
+def halve_groups(chunk, groups, me, size, wire):
+    for group in groups:
+        if len(group) == 1:
+            chunk = halve(chunk, list(group), me, size, wire)
+            continue
+        high, low = group
+        chunk = chunk.reshape((4,) + chunk.shape[2:])
+        mine = ((me >> high) & 1) * 2 + ((me >> low) & 1)
+        masks = group_masks(group)
+        total = lax.dynamic_index_in_dim(chunk, mine, axis=0, keepdims=False)
+        for t in range(1, 4):
+            send = lax.dynamic_index_in_dim(chunk, mine ^ t, axis=0, keepdims=False)
+            total = total + xor_exchange(send.astype(wire), masks[t], size).astype(chunk.dtype)
+        chunk = total
+    return chunk
+
+
+def double_groups(block, groups, me, size, bits):
+    held = []
+    for group in reversed(groups):
+        if len(group) == 1:
+            (bit,) = group
+            other = xor_exchange(block, 1 << bit, size)
+            mine = (me >> bit) & 1
+            block = jnp.where(mine == 0, jnp.stack([block, other]), jnp.stack([other, block]))
+            held.insert(0, bit)
+            continue
+        high, low = group
+        masks = group_masks(group)
+        mine = ((me >> high) & 1) * 2 + ((me >> low) & 1)
+        pieces = jnp.stack([block] + [xor_exchange(block, masks[t], size) for t in range(1, 4)])
+        block = jnp.take(pieces, jnp.arange(4) ^ mine, axis=0)
+        block = block.reshape((2, 2) + block.shape[1:])
+        held = [high, low] + held
+    canonical = list(range(bits - 1, -1, -1))
+    rest = list(range(len(held), block.ndim))
+    block = jnp.transpose(block, [held.index(bit) for bit in canonical] + rest)
+    return block.reshape((-1,) + block.shape[len(held) + 1 :])
+
+
 def ordered(piece, order, size, bits):
     shaped = piece.reshape((2,) * bits + (piece.shape[0] // size,) + piece.shape[1:])
     canonical = list(range(bits - 1, -1, -1))
@@ -234,9 +279,11 @@
     joined = jnp.concatenate(blocks)
     rows = joined.shape[0]
     joined = jnp.pad(joined, ((0, (-rows) % (size * 8)), (0, 0)))
-    chunk = ordered(joined, orders[0], size, bits)
-    block = halve(chunk, orders[0], me, size, wire)
-    full = double(block, orders[0], me, size, bits)
+    order = orders[0]
+    groups = [(bit,) for bit in order[:-2]] + [tuple(order[-2:])] if bits >= 2 else [(b,) for b in order]
+    chunk = ordered(joined, order, size, bits)
+    block = halve_groups(chunk, groups, me, size, wire)
+    full = double_groups(block, groups, me, size, bits)
     replicated_out = []
     offset = 0
     for piece in replicated:

time: 409 us -> 397 us (0.971)
  waiting for transfers between devices: 61.7 us -> 45.5 us
    ppermute x20 -> x22, waiting for transfers between devices: 40.3 us -> 25.4 us  [xor_exchange(): return lax.ppermute(values, 'dp', [(i, i ^ step) for i in range(size)])]
    ppermute x20 -> x22, starting transfers between devices: 27.1 us -> 30.5 us  [xor_exchange(): return lax.ppermute(values, 'dp', [(i, i ^ step) for i in range(size)])]
    convert_element_type x16 -> x14, local copies, waits for them, and re-layouts: 10.5 us -> 12 us  [halve(): send.astype(wire)]
    add x15 -> x13, other arithmetic: 11.6 us -> 11.5 us  [halve(): keep + xor_exchange(send.astype(wire), 1 << bit, size).astype(chunk.dtype)]
    unnamed x238 -> x242, local copies, waits for them, and re-layouts: 20.9 us -> 20.9 us
  transfers between devices with their start and end apart: 33 -> 35, of which waited for: 14 -> 13; matrix products, arithmetic and copies ran while one was open for 39% -> 41% of each run, Pallas kernels for 0% -> 0%
where the time goes in v11:
time: 397 us; the launch traced here: 392 us
  matrix products  108 us (27%)
  local copies, waits for them, and re-layouts  107 us (27%)
  other arithmetic  73.5 us (19%)
  waiting for transfers between devices  45.5 us (11%)
  starting transfers between devices  32.1 us (8%)
  between operations  16.4 us (4%)
  blocking collectives  8.64 us (2%)
    ppermute x22, starting transfers between devices, xor_exchange(): return lax.ppermute(values, 'dp', [(i, i ^ step) for i in range(size)])  30.5 us
    ppermute x22, waiting for transfers between devices, xor_exchange(): return lax.ppermute(values, 'dp', [(i, i ^ step) for i in range(size)])  25.4 us
    unnamed x242, local copies, waits for them, and re-layouts  20.9 us
    reduce_sum x8, other arithmetic, layer_norm(): centered = values - jnp.mean(values, axis=-1, keepdims=True)  12.6 us
    convert_element_type x14, local copies, waits for them, and re-layouts, halve(): send.astype(wire)  12 us
    add x13, other arithmetic, halve(): keep + xor_exchange(send.astype(wire), 1 << bit, size).astype(chunk.dtype)  11.5 us
    dot_general x2, matrix products, feed_back(): jnp.einsum('rd,fd->rf', full_grad, w_down, preferred_element_type=jnp.flo...  9.76 us
    dot_general x2, matrix products, feed_forward(): jnp.dot(full_rows, w_up, preferred_element_type=jnp.float32) + up_bias  9.5 us
  transfers between devices with their start and end apart: 35, of which 13 were waited for; matrix products, arithmetic and copies ran while one was open for 41% of the time, Pallas kernels for 0%

profile of v11, /device:TPU:0, one launch (start us, length us, event | category | flops | bytes accessed | tf_op | source)
XLA Modules:
  0.0 391.7 jit_solution(8011149500242727201)
XLA Ops:
  22.1 4.0 %convolution_bitcast_fusion = f32[3,1024,384]{1,2,0:T(8,128)S(1)} fusion(bf16[3,768,384]{2,1,0:T(8,128)(2,1)} %param.32, bf16[1024,768]{1,0:T(8,128)(2,1)} %all-gather.5.cloned.1.call-done), kind=kOutput, calls=%fused_computation.121 | convolution fusion | flops 1811939328 | bytes 8060928 | tf_op jit(solution)/shard_map/rd,kde->kre/dot_general | solution.py:27
  28.2 3.6 squeeze.166
  34.4 3.4 squeeze.165
  37.8 3.6 fusion.103
  43.1 18.1 %while.34 = (s32[]{:T(128)}, bf16[2,512,6,64]{1,3,2,0:T(8,128)(2,1)}, bf16[2,512,6,16]{1,3,2,0:T(8,128)(2,1)}, f32[2,6,512,1]{2,1,3,0:T(8,128)}, bf16[2,512,6,64...) while((s32[]{:T(128)}, ...), condition=%wide.region_3.4_spmd, body=%wide.region_0.3_spmd.sunk | while | flops 519287808 | bytes 54970212 | solution.py:343
  83.2 5.6 %reduce-scatter.13.cloned.1.call-done = bf16[512,192]{0,1:T(8,128)(2,1)} async-done(((bf16[1024,192]{0,1:T(8,128)(2,1)}), bf16[512,192]{0,1:T(8,128)(2,1)}) %reduce-scatter.13.cloned.1.call-update) | async-done | bytes 196624 | tf_op jit(solution)/shard_map/reduce_scatter | solution.py:352
  101.7 7.1 %multiply_convert_fusion.1 = (bf16[1024,1536]{1,0:T(8,128)(2,1)S(1)}, f32[1024,1536]{1,0:T(8,128)}) fusion(f32[1536]{0:T(1024)} %convert_element_type.440, bf16[1024,768]{1,0:T(8,128)(2,1)} %all-gather.7.cloned.1.call-done, bf16[768,1536]{1,0:T(8,128)(2,1)S(1)} %copy-done), kind=kOutput, calls=%fused_computation.104 | convolution fusion | flops 2425356288 | bytes 13375488 | tf_op jit(solution)/shard_map/dot_general | solution.py:123
  110.5 3.7 convolution_convert_fusion.4
  120.0 5.7 %reduce-scatter.11.cloned.1.call-done = bf16[512,768]{1,0:T(8,128)(2,1)} async-done(((bf16[1024,768]{1,0:T(8,128)(2,1)}), bf16[512,768]{1,0:T(8,128)(2,1)}) %reduce-scatter.11.cloned.1.call-update) | async-done | bytes 786448 | tf_op jit(solution)/shard_map/reduce_scatter | solution.py:383
  146.2 8.2 %convert_reduce_fusion = (f32[1536]{0:T(1024)}, bf16[1024,1536]{1,0:T(8,128)(2,1)S(1)}) fusion(f32[1024,1536]{1,0:T(8,128)} %get-tuple-element.476, f32[1536]{0:T(1024)} %convert_element_type.440, bf16[1024,768]{1,0:T(8,128)(2,1)} %all-gather.9.cloned.1.call-done, bf16[1536,768]{1,0:T(8,128)(2,1)} %param.38), kind=kOutput, calls=%fused_computation.102 | convolution fusion | flops 2441083392 | bytes 13381632 | tf_op jit(solution)/shard_map/rd,fd->rf/dot_general | solution.py:131
  156.1 3.8 convolution_convert_fusion.3
  174.9 7.3 %fusion.178 = f32[768,1536]{1,0:T(8,128)} fusion(bf16[1024,768]{1,0:T(8,128)(2,1)} %all-gather.9.cloned.1.call-done, bf16[1024,1536]{1,0:T(8,128)(2,1)} %copy-done.45), kind=kOutput, calls=%fused_computation.360 | convolution fusion | flops 2415919104 | bytes 9437184 | tf_op jit(solution)/shard_map/rf,rd->df/dot_general | solution.py:130
  182.3 3.4 multiply_reduce_fusion.1
  190.5 6.2 %fusion.177 = f32[768,1536]{1,0:T(8,128)} fusion(bf16[1024,768]{1,0:T(8,128)(2,1)S(1)} %copy-done.58, bf16[1024,1536]{1,0:T(8,128)(2,1)} %copy-done.46), kind=kOutput, calls=%fused_computation.359 | convolution fusion | flops 2415919104 | bytes 9437184 | tf_op jit(solution)/shard_map/rd,rf->df/dot_general | solution.py:133
  197.3 3.5 all-gather.11.cloned.1.call-done
  209.2 32.9 %while.35 = (s32[]{:T(128)}, bf16[2,512,6,64]{1,3,2,0:T(8,128)(2,1)}, bf16[2,512,6,64]{1,3,2,0:T(8,128)(2,1)}, bf16[2,512,6,64]{1,3,2,0:T(8,128)(2,1)}, bf16[2,5...) while((s32[]{:T(128)}, ...), condition=%wide.region_28.29_spmd, body=%wide.region_26.28_spmd.sunk | while | flops 1279964160 | bytes 114307136 | solution.py:454
  255.3 3.9 fusion.117
  259.2 3.9 %fusion.119 = f32[1024,768]{1,0:T(8,128)} fusion(bf16[1024,384]{0,1:T(8,128)(2,1)S(1)} %bitcast.531, bf16[3,768,384]{2,1,0:T(8,128)(2,1)} %param.32), kind=kOutput, calls=%fused_computation.200 | convolution fusion | flops 603979776 | bytes 4521984 | tf_op jit(solution)/shard_map/re,de->rd/dot_general | solution.py:147
  278.1 3.3 collective-permute-done.5
  292.4 3.2 add_convert_fusion.1
  295.7 6.1 %copy.147 = f32[768,4,384]{2,0,1:T(8,128)} copy(f32[768,4,384]{0,2,1:T(8,128)} %pad_maximum_fusion) | data formatting | bytes 9437184 | tf_op jit(solution)/shard_map/optimization_barrier | solution.py:528
  313.1 5.8 %collective-permute-done.13 = f32[2,2,120,128]{3,2,1,0:T(8,128)S(1)} collective-permute-done((f32[2,2,120,128]{3,2,1,0:T(8,128)S(1)}, f32[2,2,120,128]{3,2,1,0:T(8,128)S(1)}, u32[]{:S(2)}, u32[]{:S(2)}) %collective-permute-start.13) | collective-permute-done | bytes 245792 | tf_op jit(solution)/shard_map/ppermute | solution.py:176
  331.2 7.1 %collective-permute-done.1 = bf16[2,2,2,48,4,384]{5,3,0,1,2,4:T(8,128)(2,1)} collective-permute-done((bf16[2,2,2,48,4,384]{5,3,0,1,2,4:T(8,128)(2,1)}, bf16[2,2,2,48,4,384]{5,3,0,1,2,4:T(8,128)(2,1)}, u32[]{:S(2)}, u32[]{:S(2)}) %collective-permute-start.1) | collective-permute-done | bytes 1179680 | tf_op jit(solution)/shard_map/ppermute | solution.py:176
  372.8 6.1 %collective-permute-done.4 = bf16[48,4,384]{2,0,1:T(8,128)(2,1)S(1)} collective-permute-done((bf16[48,4,384]{2,0,1:T(8,128)(2,1)S(1)}, bf16[48,4,384]{2,0,1:T(8,128)(2,1)S(1)}, u32[]{:S(2)}, u32[]{:S(2)}) %collective-permute-start.4) | collective-permute-done | bytes 147488 | tf_op jit(solution)/shard_map/ppermute | solution.py:176
  (666 shorter events, 266.2 us)
Async XLA Ops:
  7.2 14.9 %all-gather.5.cloned.1.call-start = ((), (), s32[]{:S(2)}) async-start(), calls=%async_computation.8 | async-start | bytes 2359296 | tf_op jit(solution)/shard_map/all_gather | solution.py:327
  7.9 70.3 %reduce-scatter.9.cloned.1.call-start = ((), (), s32[]{:S(2)}) async-start(), calls=%async_computation.9 | async-start | bytes 2359296 | tf_op jit(solution)/shard_map/reduce_scatter | solution.py:349
  66.5 22.3 %reduce-scatter.13.cloned.1.call-start = ((), (), s32[]{:S(2)}) async-start(), calls=%async_computation.12 | async-start | bytes 589824 | tf_op jit(solution)/shard_map/reduce_scatter | solution.py:352
  78.1 23.6 %all-gather.7.cloned.1.call-start = ((), (), s32[]{:S(2)}) async-start(), calls=%async_computation.10 | async-start | bytes 2359296 | tf_op jit(solution)/shard_map/all_gather | solution.py:373
  83.1 32.4 %reduce-scatter.15.cloned.1.call-start = ((), (), s32[]{:S(2)}) async-start(), calls=%async_computation.13 | async-start | bytes 589824 | tf_op jit(solution)/shard_map/reduce_scatter | solution.py:386
  99.9 25.8 %reduce-scatter.11.cloned.1.call-start = ((), (), s32[]{:S(2)}) async-start(), calls=%async_computation.11 | async-start | bytes 2359296 | tf_op jit(solution)/shard_map/reduce_scatter | solution.py:383
  114.3 31.9 %all-gather.9.cloned.1.call-start = ((), (), s32[]{:S(2)}) async-start(), calls=%async_computation.14 | async-start | bytes 2359296 | tf_op jit(solution)/shard_map/all_gather | solution.py:408
  134.9 29.4 %reduce-scatter.19.cloned.1.call-start = ((), (), s32[]{:S(2)}) async-start(), calls=%async_computation.17 | async-start | bytes 589824 | tf_op jit(solution)/shard_map/reduce_scatter | solution.py:421
  145.0 37.2 %reduce-scatter.17.cloned.1.call-start = ((), (), s32[]{:S(2)}) async-start(), calls=%async_computation.15 | async-start | bytes 2359296 | tf_op jit(solution)/shard_map/reduce_scatter | solution.py:418
  159.9 40.8 %all-gather.11.cloned.1.call-start = ((), (), s32[]{:S(2)}) async-start(), calls=%async_computation.16 | async-start | bytes 2359296 | tf_op jit(solution)/shard_map/all_gather | solution.py:434
  189.7 130.9 %reduce-scatter.23.cloned.1.call-start = ((), (), s32[]{:S(2)}) async-start(), calls=%async_computation.19 | async-start | bytes 589824 | tf_op jit(solution)/shard_map/reduce_scatter | solution.py:485
  255.2 126.5 %reduce-scatter.21.cloned.1.call-start = ((), (), s32[]{:S(2)}) async-start(), calls=%async_computation.18 | async-start | bytes 2359296 | tf_op jit(solution)/shard_map/reduce_scatter | solution.py:482
  286.4 36.0 %collective-permute-start.19 = (bf16[2,2,2,48,1536]{4,3,2,1,0:T(8,128)(2,1)}, bf16[2,2,2,48,1536]{4,3,2,1,0:T(8,128)(2,1)}, u32[]{:S(2)}, u32[]{:S(2)}) collective-permute-start(bf16[2,2,2,48,1536]{4,3,2,1,0:T(8,128)(2,1)} %fusion.111), channel_id=1, source_target_pairs={{0,4},{2,6},{4,0},{6,2},{8,12},{10,14},{12,8},{14,10},{16,20},{18,... | collective-permute-start | bytes 3538952 | tf_op jit(solution)/shard_map/ppermute | solution.py:176
  286.6 40.5 %collective-permute-start.15 = (bf16[2,2,2,48,1536]{4,3,2,1,0:T(8,128)(2,1)}, bf16[2,2,2,48,1536]{4,3,2,1,0:T(8,128)(2,1)}, u32[]{:S(2)}, u32[]{:S(2)}) collective-permute-start(bf16[2,2,2,48,1536]{4,3,2,1,0:T(8,128)(2,1)} %fusion.110), channel_id=1, source_target_pairs={{0,2},{2,0},{4,6},{6,4},{8,10},{10,8},{12,14},{14,12},{16,18},{18,... | collective-permute-start | bytes 3538952 | tf_op jit(solution)/shard_map/ppermute | solution.py:176
  288.4 13.3 %collective-permute-start.7 = (bf16[120,128]{1,0:T(8,128)(2,1)S(1)}, bf16[120,128]{1,0:T(8,128)(2,1)S(1)}, u32[]{:S(2)}, u32[]{:S(2)}) collective-permute-start(bf16[120,128]{1,0:T(8,128)(2,1)S(1)} %get-tuple-element.466), channel_id=1, source_target_pairs={{0,16},{2,18},{4,20},{6,22},{8,24},{10,26},{12,28},{14,30},{16,0},... | collective-permute-start | bytes 92168 | tf_op jit(solution)/shard_map/ppermute | solution.py:176
  290.9 10.8 %collective-permute-start.9 = (bf16[120,128]{1,0:T(8,128)(2,1)S(1)}, bf16[120,128]{1,0:T(8,128)(2,1)S(1)}, u32[]{:S(2)}, u32[]{:S(2)}) collective-permute-start(bf16[120,128]{1,0:T(8,128)(2,1)S(1)} %get-tuple-element.467), channel_id=1, source_target_pairs={{0,24},{2,26},{4,28},{6,30},{8,16},{10,18},{12,20},{14,22},{16,8},... | collective-permute-start | bytes 92168 | tf_op jit(solution)/shard_map/ppermute | solution.py:176
  292.4 9.4 %collective-permute-start.8 = (bf16[120,128]{1,0:T(8,128)(2,1)S(1)}, bf16[120,128]{1,0:T(8,128)(2,1)S(1)}, u32[]{:S(2)}, u32[]{:S(2)}) collective-permute-start(bf16[120,128]{1,0:T(8,128)(2,1)S(1)} %get-tuple-element.468), channel_id=1, source_target_pairs={{0,8},{2,10},{4,12},{6,14},{8,0},{10,2},{12,4},{14,6},{16,24},{18,... | collective-permute-start | bytes 92168 | tf_op jit(solution)/shard_map/ppermute | solution.py:176
  309.1 29.2 %collective-permute-start.1 = (bf16[2,2,2,48,4,384]{5,3,0,1,2,4:T(8,128)(2,1)}, bf16[2,2,2,48,4,384]{5,3,0,1,2,4:T(8,128)(2,1)}, u32[]{:S(2)}, u32[]{:S(2)}) collective-permute-start(bf16[2,2,2,48,4,384]{5,3,0,1,2,4:T(8,128)(2,1)} %fusion.109), channel_id=1, source_target_pairs={{0,8},{2,10},{4,12},{6,14},{8,0},{10,2},{12,4},{14,6},{16,24},{18,... | collective-permute-start | bytes 3538952 | tf_op jit(solution)/shard_map/ppermute | solution.py:176
  318.9 22.5 %collective-permute-start.14 = (f32[2,2,2,120,128]{4,3,2,1,0:T(8,128)S(1)}, f32[2,2,2,120,128]{4,3,2,1,0:T(8,128)}, u32[]{:S(2)}, u32[]{:S(2)}) collective-permute-start(f32[2,2,2,120,128]{4,3,2,1,0:T(8,128)S(1)} %maximum_select_fusion.2), channel_id=1, source_target_pairs={{0,2},{2,0},{4,6},{6,4},{8,10},{10,8},{12,14},{14,12},{16,18},{18,... | collective-permute-start | bytes 1474568 | tf_op jit(solution)/shard_map/ppermute | solution.py:176
  325.7 30.0 %collective-permute-start.20 = (bf16[2,2,48,1536]{3,2,1,0:T(8,128)(2,1)}, bf16[2,2,48,1536]{3,2,1,0:T(8,128)(2,1)}, u32[]{:S(2)}, u32[]{:S(2)}) collective-permute-start(bf16[2,2,48,1536]{3,2,1,0:T(8,128)(2,1)} %fusion.115), channel_id=1, source_target_pairs={{0,8},{2,10},{4,12},{6,14},{8,0},{10,2},{12,4},{14,6},{16,24},{18,... | collective-permute-start | bytes 1769480 | tf_op jit(solution)/shard_map/ppermute | solution.py:176
  330.6 28.5 %collective-permute-start.16 = (bf16[2,2,48,1536]{3,2,1,0:T(8,128)(2,1)}, bf16[2,2,48,1536]{3,2,1,0:T(8,128)(2,1)}, u32[]{:S(2)}, u32[]{:S(2)}) collective-permute-start(bf16[2,2,48,1536]{3,2,1,0:T(8,128)(2,1)} %fusion.114), channel_id=1, source_target_pairs={{0,4},{2,6},{4,0},{6,2},{8,12},{10,14},{12,8},{14,10},{16,20},{18,... | collective-permute-start | bytes 1769480 | tf_op jit(solution)/shard_map/ppermute | solution.py:176
  340.8 20.7 %collective-permute-start.2 = (bf16[2,2,48,4,384]{4,2,0,1,3:T(8,128)(2,1)}, bf16[2,2,48,4,384]{4,2,0,1,3:T(8,128)(2,1)}, u32[]{:S(2)}, u32[]{:S(2)}) collective-permute-start(bf16[2,2,48,4,384]{4,2,0,1,3:T(8,128)(2,1)} %fusion.113), channel_id=1, source_target_pairs={{0,2},{2,0},{4,6},{6,4},{8,10},{10,8},{12,14},{14,12},{16,18},{18,... | collective-permute-start | bytes 1769480 | tf_op jit(solution)/shard_map/ppermute | solution.py:176
  360.3 11.7 %collective-permute-start.17 = (bf16[2,48,1536]{2,1,0:T(8,128)(2,1)S(1)}, bf16[2,48,1536]{2,1,0:T(8,128)(2,1)S(1)}, u32[]{:S(2)}, u32[]{:S(2)}) collective-permute-start(bf16[2,48,1536]{2,1,0:T(8,128)(2,1)S(1)} %fusion.136), channel_id=1, source_target_pairs={{0,8},{2,10},{4,12},{6,14},{8,0},{10,2},{12,4},{14,6},{16,24},{18,... | collective-permute-start | bytes 884744 | tf_op jit(solution)/shard_map/ppermute | solution.py:176
  364.4 15.2 %collective-permute-start.22 = (bf16[48,1536]{1,0:T(8,128)(2,1)S(1)}, bf16[48,1536]{1,0:T(8,128)(2,1)S(1)}, u32[]{:S(2)}, u32[]{:S(2)}) collective-permute-start(bf16[48,1536]{1,0:T(8,128)(2,1)S(1)} %fusion.142), channel_id=1, source_target_pairs={{0,16},{2,18},{4,20},{6,22},{8,24},{10,26},{12,28},{14,30},{16,0},... | collective-permute-start | bytes 442376 | tf_op jit(solution)/shard_map/ppermute | solution.py:176
  (167 other events, 615.0 us)
Sparse Core Ops, SparseCore 0:
  9.6 12.5 all-gather.4
  66.6 10.2 reduce-scatter.8
  79.7 9.0 reduce-scatter.12
  90.8 10.9 all-gather.6
  104.4 8.9 reduce-scatter.14
  115.5 10.1 reduce-scatter.10
  135.1 11.0 all-gather.8
  148.4 8.9 reduce-scatter.18
  160.0 10.2 reduce-scatter.16
  189.8 10.9 all-gather.10
  255.3 8.9 reduce-scatter.22
  309.2 8.6 reduce-scatter.20

commit v12 on v11

--- a/solution.py
+++ b/solution.py
@@ -279,8 +279,8 @@
     joined = jnp.concatenate(blocks)
     rows = joined.shape[0]
     joined = jnp.pad(joined, ((0, (-rows) % (size * 8)), (0, 0)))
-    order = orders[0]
-    groups = [(bit,) for bit in order[:-2]] + [tuple(order[-2:])] if bits >= 2 else [(b,) for b in order]
+    order = orders[0][-2:] + orders[0][:-2] if bits >= 2 else orders[0]
+    groups = [tuple(order[:2])] + [(bit,) for bit in order[2:]] if bits >= 2 else [(order[0],)]
     chunk = ordered(joined, order, size, bits)
     block = halve_groups(chunk, groups, me, size, wire)
     full = double_groups(block, groups, me, size, bits)

time: 397 us -> 430 us (1.083)
  waiting for transfers between devices: 45.5 us -> 86.4 us
  local copies, waits for them, and re-layouts: 107 us -> 96.9 us
  starting transfers between devices: 32.1 us -> 38.2 us
  other arithmetic: 73.5 us -> 68.3 us
    ppermute x22, waiting for transfers between devices: 25.4 us -> 66.3 us  [xor_exchange(): return lax.ppermute(values, 'dp', [(i, i ^ step) for i in range(size)])]
    ppermute x22, starting transfers between devices: 30.5 us -> 36.3 us  [xor_exchange(): return lax.ppermute(values, 'dp', [(i, i ^ step) for i in range(size)])]
    unnamed x242 -> x232, local copies, waits for them, and re-layouts: 20.9 us -> 19.3 us
  transfers between devices with their start and end apart: 35 -> 35, of which waited for: 13 -> 18; matrix products, arithmetic and copies ran while one was open for 41% -> 31% of each run, Pallas kernels for 0% -> 0%
where the time goes in v12:
time: 430 us; the launch traced here: 425 us
  matrix products  109 us (25%)
  local copies, waits for them, and re-layouts  96.9 us (23%)
  waiting for transfers between devices  86.4 us (20%)
  other arithmetic  68.3 us (16%)
  starting transfers between devices  38.2 us (9%)
  between operations  16.4 us (4%)
  blocking collectives  8.64 us (2%)
    ppermute x22, waiting for transfers between devices, xor_exchange(): return lax.ppermute(values, 'dp', [(i, i ^ step) for i in range(size)])  66.3 us
    ppermute x22, starting transfers between devices, xor_exchange(): return lax.ppermute(values, 'dp', [(i, i ^ step) for i in range(size)])  36.3 us
    unnamed x232, local copies, waits for them, and re-layouts  19.3 us
    reduce_sum x8, other arithmetic, layer_norm(): centered = values - jnp.mean(values, axis=-1, keepdims=True)  12.6 us
    dot_general x2, matrix products, feed_back(): jnp.einsum('rd,fd->rf', full_grad, w_down, preferred_element_type=jnp.flo...  9.71 us
    dot_general x2, matrix products, feed_forward(): jnp.dot(full_rows, w_up, preferred_element_type=jnp.float32) + up_bias  9.58 us
    dot_general x2, matrix products, feed_back(): jnp.einsum(down_spec, active_low, full_grad, preferred_element_type=jnp.f...  9.44 us
  transfers between devices with their start and end apart: 35, of which 18 were waited for; matrix products, arithmetic and copies ran while one was open for 31% of the time, Pallas kernels for 0%

profile of v12, /device:TPU:0, one launch (start us, length us, event | category | flops | bytes accessed | tf_op | source)
XLA Modules:
  0.0 424.6 jit_solution(13828783571218120386)
XLA Ops:
  22.1 4.0 convolution_bitcast_fusion
  28.2 3.6 squeeze.166
  34.4 3.4 squeeze.165
  37.8 3.6 fusion.103
  43.1 18.1 %while.34 = (s32[]{:T(128)}, bf16[2,512,6,64]{1,3,2,0:T(8,128)(2,1)}, bf16[2,512,6,16]{1,3,2,0:T(8,128)(2,1)}, f32[2,6,512,1]{2,1,3,0:T(8,128)}, bf16[2,512,6,64...) while((s32[]{:T(128)}, ...), condition=%wide.region_3.4_spmd, body=%wide.region_0.3_spmd.sunk | while | flops 519287808 | bytes 54970212 | solution.py:343
  83.1 5.6 %reduce-scatter.13.cloned.1.call-done = bf16[512,192]{0,1:T(8,128)(2,1)} async-done(((bf16[1024,192]{0,1:T(8,128)(2,1)}), bf16[512,192]{0,1:T(8,128)(2,1)}) %reduce-scatter.13.cloned.1.call-update) | async-done | bytes 196624 | tf_op jit(solution)/shard_map/reduce_scatter | solution.py:352
  101.7 7.1 %multiply_convert_fusion.1 = (bf16[1024,1536]{1,0:T(8,128)(2,1)S(1)}, f32[1024,1536]{1,0:T(8,128)}) fusion(f32[1536]{0:T(1024)} %convert_element_type.437, bf16[1024,768]{1,0:T(8,128)(2,1)} %all-gather.7.cloned.1.call-done, bf16[768,1536]{1,0:T(8,128)(2,1)S(1)} %copy-done), kind=kOutput, calls=%fused_computation.104 | convolution fusion | flops 2425356288 | bytes 13375488 | tf_op jit(solution)/shard_map/dot_general | solution.py:123
  110.5 3.7 convolution_convert_fusion.4
  119.9 5.7 %reduce-scatter.11.cloned.1.call-done = bf16[512,768]{1,0:T(8,128)(2,1)} async-done(((bf16[1024,768]{1,0:T(8,128)(2,1)}), bf16[512,768]{1,0:T(8,128)(2,1)}) %reduce-scatter.11.cloned.1.call-update) | async-done | bytes 786448 | tf_op jit(solution)/shard_map/reduce_scatter | solution.py:383
  146.1 8.2 %convert_reduce_fusion = (f32[1536]{0:T(1024)}, bf16[1024,1536]{1,0:T(8,128)(2,1)S(1)}) fusion(f32[1024,1536]{1,0:T(8,128)} %get-tuple-element.476, f32[1536]{0:T(1024)} %convert_element_type.437, bf16[1024,768]{1,0:T(8,128)(2,1)} %all-gather.9.cloned.1.call-done, bf16[1536,768]{1,0:T(8,128)(2,1)} %param.38), kind=kOutput, calls=%fused_computation.102 | convolution fusion | flops 2441083392 | bytes 13381632 | tf_op jit(solution)/shard_map/rd,fd->rf/dot_general | solution.py:131
  156.1 3.8 convolution_convert_fusion.3
  174.9 7.3 %fusion.176 = f32[768,1536]{1,0:T(8,128)} fusion(bf16[1024,768]{1,0:T(8,128)(2,1)} %all-gather.9.cloned.1.call-done, bf16[1024,1536]{1,0:T(8,128)(2,1)} %copy-done.41), kind=kOutput, calls=%fused_computation.356 | convolution fusion | flops 2415919104 | bytes 9437184 | tf_op jit(solution)/shard_map/rf,rd->df/dot_general | solution.py:130
  190.4 6.2 %fusion.175 = f32[768,1536]{1,0:T(8,128)} fusion(bf16[1024,768]{1,0:T(8,128)(2,1)S(1)} %copy-done.54, bf16[1024,1536]{1,0:T(8,128)(2,1)} %copy-done.42), kind=kOutput, calls=%fused_computation.355 | convolution fusion | flops 2415919104 | bytes 9437184 | tf_op jit(solution)/shard_map/rd,rf->df/dot_general | solution.py:133
  197.2 3.5 all-gather.11.cloned.1.call-done
  209.1 32.9 %while.35 = (s32[]{:T(128)}, bf16[2,512,6,64]{1,3,2,0:T(8,128)(2,1)}, bf16[2,512,6,64]{1,3,2,0:T(8,128)(2,1)}, bf16[2,512,6,64]{1,3,2,0:T(8,128)(2,1)}, bf16[2,5...) while((s32[]{:T(128)}, ...), condition=%wide.region_28.29_spmd, body=%wide.region_26.28_spmd.sunk | while | flops 1279964160 | bytes 114307136 | solution.py:454
  273.1 8.0 %collective-permute-done.5 = bf16[2,2,120,128]{3,2,1,0:T(8,128)(2,1)S(1)} collective-permute-done((bf16[2,2,120,128]{3,2,1,0:T(8,128)(2,1)S(1)}, bf16[2,2,120,128]{3,2,1,0:T(8,128)(2,1)S(1)}, u32[]{:S(2)}, u32[]{:S(2)}) %collective-permute-start.5) | collective-permute-done | bytes 122912 | tf_op jit(solution)/shard_map/ppermute | solution.py:176
  295.2 6.1 %copy.143 = f32[768,4,384]{2,0,1:T(8,128)} copy(f32[768,4,384]{0,2,1:T(8,128)} %pad_maximum_fusion) | data formatting | bytes 9437184 | tf_op jit(solution)/shard_map/optimization_barrier | solution.py:528
  303.9 5.2 %add_convert_fusion.1 = bf16[1024,768]{1,0:T(8,128)(2,1)} fusion(f32[1024,768]{1,0:T(8,128)} %fusion.118, f32[1024,768]{1,0:T(8,128)} %fusion.116, bf16[1024,384]{0,1:T(8,128)(2,1)S(1)} %bitcast.520, bf16[3,768,384]{2,1,0:T(8,128)(2,1)} %param.32), kind=kOutput, calls=%fused_computation.107 | convolution fusion | flops 606339072 | bytes 9240576 | tf_op jit(solution)/shard_map/re,de->rd/dot_general | solution.py:153
  309.2 20.2 %collective-permute-done.11 = f32[2,120,128]{2,1,0:T(8,128)S(1)} collective-permute-done((f32[2,120,128]{2,1,0:T(8,128)S(1)}, f32[2,120,128]{2,1,0:T(8,128)S(1)}, u32[]{:S(2)}, u32[]{:S(2)}) %collective-permute-start.11) | collective-permute-done | bytes 122912 | tf_op jit(solution)/shard_map/ppermute | solution.py:176
  329.4 3.8 collective-permute-start.14
  340.2 9.0 %collective-permute-start.1 = (bf16[2,2,2,48,4,384]{5,3,0,1,2,4:T(8,128)(2,1)S(1)}, bf16[2,2,2,48,4,384]{5,3,0,1,2,4:T(8,128)(2,1)}, u32[]{:S(2)}, u32[]{:S(2)}) collective-permute-start(bf16[2,2,2,48,4,384]{5,3,0,1,2,4:T(8,128)(2,1)S(1)} %fusion.109), channel_id=1, source_target_pairs={{0,8},{2,10},{4,12},{6,14},{8,0},{10,2},{12,4},{14,6},{16,24},{18,... | collective-permute-start | bytes 3538952 | tf_op jit(solution)/shard_map/ppermute | solution.py:176
  369.8 7.2 %collective-permute-done.1 = bf16[2,2,2,48,4,384]{5,3,0,1,2,4:T(8,128)(2,1)} collective-permute-done((bf16[2,2,2,48,4,384]{5,3,0,1,2,4:T(8,128)(2,1)S(1)}, bf16[2,2,2,48,4,384]{5,3,0,1,2,4:T(8,128)(2,1)}, u32[]{:S(2)}, u32[]{:S(2)}) %collective-permute-start.1) | collective-permute-done | bytes 1179680 | tf_op jit(solution)/shard_map/ppermute | solution.py:176
  380.2 5.0 %collective-permute-done.20 = bf16[2,2,48,1536]{3,2,1,0:T(8,128)(2,1)S(1)} collective-permute-done((bf16[2,2,48,1536]{3,2,1,0:T(8,128)(2,1)S(1)}, bf16[2,2,48,1536]{3,2,1,0:T(8,128)(2,1)S(1)}, u32[]{:S(2)}, u32[]{:S(2)}) %collective-permute-start.20) | collective-permute-done | bytes 589856 | tf_op jit(solution)/shard_map/ppermute | solution.py:176
  402.0 9.8 %collective-permute-done.4 = bf16[48,4,384]{2,0,1:T(8,128)(2,1)S(1)} collective-permute-done((bf16[48,4,384]{2,0,1:T(8,128)(2,1)S(1)}, bf16[48,4,384]{2,0,1:T(8,128)(2,1)S(1)}, u32[]{:S(2)}, u32[]{:S(2)}) %collective-permute-start.4) | collective-permute-done | bytes 147488 | tf_op jit(solution)/shard_map/ppermute | solution.py:176
  (657 shorter events, 267.8 us)
Async XLA Ops:
  7.2 14.9 %all-gather.5.cloned.1.call-start = ((), (), s32[]{:S(2)}) async-start(), calls=%async_computation.8 | async-start | bytes 2359296 | tf_op jit(solution)/shard_map/all_gather | solution.py:327
  7.9 70.3 %reduce-scatter.9.cloned.1.call-start = ((), (), s32[]{:S(2)}) async-start(), calls=%async_computation.9 | async-start | bytes 2359296 | tf_op jit(solution)/shard_map/reduce_scatter | solution.py:349
  66.4 22.3 %reduce-scatter.13.cloned.1.call-start = ((), (), s32[]{:S(2)}) async-start(), calls=%async_computation.12 | async-start | bytes 589824 | tf_op jit(solution)/shard_map/reduce_scatter | solution.py:352
  78.1 23.5 %all-gather.7.cloned.1.call-start = ((), (), s32[]{:S(2)}) async-start(), calls=%async_computation.10 | async-start | bytes 2359296 | tf_op jit(solution)/shard_map/all_gather | solution.py:373
  83.1 32.4 %reduce-scatter.15.cloned.1.call-start = ((), (), s32[]{:S(2)}) async-start(), calls=%async_computation.13 | async-start | bytes 589824 | tf_op jit(solution)/shard_map/reduce_scatter | solution.py:386
  99.8 25.8 %reduce-scatter.11.cloned.1.call-start = ((), (), s32[]{:S(2)}) async-start(), calls=%async_computation.11 | async-start | bytes 2359296 | tf_op jit(solution)/shard_map/reduce_scatter | solution.py:383
  114.2 31.9 %all-gather.9.cloned.1.call-start = ((), (), s32[]{:S(2)}) async-start(), calls=%async_computation.14 | async-start | bytes 2359296 | tf_op jit(solution)/shard_map/all_gather | solution.py:408
  134.9 29.4 %reduce-scatter.19.cloned.1.call-start = ((), (), s32[]{:S(2)}) async-start(), calls=%async_computation.17 | async-start | bytes 589824 | tf_op jit(solution)/shard_map/reduce_scatter | solution.py:421
  145.0 37.2 %reduce-scatter.17.cloned.1.call-start = ((), (), s32[]{:S(2)}) async-start(), calls=%async_computation.15 | async-start | bytes 2359296 | tf_op jit(solution)/shard_map/reduce_scatter | solution.py:418
  159.9 40.9 %all-gather.11.cloned.1.call-start = ((), (), s32[]{:S(2)}) async-start(), calls=%async_computation.16 | async-start | bytes 2359296 | tf_op jit(solution)/shard_map/all_gather | solution.py:434
  189.6 172.7 %reduce-scatter.23.cloned.1.call-start = ((), (), s32[]{:S(2)}) async-start(), calls=%async_computation.19 | async-start | bytes 589824 | tf_op jit(solution)/shard_map/reduce_scatter | solution.py:485
  284.7 130.0 %reduce-scatter.21.cloned.1.call-start = ((), (), s32[]{:S(2)}) async-start(), calls=%async_computation.18 | async-start | bytes 2359296 | tf_op jit(solution)/shard_map/reduce_scatter | solution.py:482
  301.2 62.9 %collective-permute-start.19 = (bf16[2,2,2,48,1536]{4,3,2,1,0:T(8,128)(2,1)}, bf16[2,2,2,48,1536]{4,3,2,1,0:T(8,128)(2,1)}, u32[]{:S(2)}, u32[]{:S(2)}) collective-permute-start(bf16[2,2,2,48,1536]{4,3,2,1,0:T(8,128)(2,1)} %fusion.111), channel_id=1, source_target_pairs={{0,4},{2,6},{4,0},{6,2},{8,12},{10,14},{12,8},{14,10},{16,20},{18,... | collective-permute-start | bytes 3538952 | tf_op jit(solution)/shard_map/ppermute | solution.py:176
  301.8 65.5 %collective-permute-start.15 = (bf16[2,2,2,48,1536]{4,3,2,1,0:T(8,128)(2,1)}, bf16[2,2,2,48,1536]{4,3,2,1,0:T(8,128)(2,1)}, u32[]{:S(2)}, u32[]{:S(2)}) collective-permute-start(bf16[2,2,2,48,1536]{4,3,2,1,0:T(8,128)(2,1)} %fusion.110), channel_id=1, source_target_pairs={{0,2},{2,0},{4,6},{6,4},{8,10},{10,8},{12,14},{14,12},{16,18},{18,... | collective-permute-start | bytes 3538952 | tf_op jit(solution)/shard_map/ppermute | solution.py:176
  303.3 26.0 %collective-permute-start.11 = (f32[2,120,128]{2,1,0:T(8,128)S(1)}, f32[2,120,128]{2,1,0:T(8,128)S(1)}, u32[]{:S(2)}, u32[]{:S(2)}) collective-permute-start(f32[2,120,128]{2,1,0:T(8,128)S(1)} %maximum_select_fusion.3), channel_id=1, source_target_pairs={{0,2},{2,0},{4,6},{6,4},{8,10},{10,8},{12,14},{14,12},{16,18},{18,... | collective-permute-start | bytes 368648 | tf_op jit(solution)/shard_map/ppermute | solution.py:176
  333.2 16.0 %collective-permute-start.13 = (f32[2,2,120,128]{3,2,1,0:T(8,128)S(1)}, f32[2,2,120,128]{3,2,1,0:T(8,128)S(1)}, u32[]{:S(2)}, u32[]{:S(2)}) collective-permute-start(f32[2,2,120,128]{3,2,1,0:T(8,128)S(1)} %maximum_select_fusion.1), channel_id=1, source_target_pairs={{0,8},{2,10},{4,12},{6,14},{8,0},{10,2},{12,4},{14,6},{16,24},{18,... | collective-permute-start | bytes 737288 | tf_op jit(solution)/shard_map/ppermute | solution.py:176
  335.0 16.6 %collective-permute-start.12 = (f32[2,2,120,128]{3,2,1,0:T(8,128)S(1)}, f32[2,2,120,128]{3,2,1,0:T(8,128)S(1)}, u32[]{:S(2)}, u32[]{:S(2)}) collective-permute-start(f32[2,2,120,128]{3,2,1,0:T(8,128)S(1)} %maximum_select_fusion.1), channel_id=1, source_target_pairs={{0,16},{2,18},{4,20},{6,22},{8,24},{10,26},{12,28},{14,30},{16,0},... | collective-permute-start | bytes 737288 | tf_op jit(solution)/shard_map/ppermute | solution.py:176
  340.2 36.8 %collective-permute-start.1 = (bf16[2,2,2,48,4,384]{5,3,0,1,2,4:T(8,128)(2,1)S(1)}, bf16[2,2,2,48,4,384]{5,3,0,1,2,4:T(8,128)(2,1)}, u32[]{:S(2)}, u32[]{:S(2)}) collective-permute-start(bf16[2,2,2,48,4,384]{5,3,0,1,2,4:T(8,128)(2,1)S(1)} %fusion.109), channel_id=1, source_target_pairs={{0,8},{2,10},{4,12},{6,14},{8,0},{10,2},{12,4},{14,6},{16,24},{18,... | collective-permute-start | bytes 3538952 | tf_op jit(solution)/shard_map/ppermute | solution.py:176
  366.6 18.6 %collective-permute-start.20 = (bf16[2,2,48,1536]{3,2,1,0:T(8,128)(2,1)S(1)}, bf16[2,2,48,1536]{3,2,1,0:T(8,128)(2,1)S(1)}, u32[]{:S(2)}, u32[]{:S(2)}) collective-permute-start(bf16[2,2,48,1536]{3,2,1,0:T(8,128)(2,1)S(1)} %fusion.114), channel_id=1, source_target_pairs={{0,8},{2,10},{4,12},{6,14},{8,0},{10,2},{12,4},{14,6},{16,24},{18,... | collective-permute-start | bytes 1769480 | tf_op jit(solution)/shard_map/ppermute | solution.py:176
  369.7 18.1 %collective-permute-start.16 = (bf16[2,2,48,1536]{3,2,1,0:T(8,128)(2,1)S(1)}, bf16[2,2,48,1536]{3,2,1,0:T(8,128)(2,1)S(1)}, u32[]{:S(2)}, u32[]{:S(2)}) collective-permute-start(bf16[2,2,48,1536]{3,2,1,0:T(8,128)(2,1)S(1)} %fusion.113), channel_id=1, source_target_pairs={{0,4},{2,6},{4,0},{6,2},{8,12},{10,14},{12,8},{14,10},{16,20},{18,... | collective-permute-start | bytes 1769480 | tf_op jit(solution)/shard_map/ppermute | solution.py:176
  378.6 13.1 %collective-permute-start.2 = (bf16[2,2,48,4,384]{4,2,0,1,3:T(8,128)(2,1)S(1)}, bf16[2,2,48,4,384]{4,2,0,1,3:T(8,128)(2,1)S(1)}, u32[]{:S(2)}, u32[]{:S(2)}) collective-permute-start(bf16[2,2,48,4,384]{4,2,0,1,3:T(8,128)(2,1)S(1)} %fusion.112), channel_id=1, source_target_pairs={{0,2},{2,0},{4,6},{6,4},{8,10},{10,8},{12,14},{14,12},{16,18},{18,... | collective-permute-start | bytes 1769480 | tf_op jit(solution)/shard_map/ppermute | solution.py:176
  395.0 17.5 %collective-permute-start.22 = (bf16[48,1536]{1,0:T(8,128)(2,1)S(1)}, bf16[48,1536]{1,0:T(8,128)(2,1)S(1)}, u32[]{:S(2)}, u32[]{:S(2)}) collective-permute-start(bf16[48,1536]{1,0:T(8,128)(2,1)S(1)} %fusion.141), channel_id=1, source_target_pairs={{0,16},{2,18},{4,20},{6,22},{8,24},{10,26},{12,28},{14,30},{16,0},... | collective-permute-start | bytes 442376 | tf_op jit(solution)/shard_map/ppermute | solution.py:176
  398.8 12.9 %collective-permute-start.4 = (bf16[48,4,384]{2,0,1:T(8,128)(2,1)S(1)}, bf16[48,4,384]{2,0,1:T(8,128)(2,1)S(1)}, u32[]{:S(2)}, u32[]{:S(2)}) collective-permute-start(bf16[48,4,384]{2,0,1:T(8,128)(2,1)S(1)} %fusion.139), channel_id=1, source_target_pairs={{0,16},{2,18},{4,20},{6,22},{8,24},{10,26},{12,28},{14,30},{16,0},... | collective-permute-start | bytes 442376 | tf_op jit(solution)/shard_map/ppermute | solution.py:176
  399.2 14.7 %collective-permute-start.18 = (bf16[48,1536]{1,0:T(8,128)(2,1)S(1)}, bf16[48,1536]{1,0:T(8,128)(2,1)S(1)}, u32[]{:S(2)}, u32[]{:S(2)}) collective-permute-start(bf16[48,1536]{1,0:T(8,128)(2,1)S(1)} %fusion.140), channel_id=1, source_target_pairs={{0,16},{2,18},{4,20},{6,22},{8,24},{10,26},{12,28},{14,30},{16,0},... | collective-permute-start | bytes 442376 | tf_op jit(solution)/shard_map/ppermute | solution.py:176
  (162 other events, 582.2 us)
Sparse Core Ops, SparseCore 0:
  9.6 12.5 all-gather.4
  66.5 10.2 reduce-scatter.8
  79.6 9.0 reduce-scatter.12
  90.7 10.8 all-gather.6
  104.3 8.9 reduce-scatter.14
  115.4 10.1 reduce-scatter.10
  135.0 11.0 all-gather.8
  148.4 8.9 reduce-scatter.18
  160.0 10.2 reduce-scatter.16
  189.7 10.9 all-gather.10
  284.8 8.2 reduce-scatter.22
  337.0 8.6 reduce-scatter.20
